TPU v7x, 256 devices: a whole 4x4x8 slice. The times are simulated.
256 devices in a mesh: seq: 32 (over x_hi, z, core), tp: 8 (over y, x_lo).
Axes of the slice: x: 4 (x_hi: 2, x_lo: 2; x = x_hi * 2 + x_lo), y: 4, z: 8, core: 2. Of those that a mesh axis runs over, the one named last changes fastest.
Arguments:
- proj: bfloat16 [4096, 3, 8192], P('seq', None, 'tp'), may hold values from -6 to 6
- cotangent: bfloat16 [4096, 8192], P('seq', 'tp'), may hold values from -6 to 6
- out_weight: bfloat16 [8192, 8192], P('seq', 'tp'), may hold values from -0.125 to 0.125
- short_weight: float32 [7, 3, 8192], P(None, None, 'tp'), may hold values from -2 to 2
- long_filter: float32 [4096, 8192], P('seq', 'tp')
Outputs:
- grad_proj: bfloat16 [4096, 3, 8192], P('seq', None, 'tp')
- grad_short: float32 [7, 3, 8192], P(None, None, 'tp')
- grad_filter: float32 [4096, 8192], P('seq', 'tp')
All inputs are finite; a program needn't handle non-finite values.
Results may differ from a plain program's by a relative error of at most 0.025.
Values may be sent and summed in bfloat16 or wider, within the bound.
No kernel may reach another device: no remote copies, remote signals or barrier semaphores. Data moves between devices by JAX's collectives and lax.ppermute only.
A program may use at most 128 MiB of HBM per device.

v0:
```python
import math

import jax
import jax.numpy as jnp
from jax import lax
from jax.sharding import PartitionSpec as P

highest = lax.Precision.HIGHEST


def shifted(value, axis, by):
    devices = lax.axis_size(axis)
    pairs = [(i, i + by) for i in range(devices) if 0 <= i + by < devices]
    return lax.ppermute(value, axis, pairs)


def angle_tables(row_count, col_count, modulus):
    row_index = jnp.arange(row_count, dtype=jnp.int32)[:, None]
    col_index = jnp.arange(col_count, dtype=jnp.int32)[None, :]
    phase = (row_index * col_index % modulus).astype(jnp.float32) * (2.0 * math.pi / modulus)
    return (jnp.cos(phase), jnp.sin(phase))


def split_length(length):
    whole_len = 2 * length
    ceiling = 1 << whole_len.bit_length() // 2 - 1
    first_len = 2 * math.gcd(length, ceiling)
    return (first_len, whole_len // first_len)


def spectrum(columns):
    length, channels = columns.shape
    first_len, second_len = split_length(length)
    lower_half = first_len // 2
    whole_len = first_len * second_len
    values = columns.astype(jnp.float32).reshape(lower_half, second_len * channels)
    cos_first, sin_first = angle_tables(first_len, lower_half, first_len)
    real_one = jnp.dot(cos_first, values, precision=highest).reshape(
        first_len, second_len, channels
    )
    imag_one = -jnp.dot(sin_first, values, precision=highest).reshape(
        first_len, second_len, channels
    )
    twist_cos, twist_sin = angle_tables(first_len, second_len, whole_len)
    twist_cos = twist_cos[:, :, None]
    twist_sin = twist_sin[:, :, None]
    real_two = real_one * twist_cos + imag_one * twist_sin
    imag_two = imag_one * twist_cos - real_one * twist_sin
    cos_second, sin_second = angle_tables(second_len, second_len, second_len)
    real_out = jnp.einsum("amc,ml->alc", real_two, cos_second, precision=highest) + jnp.einsum(
        "amc,ml->alc", imag_two, sin_second, precision=highest
    )
    imag_out = jnp.einsum("amc,ml->alc", imag_two, cos_second, precision=highest) - jnp.einsum(
        "amc,ml->alc", real_two, sin_second, precision=highest
    )
    return (real_out, imag_out)


def signal(real_in, imag_in):
    first_len, second_len, channels = real_in.shape
    lower_half = first_len // 2
    whole_len = first_len * second_len
    cos_second, sin_second = angle_tables(second_len, second_len, second_len)
    real_one = jnp.einsum("alc,lm->amc", real_in, cos_second, precision=highest) - jnp.einsum(
        "alc,lm->amc", imag_in, sin_second, precision=highest
    )
    imag_one = jnp.einsum("alc,lm->amc", real_in, sin_second, precision=highest) + jnp.einsum(
        "alc,lm->amc", imag_in, cos_second, precision=highest
    )
    twist_cos, twist_sin = angle_tables(first_len, second_len, whole_len)
    twist_cos = twist_cos[:, :, None]
    twist_sin = twist_sin[:, :, None]
    real_two = real_one * twist_cos - imag_one * twist_sin
    imag_two = real_one * twist_sin + imag_one * twist_cos
    cos_first, sin_first = angle_tables(lower_half, first_len, first_len)
    merged = jnp.dot(
        cos_first, real_two.reshape(first_len, second_len * channels), precision=highest
    ) - jnp.dot(sin_first, imag_two.reshape(first_len, second_len * channels), precision=highest)
    return merged.reshape(lower_half * second_len, channels) / whole_len


def complex_product(left_real, left_imag, right_real, right_imag):
    return (
        left_real * right_real - left_imag * right_imag,
        left_real * right_imag + left_imag * right_real,
    )


def conj_product(left_real, left_imag, right_real, right_imag):
    return (
        left_real * right_real + left_imag * right_imag,
        left_imag * right_real - left_real * right_imag,
    )


def times_bf16(left_array, right_array):
    return (left_array.astype(jnp.float32) * right_array.astype(jnp.float32)).astype(jnp.bfloat16)


def body(proj, cotangent, out_weight, short_weight, long_filter):
    tok_rows = proj.shape[0]
    channels = proj.shape[2]
    taps_count = short_weight.shape[0]
    rim_rows = taps_count - 1
    partial_value = lax.dot_general(
        cotangent,
        lax.all_gather(out_weight, "seq", axis=0, tiled=True),
        (((1,), (1,)), ((), ())),
        preferred_element_type=jnp.float32,
    )
    summed = lax.psum(partial_value.astype(jnp.bfloat16), "tp").astype(jnp.float32)
    grad_out = lax.dynamic_slice_in_dim(summed, lax.axis_index("tp") * channels, channels, 1)
    grad_out = grad_out.astype(jnp.bfloat16)
    lower_rows = shifted(proj[tok_rows - rim_rows :], "seq", 1)
    extended = jnp.concatenate([lower_rows, proj], axis=0)
    primed = short_weight[0] * extended[rim_rows : rim_rows + tok_rows]
    for offset in range(1, taps_count):
        primed = (
            primed
            + short_weight[offset] * extended[rim_rows - offset : rim_rows - offset + tok_rows]
        )
    primed = primed.astype(jnp.bfloat16)
    query_conv = primed[:, 0]
    keys_conv = primed[:, 1]
    value_conv = primed[:, 2]
    gated_input = times_bf16(keys_conv, value_conv)
    filter_cols = lax.all_to_all(
        long_filter.astype(jnp.bfloat16), "seq", split_axis=1, concat_axis=0, tiled=True
    ).astype(long_filter.dtype)
    filter_real, filter_imag = spectrum(filter_cols)
    gated_cols = lax.all_to_all(gated_input, "seq", split_axis=1, concat_axis=0, tiled=True)
    gated_real, gated_imag = spectrum(gated_cols)
    conv_cols = signal(*complex_product(gated_real, gated_imag, filter_real, filter_imag)).astype(
        jnp.bfloat16
    )
    conv_out = lax.all_to_all(conv_cols, "seq", split_axis=0, concat_axis=1, tiled=True)
    grad_query = times_bf16(grad_out, conv_out)
    grad_conv = times_bf16(grad_out, query_conv)
    grad_cols = lax.all_to_all(grad_conv, "seq", split_axis=1, concat_axis=0, tiled=True)
    grad_real, grad_imag = spectrum(grad_cols)
    gated_grad_cols = signal(*conj_product(grad_real, grad_imag, filter_real, filter_imag)).astype(
        jnp.bfloat16
    )
    filter_grad_cols = signal(*conj_product(grad_real, grad_imag, gated_real, gated_imag))
    gated_grad = lax.all_to_all(gated_grad_cols, "seq", split_axis=0, concat_axis=1, tiled=True)
    grad_filter = lax.all_to_all(
        filter_grad_cols.astype(jnp.bfloat16), "seq", split_axis=0, concat_axis=1, tiled=True
    ).astype(filter_grad_cols.dtype)
    grad_keys = times_bf16(gated_grad, value_conv)
    grad_value = times_bf16(gated_grad, keys_conv)
    grad_primed = jnp.stack([grad_query, grad_keys, grad_value], axis=1)
    next_rows = shifted(grad_primed[:rim_rows], "seq", -1)
    trailing = jnp.concatenate([grad_primed, next_rows], axis=0)
    grad_sum = short_weight[0] * trailing[0:tok_rows]
    for offset in range(1, taps_count):
        grad_sum = grad_sum + short_weight[offset] * trailing[offset : offset + tok_rows]
    grad_proj = grad_sum.astype(jnp.bfloat16)
    grad_wide = grad_primed.astype(jnp.float32)
    local_short = jnp.stack(
        [
            jnp.sum(
                grad_wide
                * extended[rim_rows - offset : rim_rows - offset + tok_rows].astype(jnp.float32),
                axis=0,
            )
            for offset in range(taps_count)
        ]
    )
    grad_short = lax.psum(local_short.astype(jnp.bfloat16), "seq").astype(jnp.float32)
    return (grad_proj, grad_short, grad_filter)


def solution(mesh):
    in_specs = (
        P("seq", None, "tp"),
        P("seq", "tp"),
        P("seq", "tp"),
        P(None, None, "tp"),
        P("seq", "tp"),
    )
    out_specs = (P("seq", None, "tp"), P(None, None, "tp"), P("seq", "tp"))
    return jax.shard_map(body, mesh=mesh, in_specs=in_specs, out_specs=out_specs, check_vma=False)
```

profile of v0, /device:TPU:6, one launch (start us, length us, event | category | flops | bytes accessed | tf_op | source)
XLA Modules:
  0.0 534.8 jit_solution(11234137039616669725)
XLA Ops:
  12.6 12.3 %all-to-all-start.1 = ((bf16[128,32,32]{0,2,1:T(8,128)(2,1)}), bf16[128,32,32]{0,2,1:T(8,128)(2,1)S(1)}, u32[]{:S(2)}, u32[]{:S(2)}) async-start(bf16[128,32,32]{0,2,1:T(8,128)(2,1)} %bitcast.8), calls=%async_computation.1 | async-start | bytes 524288 | tf_op jit(solution)/shard_map/all_to_all | solution.py:127
  27.7 10.1 %all-to-all-done.1 = bf16[128,32,32]{0,2,1:T(8,128)(2,1)S(1)} async-done(((bf16[128,32,32]{0,2,1:T(8,128)(2,1)}), bf16[128,32,32]{0,2,1:T(8,128)(2,1)S(1)}, u32[]{:S(2)}, u32[]{:S(2)}) %all-to-all-start.1) | async-done | bytes 262176 | tf_op jit(solution)/shard_map/all_to_all | solution.py:127
  37.8 6.9 %all-to-all-start = ((bf16[128,32,32]{0,2,1:T(8,128)(2,1)}), bf16[128,32,32]{0,2,1:T(8,128)(2,1)S(1)}, u32[]{:S(2)}, u32[]{:S(2)}) async-start(bf16[128,32,32]{0,2,1:T(8,128)(2,1)} %bitcast.2), calls=%async_computation | async-start | bytes 524288 | tf_op jit(solution)/shard_map/all_to_all | solution.py:131
  50.1 2.2 fusion.73
  52.3 103.5 %all-gather.2.cloned.1.call-done = bf16[8192,1024]{1,0:T(8,128)(2,1)} async-done(((bf16[256,1024]{1,0:T(8,128)(2,1)}), bf16[8192,1024]{1,0:T(8,128)(2,1)}) %all-gather.2.cloned.1.call-update) | async-done | bytes 16777232 | tf_op jit(solution)/shard_map/all_gather | solution.py:107
  155.8 12.7 %convolution_convert_fusion = bf16[128,8192]{1,0:T(8,128)(2,1)} fusion(bf16[128,1024]{1,0:T(8,128)(2,1)S(1)} %copy-done, bf16[8192,1024]{1,0:T(8,128)(2,1)} %all-gather.2.cloned.1.call-done), kind=kOutput, calls=%fused_computation | convolution fusion | flops 2148532224 | bytes 19136512 | tf_op jit(solution)/shard_map/dot_general | solution.py:105
  168.6 3.4 convolution_subtract_fusion.7
  173.1 2.1 convolution_add_fusion.4
  182.0 2.2 convolution_subtract_fusion.8
  184.2 91.1 %all-reduce.2.cloned.1.call-done = bf16[128,8192]{1,0:T(8,128)(2,1)} async-done(((bf16[128,8192]{1,0:T(8,128)(2,1)}), bf16[128,8192]{1,0:T(8,128)(2,1)}) %all-reduce.2.cloned.1.call-update) | async-done | bytes 2097168 | tf_op jit(solution)/shard_map/psum | solution.py:111
  277.1 10.1 %all-to-all-start.3 = ((bf16[128,32,32]{0,2,1:T(8,128)(2,1)}), bf16[128,32,32]{0,2,1:T(8,128)(2,1)S(1)}, u32[]{:S(2)}, u32[]{:S(2)}) async-start(bf16[128,32,32]{0,2,1:T(8,128)(2,1)} %bitcast.22), calls=%async_computation.3 | async-start | bytes 524288 | tf_op jit(solution)/shard_map/all_to_all | solution.py:139
  288.4 2.2 convolution_add_fusion.5
  290.6 8.4 %all-to-all-done.3 = bf16[128,32,32]{0,2,1:T(8,128)(2,1)S(1)} async-done(((bf16[128,32,32]{0,2,1:T(8,128)(2,1)}), bf16[128,32,32]{0,2,1:T(8,128)(2,1)S(1)}, u32[]{:S(2)}, u32[]{:S(2)}) %all-to-all-start.3) | async-done | bytes 262176 | tf_op jit(solution)/shard_map/all_to_all | solution.py:139
  306.9 2.0 multiply_subtract_fusion.1
  322.0 3.4 multiply_add_fusion
  331.3 6.7 %all-to-all-start.5 = ((bf16[32,128,32]{1,2,0:T(8,128)(2,1)}), bf16[32,128,32]{1,2,0:T(8,128)(2,1)S(1)}, u32[]{:S(2)}, u32[]{:S(2)}) async-start(bf16[32,128,32]{1,2,0:T(8,128)(2,1)} %copy.66), calls=%async_computation.5 | async-start | bytes 524288 | tf_op jit(solution)/shard_map/all_to_all | solution.py:146
  347.6 2.1 all-to-all-done.5
  349.7 7.8 %all-to-all-start.2 = ((bf16[32,128,32]{1,2,0:T(8,128)(2,1)}), bf16[32,128,32]{1,2,0:T(8,128)(2,1)}, u32[]{:S(2)}, u32[]{:S(2)}) async-start(bf16[32,128,32]{1,2,0:T(8,128)(2,1)} %copy.52), calls=%async_computation.2 | async-start | bytes 524288 | tf_op jit(solution)/shard_map/all_to_all | solution.py:136
  362.1 7.3 %all-to-all-done.2 = bf16[32,128,32]{1,2,0:T(8,128)(2,1)} async-done(((bf16[32,128,32]{1,2,0:T(8,128)(2,1)}), bf16[32,128,32]{1,2,0:T(8,128)(2,1)}, u32[]{:S(2)}, u32[]{:S(2)}) %all-to-all-start.2) | async-done | bytes 262176 | tf_op jit(solution)/shard_map/all_to_all | solution.py:136
  369.3 6.7 %all-to-all-start.4 = ((bf16[32,128,32]{1,2,0:T(8,128)(2,1)}), bf16[32,128,32]{1,2,0:T(8,128)(2,1)S(1)}, u32[]{:S(2)}, u32[]{:S(2)}) async-start(bf16[32,128,32]{1,2,0:T(8,128)(2,1)} %copy.61), calls=%async_computation.4 | async-start | bytes 524288 | tf_op jit(solution)/shard_map/all_to_all | solution.py:145
  378.3 9.4 %all-to-all-done.4 = bf16[32,128,32]{1,2,0:T(8,128)(2,1)S(1)} async-done(((bf16[32,128,32]{1,2,0:T(8,128)(2,1)}), bf16[32,128,32]{1,2,0:T(8,128)(2,1)S(1)}, u32[]{:S(2)}, u32[]{:S(2)}) %all-to-all-start.4) | async-done | bytes 262176 | tf_op jit(solution)/shard_map/all_to_all | solution.py:145
  391.2 3.2 collective-permute-start.1
  394.6 130.0 %psum.15 = bf16[7,3,1024]{2,1,0:T(4,128)(2,1)S(1)} all-reduce(bf16[7,3,1024]{2,1,0:T(4,128)(2,1)S(1)} %constant_dynamic-update-slice_fusion), channel_id=1, replica_groups=mesh['seq'=32,'tp'=8] {'seq'}, use_global_device_ids=true, to_apply=%region_8.9 | all-reduce | flops 21504 | bytes 86016 | tf_op jit(solution)/shard_map/psum | solution.py:169
  525.4 2.3 fusion.19
  (135 shorter events, 71.4 us)
Async XLA Ops:
  7.2 148.6 %copy-start = (bf16[128,1024]{1,0:T(8,128)(2,1)S(1)}, bf16[128,1024]{1,0:T(8,128)(2,1)}, u32[]{:S(2)}) copy-start(bf16[128,1024]{1,0:T(8,128)(2,1)} %param.6) | copy-start | bytes 786436
  7.2 18.1 %copy-start.9 = (bf16[128,3,1024]{2,0,1:T(8,128)(2,1)S(1)}, bf16[128,3,1024]{2,0,1:T(8,128)(2,1)}, u32[]{:S(2)}) copy-start(bf16[128,3,1024]{2,0,1:T(8,128)(2,1)} %param.5) | copy-start | bytes 2359300
  7.2 17.7 %copy-start.21 = (f32[7,3,1024]{2,0,1:T(8,128)S(1)}, f32[7,3,1024]{2,0,1:T(8,128)}, u32[]{:S(2)}) copy-start(f32[7,3,1024]{2,0,1:T(8,128)} %param.8) | copy-start | bytes 258052
  7.2 148.6 %all-gather.2.cloned.1.call-start = ((), (), s32[]{:S(2)}) async-start(), calls=%async_computation.6 | async-start | bytes 17301504 | tf_op jit(solution)/shard_map/all_gather | solution.py:107
  8.8 16.5 %collective-permute-start = (bf16[6,3,1024]{2,0,1:T(8,128)(2,1)S(1)}, bf16[6,3,1024]{2,0,1:T(8,128)(2,1)S(1)}, u32[]{:S(2)}, u32[]{:S(2)}) collective-permute-start(bf16[6,3,1024]{2,0,1:T(8,128)(2,1)S(1)} %slice.87), channel_id=1, source_target_pairs={{0,8},{8,16},{16,24},{24,32},{32,40},{40,48},{48,56},{56,64},{64,7... | collective-permute-start | bytes 110600 | tf_op jit(solution)/shard_map/ppermute | solution.py:14
  12.6 25.2 %all-to-all-start.1 = ((bf16[128,32,32]{0,2,1:T(8,128)(2,1)}), bf16[128,32,32]{0,2,1:T(8,128)(2,1)S(1)}, u32[]{:S(2)}, u32[]{:S(2)}) async-start(bf16[128,32,32]{0,2,1:T(8,128)(2,1)} %bitcast.8), calls=%async_computation.1 | async-start | bytes 524288 | tf_op jit(solution)/shard_map/all_to_all | solution.py:127
  25.0 2.7 copy-start.11
  25.0 2.7 copy-start.13
  25.0 2.7 copy-start.15
  25.1 2.7 copy-start.17
  25.2 12.6 %copy-start.19 = (f32[1,3,1024]{2,1,0:T(4,128)}, f32[1,3,1024]{2,1,0:T(4,128)S(1)}, u32[]{:S(2)}) copy-start(f32[1,3,1024]{2,1,0:T(4,128)S(1)} %copy.95) | copy-start | bytes 36868
  37.8 137.5 %all-to-all-start = ((bf16[128,32,32]{0,2,1:T(8,128)(2,1)}), bf16[128,32,32]{0,2,1:T(8,128)(2,1)S(1)}, u32[]{:S(2)}, u32[]{:S(2)}) async-start(bf16[128,32,32]{0,2,1:T(8,128)(2,1)} %bitcast.2), calls=%async_computation | async-start | bytes 524288 | tf_op jit(solution)/shard_map/all_to_all | solution.py:131
  44.7 230.6 %all-reduce.2.cloned.1.call-start = ((), (), s32[]{:S(2)}) async-start(), calls=%async_computation.7 | async-start | bytes 4194304 | tf_op jit(solution)/shard_map/psum | solution.py:111
  277.1 21.9 %all-to-all-start.3 = ((bf16[128,32,32]{0,2,1:T(8,128)(2,1)}), bf16[128,32,32]{0,2,1:T(8,128)(2,1)S(1)}, u32[]{:S(2)}, u32[]{:S(2)}) async-start(bf16[128,32,32]{0,2,1:T(8,128)(2,1)} %bitcast.22), calls=%async_computation.3 | async-start | bytes 524288 | tf_op jit(solution)/shard_map/all_to_all | solution.py:139
  331.3 18.4 %all-to-all-start.5 = ((bf16[32,128,32]{1,2,0:T(8,128)(2,1)}), bf16[32,128,32]{1,2,0:T(8,128)(2,1)S(1)}, u32[]{:S(2)}, u32[]{:S(2)}) async-start(bf16[32,128,32]{1,2,0:T(8,128)(2,1)} %copy.66), calls=%async_computation.5 | async-start | bytes 524288 | tf_op jit(solution)/shard_map/all_to_all | solution.py:146
  349.7 19.6 %all-to-all-start.2 = ((bf16[32,128,32]{1,2,0:T(8,128)(2,1)}), bf16[32,128,32]{1,2,0:T(8,128)(2,1)}, u32[]{:S(2)}, u32[]{:S(2)}) async-start(bf16[32,128,32]{1,2,0:T(8,128)(2,1)} %copy.52), calls=%async_computation.2 | async-start | bytes 524288 | tf_op jit(solution)/shard_map/all_to_all | solution.py:136
  369.3 18.4 %all-to-all-start.4 = ((bf16[32,128,32]{1,2,0:T(8,128)(2,1)}), bf16[32,128,32]{1,2,0:T(8,128)(2,1)S(1)}, u32[]{:S(2)}, u32[]{:S(2)}) async-start(bf16[32,128,32]{1,2,0:T(8,128)(2,1)} %copy.61), calls=%async_computation.4 | async-start | bytes 524288 | tf_op jit(solution)/shard_map/all_to_all | solution.py:145
  389.4 135.9 %copy-start.12 = (f32[3,1024]{1,0:T(4,128)S(1)}, f32[3,1024]{1,0:T(4,128)}, u32[]{:S(2)}) copy-start(f32[3,1024]{1,0:T(4,128)} %copy-done.11) | copy-start | bytes 36868
  389.4 136.0 %copy-start.14 = (f32[3,1024]{1,0:T(4,128)S(1)}, f32[3,1024]{1,0:T(4,128)}, u32[]{:S(2)}) copy-start(f32[3,1024]{1,0:T(4,128)} %copy-done.13) | copy-start | bytes 36868
  389.4 136.0 %copy-start.16 = (f32[3,1024]{1,0:T(4,128)S(1)}, f32[3,1024]{1,0:T(4,128)}, u32[]{:S(2)}) copy-start(f32[3,1024]{1,0:T(4,128)} %copy-done.15) | copy-start | bytes 36868
  389.4 136.0 %copy-start.18 = (f32[3,1024]{1,0:T(4,128)S(1)}, f32[3,1024]{1,0:T(4,128)}, u32[]{:S(2)}) copy-start(f32[3,1024]{1,0:T(4,128)} %copy-done.17) | copy-start | bytes 36868
  389.4 136.0 %copy-start.20 = (f32[1,3,1024]{2,1,0:T(4,128)S(1)}, f32[1,3,1024]{2,1,0:T(4,128)}, u32[]{:S(2)}) copy-start(f32[1,3,1024]{2,1,0:T(4,128)} %copy-done.19) | copy-start | bytes 36868
  391.2 134.0 %collective-permute-start.1 = (bf16[6,3,1024]{2,0,1:T(8,128)(2,1)S(1)}, bf16[6,3,1024]{2,0,1:T(8,128)(2,1)S(1)}, u32[]{:S(2)}, u32[]{:S(2)}) collective-permute-start(bf16[6,3,1024]{2,0,1:T(8,128)(2,1)S(1)} %slice.122), channel_id=1, source_target_pairs={{8,0},{16,8},{24,16},{32,24},{40,32},{48,40},{56,48},{64,56},{72,6... | collective-permute-start | bytes 110600 | tf_op jit(solution)/shard_map/ppermute | solution.py:14
  525.4 2.3 copy-start.1
  (8 other events, 11.5 us)
Sparse Core Ops, SparseCore 0:
  10.8 144.9 all-gather.1
  168.7 106.5 all-reduce.1
where the time goes:
time: 540 us; the launch traced here: 535 us
  waiting for transfers between devices  233 us (43%)
  blocking collectives  130 us (24%)
  matrix products  64.8 us (12%)
  starting transfers between devices  56 us (10%)
  local copies, waits for them, and re-layouts  27 us (5%)
  between operations  15.1 us (3%)
  other arithmetic  9.25 us (2%)
    psum x1, blocking collectives, body(): lax.psum(local_short.astype(jnp.bfloat16), 'seq').astype(jnp.float32)  130 us
    all_gather x1, waiting for transfers between devices, body(): lax.all_gather(out_weight, 'seq', axis=0, tiled=True)  104 us
    psum x1, waiting for transfers between devices, body(): lax.psum(partial_value.astype(jnp.bfloat16), 'tp').astype(jnp.float32)  91.1 us
    dot_general x1, matrix products, body(): lax.dot_general(cotangent, lax.all_gather(out_weight, 'seq', axis=0, tile...  12.7 us
    all_to_all x1, starting transfers between devices, body(): lax.all_to_all(long_filter.astype(jnp.bfloat16), 'seq', split_axis=1, con...  12.3 us
  transfers between devices with their start and end apart: 10, of which 7 were waited for; matrix products, arithmetic and copies ran while one was open for 11% of the time, Pallas kernels for 0%

commit v1 on v0

--- a/solution.py
+++ b/solution.py
@@ -108,9 +108,9 @@
         (((1,), (1,)), ((), ())),
         preferred_element_type=jnp.float32,
     )
-    summed = lax.psum(partial_value.astype(jnp.bfloat16), "tp").astype(jnp.float32)
-    grad_out = lax.dynamic_slice_in_dim(summed, lax.axis_index("tp") * channels, channels, 1)
-    grad_out = grad_out.astype(jnp.bfloat16)
+    grad_out = lax.psum_scatter(
+        partial_value.astype(jnp.bfloat16), "tp", scatter_dimension=1, tiled=True
+    )
     lower_rows = shifted(proj[tok_rows - rim_rows :], "seq", 1)
     extended = jnp.concatenate([lower_rows, proj], axis=0)
     primed = short_weight[0] * extended[rim_rows : rim_rows + tok_rows]
@@ -166,7 +166,8 @@
             for offset in range(taps_count)
         ]
     )
-    grad_short = lax.psum(local_short.astype(jnp.bfloat16), "seq").astype(jnp.float32)
+    short_shape = local_short.shape
+    grad_short = lax.psum(local_short.reshape(-1, channels), "seq").reshape(short_shape)
     return (grad_proj, grad_short, grad_filter)
 
 

time: 540 us -> 589 us (1.091)
  waiting for transfers between devices: 233 us -> 414 us
  blocking collectives: 130 us -> 0 us
    psum x1, waiting for transfers between devices: 91.1 us -> 238 us  [body(): lax.psum(local_short.reshape(-1, channels), 'seq').reshape(short_shape)]
    psum x1 -> x0, blocking collectives: 130 us -> none  [body(): lax.psum(local_short.astype(jnp.bfloat16), 'seq').astype(jnp.float32)]
    reduce_scatter x0 -> x1, waiting for transfers between devices: none -> 24.8 us  [body(): lax.psum_scatter(partial_value.astype(jnp.bfloat16), 'tp', scatter_dimens...]
    all_gather x1, waiting for transfers between devices: 104 us -> 126 us  [body(): lax.all_gather(out_weight, 'seq', axis=0, tiled=True)]
    all_to_all x1, waiting for transfers between devices: 10.1 us -> 0.01 us  [body(): lax.all_to_all(long_filter.astype(jnp.bfloat16), 'seq', split_axis=1, con...]
  transfers between devices with their start and end apart: 10 -> 11, of which waited for: 7 -> 8; matrix products, arithmetic and copies ran while one was open for 11% -> 10% of each run, Pallas kernels for 0% -> 0%
where the time goes in v1:
time: 589 us; the launch traced here: 583 us
  waiting for transfers between devices  414 us (70%)
  matrix products  62.1 us (11%)
  starting transfers between devices  57 us (10%)
  local copies, waits for them, and re-layouts  27.9 us (5%)
  between operations  15 us (3%)
  other arithmetic  7.24 us (1%)
    psum x1, waiting for transfers between devices, body(): lax.psum(local_short.reshape(-1, channels), 'seq').reshape(short_shape)  238 us
    all_gather x1, waiting for transfers between devices, body(): lax.all_gather(out_weight, 'seq', axis=0, tiled=True)  126 us
    reduce_scatter x1, waiting for transfers between devices, body(): lax.psum_scatter(partial_value.astype(jnp.bfloat16), 'tp', scatter_dimens...  24.8 us
    dot_general x1, matrix products, body(): lax.dot_general(cotangent, lax.all_gather(out_weight, 'seq', axis=0, tile...  12.7 us
    all_to_all x1, starting transfers between devices, body(): lax.all_to_all(long_filter.astype(jnp.bfloat16), 'seq', split_axis=1, con...  12.3 us
  transfers between devices with their start and end apart: 11, of which 8 were waited for; matrix products, arithmetic and copies ran while one was open for 10% of the time, Pallas kernels for 0%

profile of v1, /device:TPU:6, one launch (start us, length us, event | category | flops | bytes accessed | tf_op | source)
XLA Modules:
  0.0 582.8 jit_solution(17212374280899392005)
XLA Ops:
  8.7 1.9 collective-permute-start
  12.6 12.3 %all-to-all-start.1 = ((bf16[128,32,32]{0,2,1:T(8,128)(2,1)}), bf16[128,32,32]{0,2,1:T(8,128)(2,1)S(1)}, u32[]{:S(2)}, u32[]{:S(2)}) async-start(bf16[128,32,32]{0,2,1:T(8,128)(2,1)} %bitcast.8), calls=%async_computation.2 | async-start | bytes 524288 | tf_op jit(solution)/shard_map/all_to_all | solution.py:127
  25.0 126.5 %all-gather.2.cloned.1.call-done = bf16[8192,1024]{1,0:T(8,128)(2,1)} async-done(((bf16[256,1024]{1,0:T(8,128)(2,1)}), bf16[8192,1024]{1,0:T(8,128)(2,1)}) %all-gather.2.cloned.1.call-update) | async-done | bytes 16777232 | tf_op jit(solution)/shard_map/all_gather | solution.py:107
  151.5 12.7 %convolution_convert_fusion = bf16[128,8192]{1,0:T(8,128)(2,1)} fusion(bf16[128,1024]{1,0:T(8,128)(2,1)S(1)} %copy-done, bf16[8192,1024]{1,0:T(8,128)(2,1)} %all-gather.2.cloned.1.call-done), kind=kOutput, calls=%fused_computation | convolution fusion | flops 2148532224 | bytes 19136512 | tf_op jit(solution)/shard_map/dot_general | solution.py:105
  167.8 7.6 %all-to-all-start = ((bf16[128,32,32]{0,2,1:T(8,128)(2,1)}), bf16[128,32,32]{0,2,1:T(8,128)(2,1)S(1)}, u32[]{:S(2)}, u32[]{:S(2)}) async-start(bf16[128,32,32]{0,2,1:T(8,128)(2,1)} %bitcast.2), calls=%async_computation.1 | async-start | bytes 524288 | tf_op jit(solution)/shard_map/all_to_all | solution.py:131
  180.0 2.1 convolution_subtract_fusion.7
  183.3 2.2 convolution_add_fusion.4
  192.1 2.2 convolution_subtract_fusion.8
  194.3 24.8 %reduce-scatter.2.cloned.1.call-done = bf16[128,1024]{1,0:T(8,128)(2,1)} async-done(((bf16[128,8192]{1,0:T(8,128)(2,1)}), bf16[128,1024]{1,0:T(8,128)(2,1)}) %reduce-scatter.2.cloned.1.call-update) | async-done | bytes 262160 | tf_op jit(solution)/shard_map/reduce_scatter | solution.py:111
  221.0 10.2 %all-to-all-start.3 = ((bf16[128,32,32]{0,2,1:T(8,128)(2,1)}), bf16[128,32,32]{0,2,1:T(8,128)(2,1)S(1)}, u32[]{:S(2)}, u32[]{:S(2)}) async-start(bf16[128,32,32]{0,2,1:T(8,128)(2,1)} %bitcast.22), calls=%async_computation.4 | async-start | bytes 524288 | tf_op jit(solution)/shard_map/all_to_all | solution.py:139
  232.3 2.1 convolution_add_fusion.5
  234.5 8.5 %all-to-all-done.3 = bf16[128,32,32]{0,2,1:T(8,128)(2,1)S(1)} async-done(((bf16[128,32,32]{0,2,1:T(8,128)(2,1)}), bf16[128,32,32]{0,2,1:T(8,128)(2,1)S(1)}, u32[]{:S(2)}, u32[]{:S(2)}) %all-to-all-start.3) | async-done | bytes 262176 | tf_op jit(solution)/shard_map/all_to_all | solution.py:139
  250.8 2.0 multiply_subtract_fusion.1
  265.9 3.5 multiply_add_fusion
  277.4 6.9 %all-to-all-start.2 = ((bf16[32,128,32]{1,2,0:T(8,128)(2,1)}), bf16[32,128,32]{1,2,0:T(8,128)(2,1)S(1)}, u32[]{:S(2)}, u32[]{:S(2)}) async-start(bf16[32,128,32]{1,2,0:T(8,128)(2,1)} %copy.52), calls=%async_computation.3 | async-start | bytes 524288 | tf_op jit(solution)/shard_map/all_to_all | solution.py:136
  291.3 4.7 all-to-all-done.2
  296.0 6.8 %all-to-all-start.4 = ((bf16[32,128,32]{1,2,0:T(8,128)(2,1)}), bf16[32,128,32]{1,2,0:T(8,128)(2,1)S(1)}, u32[]{:S(2)}, u32[]{:S(2)}) async-start(bf16[32,128,32]{1,2,0:T(8,128)(2,1)} %copy.61), calls=%async_computation.5 | async-start | bytes 524288 | tf_op jit(solution)/shard_map/all_to_all | solution.py:145
  302.8 2.5 fusion.168
  308.8 5.7 all-to-all-done.4
  314.5 6.8 %all-to-all-start.5 = ((bf16[32,128,32]{1,2,0:T(8,128)(2,1)}), bf16[32,128,32]{1,2,0:T(8,128)(2,1)S(1)}, u32[]{:S(2)}, u32[]{:S(2)}) async-start(bf16[32,128,32]{1,2,0:T(8,128)(2,1)} %copy.66), calls=%async_computation.6 | async-start | bytes 524288 | tf_op jit(solution)/shard_map/all_to_all | solution.py:146
  325.2 4.3 collective-permute-start.1
  329.6 3.4 all-to-all-done.5
  334.3 2.3 fusion.19
  336.6 237.6 %all-reduce.2.cloned.1.call-done = f32[7,3,1024]{2,1,0:T(4,128)} async-done(((f32[7,3,1024]{2,1,0:T(4,128)}), f32[7,3,1024]{2,1,0:T(4,128)}) %all-reduce.2.cloned.1.call-update) | async-done | bytes 86032 | tf_op jit(solution)/shard_map/psum | solution.py:170
  (137 shorter events, 68.1 us)
Async XLA Ops:
  7.2 144.4 %copy-start = (bf16[128,1024]{1,0:T(8,128)(2,1)S(1)}, bf16[128,1024]{1,0:T(8,128)(2,1)}, u32[]{:S(2)}) copy-start(bf16[128,1024]{1,0:T(8,128)(2,1)} %param.6) | copy-start | bytes 786436
  7.2 17.8 %copy-start.21 = (f32[7,3,1024]{2,0,1:T(8,128)S(1)}, f32[7,3,1024]{2,0,1:T(8,128)}, u32[]{:S(2)}) copy-start(f32[7,3,1024]{2,0,1:T(8,128)} %param.8) | copy-start | bytes 258052
  7.2 144.3 %all-gather.2.cloned.1.call-start = ((), (), s32[]{:S(2)}) async-start(), calls=%async_computation.7 | async-start | bytes 17301504 | tf_op jit(solution)/shard_map/all_gather | solution.py:107
  8.7 155.8 %collective-permute-start = (bf16[6,3,1024]{2,0,1:T(8,128)(2,1)S(1)}, bf16[6,3,1024]{2,0,1:T(8,128)(2,1)S(1)}, u32[]{:S(2)}, u32[]{:S(2)}) collective-permute-start(bf16[6,3,1024]{2,0,1:T(8,128)(2,1)S(1)} %slice.87), channel_id=1, source_target_pairs={{0,8},{8,16},{16,24},{24,32},{32,40},{40,48},{48,56},{56,64},{64,7... | collective-permute-start | bytes 110600 | tf_op jit(solution)/shard_map/ppermute | solution.py:14
  12.6 155.3 %all-to-all-start.1 = ((bf16[128,32,32]{0,2,1:T(8,128)(2,1)}), bf16[128,32,32]{0,2,1:T(8,128)(2,1)S(1)}, u32[]{:S(2)}, u32[]{:S(2)}) async-start(bf16[128,32,32]{0,2,1:T(8,128)(2,1)} %bitcast.8), calls=%async_computation.2 | async-start | bytes 524288 | tf_op jit(solution)/shard_map/all_to_all | solution.py:127
  24.9 194.2 %reduce-scatter.2.cloned.1.call-start = ((), (), s32[]{:S(2)}) async-start(), calls=%async_computation.8 | async-start | bytes 2359296 | tf_op jit(solution)/shard_map/reduce_scatter | solution.py:111
  164.3 3.5 copy-start.11
  164.3 3.5 copy-start.13
  164.3 3.5 copy-start.15
  164.3 3.5 copy-start.17
  164.5 3.3 copy-start.19
  167.8 19.3 %all-to-all-start = ((bf16[128,32,32]{0,2,1:T(8,128)(2,1)}), bf16[128,32,32]{0,2,1:T(8,128)(2,1)S(1)}, u32[]{:S(2)}, u32[]{:S(2)}) async-start(bf16[128,32,32]{0,2,1:T(8,128)(2,1)} %bitcast.2), calls=%async_computation.1 | async-start | bytes 524288 | tf_op jit(solution)/shard_map/all_to_all | solution.py:131
  221.0 22.0 %all-to-all-start.3 = ((bf16[128,32,32]{0,2,1:T(8,128)(2,1)}), bf16[128,32,32]{0,2,1:T(8,128)(2,1)S(1)}, u32[]{:S(2)}, u32[]{:S(2)}) async-start(bf16[128,32,32]{0,2,1:T(8,128)(2,1)} %bitcast.22), calls=%async_computation.4 | async-start | bytes 524288 | tf_op jit(solution)/shard_map/all_to_all | solution.py:139
  248.6 1.5 copy-start.3
  248.6 1.8 copy-start.4
  248.7 2.1 copy-start.5
  277.4 8.7 %copy-start.6 = (f32[128,64,32]{0,1,2:T(8,128)S(1)}, f32[128,64,32]{0,1,2:T(8,128)}, u32[]{:S(2)}) copy-start(f32[128,64,32]{0,1,2:T(8,128)} %get-tuple-element.48) | copy-start | bytes 3145732
  277.4 18.6 %all-to-all-start.2 = ((bf16[32,128,32]{1,2,0:T(8,128)(2,1)}), bf16[32,128,32]{1,2,0:T(8,128)(2,1)S(1)}, u32[]{:S(2)}, u32[]{:S(2)}) async-start(bf16[32,128,32]{1,2,0:T(8,128)(2,1)} %copy.52), calls=%async_computation.3 | async-start | bytes 524288 | tf_op jit(solution)/shard_map/all_to_all | solution.py:136
  296.0 18.5 %all-to-all-start.4 = ((bf16[32,128,32]{1,2,0:T(8,128)(2,1)}), bf16[32,128,32]{1,2,0:T(8,128)(2,1)S(1)}, u32[]{:S(2)}, u32[]{:S(2)}) async-start(bf16[32,128,32]{1,2,0:T(8,128)(2,1)} %copy.61), calls=%async_computation.5 | async-start | bytes 524288 | tf_op jit(solution)/shard_map/all_to_all | solution.py:145
  314.5 18.5 %all-to-all-start.5 = ((bf16[32,128,32]{1,2,0:T(8,128)(2,1)}), bf16[32,128,32]{1,2,0:T(8,128)(2,1)S(1)}, u32[]{:S(2)}, u32[]{:S(2)}) async-start(bf16[32,128,32]{1,2,0:T(8,128)(2,1)} %copy.66), calls=%async_computation.6 | async-start | bytes 524288 | tf_op jit(solution)/shard_map/all_to_all | solution.py:146
  321.3 252.9 %all-reduce.2.cloned.1.call-start = ((), (), s32[]{:S(2)}) async-start(), calls=%async_computation.9 | async-start | bytes 229376 | tf_op jit(solution)/shard_map/psum | solution.py:170
  325.2 9.0 %collective-permute-start.1 = (bf16[6,3,1024]{2,0,1:T(8,128)(2,1)S(1)}, bf16[6,3,1024]{2,0,1:T(8,128)(2,1)S(1)}, u32[]{:S(2)}, u32[]{:S(2)}) collective-permute-start(bf16[6,3,1024]{2,0,1:T(8,128)(2,1)S(1)} %slice.122), channel_id=1, source_target_pairs={{8,0},{16,8},{24,16},{32,24},{40,32},{48,40},{56,48},{64,56},{72,6... | collective-permute-start | bytes 110600 | tf_op jit(solution)/shard_map/ppermute | solution.py:14
  329.6 4.6 copy-start.10
  334.3 241.5 %copy-start.1 = (bf16[128,1024]{1,0:T(8,128)(2,1)S(1)}, bf16[128,1024]{1,0:T(8,128)(2,1)}, u32[]{:S(2)}) copy-start(bf16[128,1024]{1,0:T(8,128)(2,1)} %param.6) | copy-start | bytes 786436
  (9 other events, 10.3 us)
Sparse Core Ops, SparseCore 0:
  10.8 140.6 all-gather.1
  164.4 54.6 reduce-scatter.1
  334.3 239.8 all-reduce.1

commit v2 on v0

--- a/solution.py
+++ b/solution.py
@@ -97,20 +97,40 @@
     return (left_array.astype(jnp.float32) * right_array.astype(jnp.float32)).astype(jnp.bfloat16)
 
 
-def body(proj, cotangent, out_weight, short_weight, long_filter):
+def output_grad(cotangent, out_weight):
+    weight_rows = lax.all_gather(out_weight, "lo", axis=0, tiled=True)
+    token_rows = lax.all_gather(cotangent, "hi", axis=0, tiled=True)
+    partial_value = lax.dot_general(
+        token_rows,
+        weight_rows,
+        (((1,), (1,)), ((), ())),
+        preferred_element_type=jnp.float32,
+    ).astype(jnp.bfloat16)
+    summed = lax.psum_scatter(partial_value, "tp", scatter_dimension=0, tiled=True)
+    hi_count = lax.axis_size("hi")
+    tp_count = lax.axis_size("tp")
+    pairs = [
+        (row * tp_count + col, col * tp_count + row)
+        for row in range(hi_count)
+        for col in range(tp_count)
+    ]
+    return lax.ppermute(summed, ("hi", "tp"), pairs)
+
+
+def butterfly_sum(value, axis):
+    devices = lax.axis_size(axis)
+    stride = 1
+    while stride < devices:
+        value = value + lax.ppermute(value, axis, [(i, i ^ stride) for i in range(devices)])
+        stride *= 2
+    return value
+
+
+def body(proj, grad_out, short_weight, long_filter):
     tok_rows = proj.shape[0]
     channels = proj.shape[2]
     taps_count = short_weight.shape[0]
     rim_rows = taps_count - 1
-    partial_value = lax.dot_general(
-        cotangent,
-        lax.all_gather(out_weight, "seq", axis=0, tiled=True),
-        (((1,), (1,)), ((), ())),
-        preferred_element_type=jnp.float32,
-    )
-    summed = lax.psum(partial_value.astype(jnp.bfloat16), "tp").astype(jnp.float32)
-    grad_out = lax.dynamic_slice_in_dim(summed, lax.axis_index("tp") * channels, channels, 1)
-    grad_out = grad_out.astype(jnp.bfloat16)
     lower_rows = shifted(proj[tok_rows - rim_rows :], "seq", 1)
     extended = jnp.concatenate([lower_rows, proj], axis=0)
     primed = short_weight[0] * extended[rim_rows : rim_rows + tok_rows]
@@ -166,17 +186,34 @@
             for offset in range(taps_count)
         ]
     )
-    grad_short = lax.psum(local_short.astype(jnp.bfloat16), "seq").astype(jnp.float32)
+    grad_short = butterfly_sum(local_short, "seq")
     return (grad_proj, grad_short, grad_filter)
 
 
 def solution(mesh):
+    seq_count = mesh.shape["seq"]
+    tp_count = mesh.shape["tp"]
+    split_mesh = jax.sharding.Mesh(
+        mesh.devices.reshape(tp_count, seq_count // tp_count, tp_count), ("hi", "lo", "tp")
+    )
+    grad_out_fn = jax.shard_map(
+        output_grad,
+        mesh=split_mesh,
+        in_specs=(P(("hi", "lo"), "tp"), P(("hi", "lo"), "tp")),
+        out_specs=P(("hi", "lo"), "tp"),
+        check_vma=False,
+    )
     in_specs = (
         P("seq", None, "tp"),
         P("seq", "tp"),
-        P("seq", "tp"),
         P(None, None, "tp"),
         P("seq", "tp"),
     )
     out_specs = (P("seq", None, "tp"), P(None, None, "tp"), P("seq", "tp"))
-    return jax.shard_map(body, mesh=mesh, in_specs=in_specs, out_specs=out_specs, check_vma=False)
+    body_fn = jax.shard_map(body, mesh=mesh, in_specs=in_specs, out_specs=out_specs, check_vma=False)
+
+    def run(proj, cotangent, out_weight, short_weight, long_filter):
+        grad_out = grad_out_fn(cotangent, out_weight)
+        return body_fn(proj, grad_out, short_weight, long_filter)
+
+    return run

time: 540 us -> 355 us (0.66)
  blocking collectives: 130 us -> 0 us
  waiting for transfers between devices: 233 us -> 170 us
  starting transfers between devices: 56 us -> 74.7 us
  matrix products: 64.8 us -> 56.4 us
    psum x1 -> x0, blocking collectives: 130 us -> none  [body(): lax.psum(local_short.astype(jnp.bfloat16), 'seq').astype(jnp.float32)]
    psum x1 -> x0, waiting for transfers between devices: 91.1 us -> none  [body(): lax.psum(partial_value.astype(jnp.bfloat16), 'tp').astype(jnp.float32)]
    ppermute x0 -> x6, waiting for transfers between devices: none -> 35.2 us  [the longest x5 18 us: butterfly_sum(): lax.ppermute(value, axis, [(i, i ^ stride) for i in range(devices)])]
    reduce_scatter x0 -> x1, waiting for transfers between devices: none -> 25.8 us  [output_grad(): lax.psum_scatter(partial_value, 'tp', scatter_dimension=0, tiled=True)]
    ppermute x0 -> x6, starting transfers between devices: none -> 16.5 us  [the longest x5 9.9 us: butterfly_sum(): lax.ppermute(value, axis, [(i, i ^ stride) for i in range(devices)])]
    all_gather x1 -> x2, waiting for transfers between devices: 104 us -> 88.4 us  [the longest x1 64.1 us: output_grad(): token_rows = lax.all_gather(cotangent, 'hi', axis=0, tiled=True)]
    all_to_all x1, waiting for transfers between devices: 10.1 us -> 0.01 us  [body(): lax.all_to_all(long_filter.astype(jnp.bfloat16), 'seq', split_axis=1, con...]
    all_to_all x1, waiting for transfers between devices: 9.44 us -> 0.66 us  [body(): lax.all_to_all(gated_grad_cols, 'seq', split_axis=0, concat_axis=1, tiled...]
  transfers between devices with their start and end apart: 10 -> 17, of which waited for: 7 -> 13; matrix products, arithmetic and copies ran while one was open for 11% -> 16% of each run, Pallas kernels for 0% -> 0%
where the time goes in v2:
time: 355 us; the launch traced here: 350 us
  waiting for transfers between devices  170 us (48%)
  starting transfers between devices  74.7 us (21%)
  matrix products  56.4 us (16%)
  local copies, waits for them, and re-layouts  26.6 us (7%)
  between operations  15 us (4%)
  other arithmetic  7.51 us (2%)
    all_gather x1, waiting for transfers between devices, output_grad(): token_rows = lax.all_gather(cotangent, 'hi', axis=0, tiled=True)  64.1 us
    reduce_scatter x1, waiting for transfers between devices, output_grad(): lax.psum_scatter(partial_value, 'tp', scatter_dimension=0, tiled=True)  25.8 us
    all_gather x1, waiting for transfers between devices, output_grad(): weight_rows = lax.all_gather(out_weight, 'lo', axis=0, tiled=True)  24.2 us
    ppermute x5, waiting for transfers between devices, butterfly_sum(): lax.ppermute(value, axis, [(i, i ^ stride) for i in range(devices)])  18 us
    ppermute x1, waiting for transfers between devices, output_grad(): return lax.ppermute(summed, ('hi', 'tp'), pairs)  17.3 us
    all_to_all x1, starting transfers between devices, body(): lax.all_to_all(long_filter.astype(jnp.bfloat16), 'seq', split_axis=1, con...  12.3 us
    ppermute x5, starting transfers between devices, butterfly_sum(): lax.ppermute(value, axis, [(i, i ^ stride) for i in range(devices)])  9.9 us
    all_to_all x1, starting transfers between devices, body(): lax.all_to_all(grad_conv, 'seq', split_axis=1, concat_axis=0, tiled=True)  9.7 us
  transfers between devices with their start and end apart: 17, of which 13 were waited for; matrix products, arithmetic and copies ran while one was open for 16% of the time, Pallas kernels for 0%

profile of v2, /device:TPU:6, one launch (start us, length us, event | category | flops | bytes accessed | tf_op | source)
XLA Modules:
  0.0 350.0 jit_solution(6616618055552284803)
XLA Ops:
  13.3 12.3 %all-to-all-start.1 = ((bf16[128,32,32]{0,2,1:T(8,128)(2,1)}), bf16[128,32,32]{0,2,1:T(8,128)(2,1)S(1)}, u32[]{:S(2)}, u32[]{:S(2)}) async-start(bf16[128,32,32]{0,2,1:T(8,128)(2,1)} %bitcast.8), calls=%async_computation.2 | async-start | bytes 524288 | tf_op jit(solution)/shard_map/all_to_all | solution.py:147
  25.7 24.2 %all-gather.5.cloned.1.call-done = bf16[1024,1024]{1,0:T(8,128)(2,1)} async-done(((bf16[256,1024]{1,0:T(8,128)(2,1)}), bf16[1024,1024]{1,0:T(8,128)(2,1)}) %all-gather.5.cloned.1.call-update) | async-done | bytes 2097168 | tf_op jit(solution)/shard_map/all_gather | solution.py:101
  49.9 64.1 %all-gather.3.cloned.1.call-done = bf16[1024,1024]{1,0:T(8,128)(2,1)} async-done(((bf16[128,1024]{1,0:T(8,128)(2,1)}), bf16[1024,1024]{1,0:T(8,128)(2,1)}) %all-gather.3.cloned.1.call-update) | async-done | bytes 2097168 | tf_op jit(solution)/shard_map/all_gather | solution.py:102
  114.0 5.9 %convolution_convert_fusion = bf16[1024,1024]{1,0:T(8,128)(2,1)} fusion(bf16[1024,1024]{1,0:T(8,128)(2,1)} %all-gather.3.cloned.1.call-done, bf16[1024,1024]{1,0:T(8,128)(2,1)} %all-gather.5.cloned.1.call-done), kind=kOutput, calls=%fused_computation.29 | convolution fusion | flops 2148532224 | bytes 6291456 | tf_op jit(solution)/shard_map/dot_general | solution.py:103
  123.7 8.6 %all-to-all-start = ((bf16[128,32,32]{0,2,1:T(8,128)(2,1)}), bf16[128,32,32]{0,2,1:T(8,128)(2,1)S(1)}, u32[]{:S(2)}, u32[]{:S(2)}) async-start(bf16[128,32,32]{0,2,1:T(8,128)(2,1)} %bitcast.2), calls=%async_computation.1 | async-start | bytes 524288 | tf_op jit(solution)/shard_map/all_to_all | solution.py:151
  147.3 2.7 fusion.71
  150.0 25.8 %reduce-scatter.2.cloned.1.call-done = bf16[128,1024]{1,0:T(8,128)(2,1)} async-done(((bf16[1024,1024]{1,0:T(8,128)(2,1)}), bf16[128,1024]{1,0:T(8,128)(2,1)}) %reduce-scatter.2.cloned.1.call-update) | async-done | bytes 262160 | tf_op jit(solution)/shard_map/reduce_scatter | solution.py:109
  175.8 6.6 %collective-permute-start = (bf16[128,1024]{1,0:T(8,128)(2,1)}, bf16[128,1024]{1,0:T(8,128)(2,1)S(1)}, u32[]{:S(2)}, u32[]{:S(2)}) collective-permute-start(bf16[128,1024]{1,0:T(8,128)(2,1)} %reduce-scatter.2.cloned.1.call-done), channel_id=1, source_target_pairs={{0,0},{1,32},{2,64},{3,96},{4,128},{5,160},{6,192},{7,224},{32,1},... | collective-permute-start | bytes 786440 | tf_op jit(solution)/shard_map/ppermute | solution.py:117
  182.4 3.4 convolution_subtract_fusion.8
  185.8 17.3 %collective-permute-done = bf16[128,1024]{1,0:T(8,128)(2,1)S(1)} collective-permute-done((bf16[128,1024]{1,0:T(8,128)(2,1)}, bf16[128,1024]{1,0:T(8,128)(2,1)S(1)}, u32[]{:S(2)}, u32[]{:S(2)}) %collective-permute-start) | collective-permute-done | bytes 262176 | tf_op jit(solution)/shard_map/ppermute | solution.py:117
  204.7 9.7 %all-to-all-start.3 = ((bf16[128,32,32]{0,2,1:T(8,128)(2,1)}), bf16[128,32,32]{0,2,1:T(8,128)(2,1)S(1)}, u32[]{:S(2)}, u32[]{:S(2)}) async-start(bf16[128,32,32]{0,2,1:T(8,128)(2,1)} %bitcast.22), calls=%async_computation.4 | async-start | bytes 524288 | tf_op jit(solution)/shard_map/all_to_all | solution.py:159
  217.8 8.5 %all-to-all-done.3 = bf16[128,32,32]{0,2,1:T(8,128)(2,1)S(1)} async-done(((bf16[128,32,32]{0,2,1:T(8,128)(2,1)}), bf16[128,32,32]{0,2,1:T(8,128)(2,1)S(1)}, u32[]{:S(2)}, u32[]{:S(2)}) %all-to-all-start.3) | async-done | bytes 262176 | tf_op jit(solution)/shard_map/all_to_all | solution.py:159
  249.2 3.4 multiply_add_fusion
  258.4 7.1 %all-to-all-start.4 = ((bf16[32,128,32]{1,2,0:T(8,128)(2,1)}), bf16[32,128,32]{1,2,0:T(8,128)(2,1)S(1)}, u32[]{:S(2)}, u32[]{:S(2)}) async-start(bf16[32,128,32]{1,2,0:T(8,128)(2,1)} %copy.63), calls=%async_computation.5 | async-start | bytes 524288 | tf_op jit(solution)/shard_map/all_to_all | solution.py:165
  277.0 9.2 %all-to-all-start.2 = ((bf16[32,128,32]{1,2,0:T(8,128)(2,1)}), bf16[32,128,32]{1,2,0:T(8,128)(2,1)}, u32[]{:S(2)}, u32[]{:S(2)}) async-start(bf16[32,128,32]{1,2,0:T(8,128)(2,1)} %copy.54), calls=%async_computation.3 | async-start | bytes 524288 | tf_op jit(solution)/shard_map/all_to_all | solution.py:156
  289.9 8.2 %all-to-all-done.2 = bf16[32,128,32]{1,2,0:T(8,128)(2,1)} async-done(((bf16[32,128,32]{1,2,0:T(8,128)(2,1)}), bf16[32,128,32]{1,2,0:T(8,128)(2,1)}, u32[]{:S(2)}, u32[]{:S(2)}) %all-to-all-start.2) | async-done | bytes 262176 | tf_op jit(solution)/shard_map/all_to_all | solution.py:156
  298.1 6.7 %all-to-all-start.5 = ((bf16[32,128,32]{1,2,0:T(8,128)(2,1)}), bf16[32,128,32]{1,2,0:T(8,128)(2,1)S(1)}, u32[]{:S(2)}, u32[]{:S(2)}) async-start(bf16[32,128,32]{1,2,0:T(8,128)(2,1)} %copy.68), calls=%async_computation.6 | async-start | bytes 524288 | tf_op jit(solution)/shard_map/all_to_all | solution.py:166
  311.3 4.1 %collective-permute-done.4 = f32[7,3,1024]{2,1,0:T(4,128)S(1)} collective-permute-done((f32[7,3,1024]{2,1,0:T(4,128)S(1)}, f32[7,3,1024]{2,1,0:T(4,128)S(1)}, u32[]{:S(2)}, u32[]{:S(2)}) %collective-permute-start.4) | collective-permute-done | bytes 86048 | tf_op jit(solution)/shard_map/ppermute | solution.py:124
  315.5 3.4 collective-permute-start.5
  319.0 2.5 collective-permute-start.2
  324.5 4.0 %collective-permute-start.6 = (f32[7,3,1024]{2,1,0:T(4,128)S(1)}, f32[7,3,1024]{2,1,0:T(4,128)S(1)}, u32[]{:S(2)}, u32[]{:S(2)}) collective-permute-start(f32[7,3,1024]{2,1,0:T(4,128)S(1)} %add.322), channel_id=1, source_target_pairs={{0,64},{8,72},{16,80},{24,88},{32,96},{40,104},{48,112},{56,120},{... | collective-permute-start | bytes 258056 | tf_op jit(solution)/shard_map/ppermute | solution.py:124
  328.5 7.2 %collective-permute-done.6 = f32[7,3,1024]{2,1,0:T(4,128)S(1)} collective-permute-done((f32[7,3,1024]{2,1,0:T(4,128)S(1)}, f32[7,3,1024]{2,1,0:T(4,128)S(1)}, u32[]{:S(2)}, u32[]{:S(2)}) %collective-permute-start.6) | collective-permute-done | bytes 86048 | tf_op jit(solution)/shard_map/ppermute | solution.py:124
  336.3 2.3 fusion.19
  338.6 3.7 %collective-permute-done.7 = f32[7,3,1024]{2,1,0:T(4,128)S(1)} collective-permute-done((f32[7,3,1024]{2,1,0:T(4,128)S(1)}, f32[7,3,1024]{2,1,0:T(4,128)S(1)}, u32[]{:S(2)}, u32[]{:S(2)}) %collective-permute-start.7) | collective-permute-done | bytes 86048 | tf_op jit(solution)/shard_map/ppermute | solution.py:124
  (150 shorter events, 84.1 us)
Async XLA Ops:
  7.2 42.7 %all-gather.5.cloned.1.call-start = ((), (), s32[]{:S(2)}) async-start(), calls=%async_computation.8 | async-start | bytes 2621440 | tf_op jit(solution)/shard_map/all_gather | solution.py:101
  7.9 106.1 %all-gather.3.cloned.1.call-start = ((), (), s32[]{:S(2)}) async-start(), calls=%async_computation.7 | async-start | bytes 2359296 | tf_op jit(solution)/shard_map/all_gather | solution.py:102
  9.5 111.7 %collective-permute-start.1 = (bf16[6,3,1024]{2,0,1:T(8,128)(2,1)S(1)}, bf16[6,3,1024]{2,0,1:T(8,128)(2,1)S(1)}, u32[]{:S(2)}, u32[]{:S(2)}) collective-permute-start(bf16[6,3,1024]{2,0,1:T(8,128)(2,1)S(1)} %slice.87), channel_id=1, source_target_pairs={{0,8},{8,16},{16,24},{24,32},{32,40},{40,48},{48,56},{56,64},{64,7... | collective-permute-start | bytes 110600 | tf_op jit(solution)/shard_map/ppermute | solution.py:14
  13.3 110.4 %all-to-all-start.1 = ((bf16[128,32,32]{0,2,1:T(8,128)(2,1)}), bf16[128,32,32]{0,2,1:T(8,128)(2,1)S(1)}, u32[]{:S(2)}, u32[]{:S(2)}) async-start(bf16[128,32,32]{0,2,1:T(8,128)(2,1)} %bitcast.8), calls=%async_computation.2 | async-start | bytes 524288 | tf_op jit(solution)/shard_map/all_to_all | solution.py:147
  25.6 150.2 %reduce-scatter.2.cloned.1.call-start = ((), (), s32[]{:S(2)}) async-start(), calls=%async_computation.9 | async-start | bytes 2359296 | tf_op jit(solution)/shard_map/reduce_scatter | solution.py:109
  123.7 20.3 %all-to-all-start = ((bf16[128,32,32]{0,2,1:T(8,128)(2,1)}), bf16[128,32,32]{0,2,1:T(8,128)(2,1)S(1)}, u32[]{:S(2)}, u32[]{:S(2)}) async-start(bf16[128,32,32]{0,2,1:T(8,128)(2,1)} %bitcast.2), calls=%async_computation.1 | async-start | bytes 524288 | tf_op jit(solution)/shard_map/all_to_all | solution.py:151
  175.8 27.3 %collective-permute-start = (bf16[128,1024]{1,0:T(8,128)(2,1)}, bf16[128,1024]{1,0:T(8,128)(2,1)S(1)}, u32[]{:S(2)}, u32[]{:S(2)}) collective-permute-start(bf16[128,1024]{1,0:T(8,128)(2,1)} %reduce-scatter.2.cloned.1.call-done), channel_id=1, source_target_pairs={{0,0},{1,32},{2,64},{3,96},{4,128},{5,160},{6,192},{7,224},{32,1},... | collective-permute-start | bytes 786440 | tf_op jit(solution)/shard_map/ppermute | solution.py:117
  204.7 21.5 %all-to-all-start.3 = ((bf16[128,32,32]{0,2,1:T(8,128)(2,1)}), bf16[128,32,32]{0,2,1:T(8,128)(2,1)S(1)}, u32[]{:S(2)}, u32[]{:S(2)}) async-start(bf16[128,32,32]{0,2,1:T(8,128)(2,1)} %bitcast.22), calls=%async_computation.4 | async-start | bytes 524288 | tf_op jit(solution)/shard_map/all_to_all | solution.py:159
  258.4 18.7 %all-to-all-start.4 = ((bf16[32,128,32]{1,2,0:T(8,128)(2,1)}), bf16[32,128,32]{1,2,0:T(8,128)(2,1)S(1)}, u32[]{:S(2)}, u32[]{:S(2)}) async-start(bf16[32,128,32]{1,2,0:T(8,128)(2,1)} %copy.63), calls=%async_computation.5 | async-start | bytes 524288 | tf_op jit(solution)/shard_map/all_to_all | solution.py:165
  265.4 3.3 copy-start.4
  277.0 21.1 %all-to-all-start.2 = ((bf16[32,128,32]{1,2,0:T(8,128)(2,1)}), bf16[32,128,32]{1,2,0:T(8,128)(2,1)}, u32[]{:S(2)}, u32[]{:S(2)}) async-start(bf16[32,128,32]{1,2,0:T(8,128)(2,1)} %copy.54), calls=%async_computation.3 | async-start | bytes 524288 | tf_op jit(solution)/shard_map/all_to_all | solution.py:156
  289.9 16.2 %copy-start.8 = (bf16[128,1024]{1,0:T(8,128)(2,1)S(1)}, bf16[128,1024]{1,0:T(8,128)(2,1)}, u32[]{:S(2)}) copy-start(bf16[128,1024]{1,0:T(8,128)(2,1)} %copy-done.7) | copy-start | bytes 786436
  298.1 23.4 %all-to-all-start.5 = ((bf16[32,128,32]{1,2,0:T(8,128)(2,1)}), bf16[32,128,32]{1,2,0:T(8,128)(2,1)S(1)}, u32[]{:S(2)}, u32[]{:S(2)}) async-start(bf16[32,128,32]{1,2,0:T(8,128)(2,1)} %copy.68), calls=%async_computation.6 | async-start | bytes 524288 | tf_op jit(solution)/shard_map/all_to_all | solution.py:166
  308.1 1.4 collective-permute-start.3
  309.5 5.9 %collective-permute-start.4 = (f32[7,3,1024]{2,1,0:T(4,128)S(1)}, f32[7,3,1024]{2,1,0:T(4,128)S(1)}, u32[]{:S(2)}, u32[]{:S(2)}) collective-permute-start(f32[7,3,1024]{2,1,0:T(4,128)S(1)} %add.320), channel_id=1, source_target_pairs={{0,16},{8,24},{16,0},{24,8},{32,48},{40,56},{48,32},{56,40},{64,80... | collective-permute-start | bytes 258056 | tf_op jit(solution)/shard_map/ppermute | solution.py:124
  315.5 8.9 %collective-permute-start.5 = (f32[7,3,1024]{2,1,0:T(4,128)S(1)}, f32[7,3,1024]{2,1,0:T(4,128)S(1)}, u32[]{:S(2)}, u32[]{:S(2)}) collective-permute-start(f32[7,3,1024]{2,1,0:T(4,128)S(1)} %add.321), channel_id=1, source_target_pairs={{0,32},{8,40},{16,48},{24,56},{32,0},{40,8},{48,16},{56,24},{64,96... | collective-permute-start | bytes 258056 | tf_op jit(solution)/shard_map/ppermute | solution.py:124
  319.0 9.5 %collective-permute-start.2 = (bf16[6,3,1024]{2,0,1:T(8,128)(2,1)S(1)}, bf16[6,3,1024]{2,0,1:T(8,128)(2,1)S(1)}, u32[]{:S(2)}, u32[]{:S(2)}) collective-permute-start(bf16[6,3,1024]{2,0,1:T(8,128)(2,1)S(1)} %slice.122), channel_id=1, source_target_pairs={{8,0},{16,8},{24,16},{32,24},{40,32},{48,40},{56,48},{64,56},{72,6... | collective-permute-start | bytes 110600 | tf_op jit(solution)/shard_map/ppermute | solution.py:14
  321.6 14.7 %copy-start.10 = (f32[3,1024]{1,0:T(4,128)S(1)}, f32[3,1024]{1,0:T(4,128)}, u32[]{:S(2)}) copy-start(f32[3,1024]{1,0:T(4,128)} %copy-done.9) | copy-start | bytes 36868
  321.6 14.7 %copy-start.12 = (f32[3,1024]{1,0:T(4,128)S(1)}, f32[3,1024]{1,0:T(4,128)}, u32[]{:S(2)}) copy-start(f32[3,1024]{1,0:T(4,128)} %copy-done.11) | copy-start | bytes 36868
  321.6 14.7 %copy-start.14 = (f32[3,1024]{1,0:T(4,128)S(1)}, f32[3,1024]{1,0:T(4,128)}, u32[]{:S(2)}) copy-start(f32[3,1024]{1,0:T(4,128)} %copy-done.13) | copy-start | bytes 36868
  321.6 14.7 %copy-start.16 = (f32[3,1024]{1,0:T(4,128)S(1)}, f32[3,1024]{1,0:T(4,128)}, u32[]{:S(2)}) copy-start(f32[3,1024]{1,0:T(4,128)} %copy-done.15) | copy-start | bytes 36868
  321.6 14.7 %copy-start.18 = (f32[1,3,1024]{2,1,0:T(4,128)S(1)}, f32[1,3,1024]{2,1,0:T(4,128)}, u32[]{:S(2)}) copy-start(f32[1,3,1024]{2,1,0:T(4,128)} %copy-done.17) | copy-start | bytes 36868
  324.5 11.2 %collective-permute-start.6 = (f32[7,3,1024]{2,1,0:T(4,128)S(1)}, f32[7,3,1024]{2,1,0:T(4,128)S(1)}, u32[]{:S(2)}, u32[]{:S(2)}) collective-permute-start(f32[7,3,1024]{2,1,0:T(4,128)S(1)} %add.322), channel_id=1, source_target_pairs={{0,64},{8,72},{16,80},{24,88},{32,96},{40,104},{48,112},{56,120},{... | collective-permute-start | bytes 258056 | tf_op jit(solution)/shard_map/ppermute | solution.py:124
  335.7 6.5 %collective-permute-start.7 = (f32[7,3,1024]{2,1,0:T(4,128)S(1)}, f32[7,3,1024]{2,1,0:T(4,128)S(1)}, u32[]{:S(2)}, u32[]{:S(2)}) collective-permute-start(f32[7,3,1024]{2,1,0:T(4,128)S(1)} %add.323), channel_id=1, source_target_pairs={{0,128},{8,136},{16,144},{24,152},{32,160},{40,168},{48,176},{56,1... | collective-permute-start | bytes 258056 | tf_op jit(solution)/shard_map/ppermute | solution.py:124
  (13 other events, 24.2 us)
Sparse Core Ops, SparseCore 0:
  9.8 40.0 all-gather.4
  52.5 61.4 all-gather.2
  120.1 55.6 reduce-scatter.1

commit v3 on v2

--- a/solution.py
+++ b/solution.py
@@ -6,6 +6,7 @@
 from jax.sharding import PartitionSpec as P
 
 highest = lax.Precision.HIGHEST
+SEQ = ("hi", "lo")
 
 
 def shifted(value, axis, by):
@@ -97,9 +98,10 @@
     return (left_array.astype(jnp.float32) * right_array.astype(jnp.float32)).astype(jnp.bfloat16)
 
 
-def output_grad(cotangent, out_weight):
+def output_grad(cotangent, out_weight, ready):
     weight_rows = lax.all_gather(out_weight, "lo", axis=0, tiled=True)
     token_rows = lax.all_gather(cotangent, "hi", axis=0, tiled=True)
+    weight_rows, token_rows, _ = lax.optimization_barrier((weight_rows, token_rows, ready))
     partial_value = lax.dot_general(
         token_rows,
         weight_rows,
@@ -126,12 +128,12 @@
     return value
 
 
-def body(proj, grad_out, short_weight, long_filter):
+def body(proj, cotangent, out_weight, short_weight, long_filter):
     tok_rows = proj.shape[0]
     channels = proj.shape[2]
     taps_count = short_weight.shape[0]
     rim_rows = taps_count - 1
-    lower_rows = shifted(proj[tok_rows - rim_rows :], "seq", 1)
+    lower_rows = shifted(proj[tok_rows - rim_rows :], SEQ, 1)
     extended = jnp.concatenate([lower_rows, proj], axis=0)
     primed = short_weight[0] * extended[rim_rows : rim_rows + tok_rows]
     for offset in range(1, taps_count):
@@ -145,31 +147,32 @@
     value_conv = primed[:, 2]
     gated_input = times_bf16(keys_conv, value_conv)
     filter_cols = lax.all_to_all(
-        long_filter.astype(jnp.bfloat16), "seq", split_axis=1, concat_axis=0, tiled=True
+        long_filter.astype(jnp.bfloat16), SEQ, split_axis=1, concat_axis=0, tiled=True
     ).astype(long_filter.dtype)
     filter_real, filter_imag = spectrum(filter_cols)
-    gated_cols = lax.all_to_all(gated_input, "seq", split_axis=1, concat_axis=0, tiled=True)
+    gated_cols = lax.all_to_all(gated_input, SEQ, split_axis=1, concat_axis=0, tiled=True)
     gated_real, gated_imag = spectrum(gated_cols)
     conv_cols = signal(*complex_product(gated_real, gated_imag, filter_real, filter_imag)).astype(
         jnp.bfloat16
     )
-    conv_out = lax.all_to_all(conv_cols, "seq", split_axis=0, concat_axis=1, tiled=True)
+    conv_out = lax.all_to_all(conv_cols, SEQ, split_axis=0, concat_axis=1, tiled=True)
+    grad_out = output_grad(cotangent, out_weight, conv_out)
     grad_query = times_bf16(grad_out, conv_out)
     grad_conv = times_bf16(grad_out, query_conv)
-    grad_cols = lax.all_to_all(grad_conv, "seq", split_axis=1, concat_axis=0, tiled=True)
+    grad_cols = lax.all_to_all(grad_conv, SEQ, split_axis=1, concat_axis=0, tiled=True)
     grad_real, grad_imag = spectrum(grad_cols)
     gated_grad_cols = signal(*conj_product(grad_real, grad_imag, filter_real, filter_imag)).astype(
         jnp.bfloat16
     )
     filter_grad_cols = signal(*conj_product(grad_real, grad_imag, gated_real, gated_imag))
-    gated_grad = lax.all_to_all(gated_grad_cols, "seq", split_axis=0, concat_axis=1, tiled=True)
+    gated_grad = lax.all_to_all(gated_grad_cols, SEQ, split_axis=0, concat_axis=1, tiled=True)
     grad_filter = lax.all_to_all(
-        filter_grad_cols.astype(jnp.bfloat16), "seq", split_axis=0, concat_axis=1, tiled=True
+        filter_grad_cols.astype(jnp.bfloat16), SEQ, split_axis=0, concat_axis=1, tiled=True
     ).astype(filter_grad_cols.dtype)
     grad_keys = times_bf16(gated_grad, value_conv)
     grad_value = times_bf16(gated_grad, keys_conv)
     grad_primed = jnp.stack([grad_query, grad_keys, grad_value], axis=1)
-    next_rows = shifted(grad_primed[:rim_rows], "seq", -1)
+    next_rows = shifted(grad_primed[:rim_rows], SEQ, -1)
     trailing = jnp.concatenate([grad_primed, next_rows], axis=0)
     grad_sum = short_weight[0] * trailing[0:tok_rows]
     for offset in range(1, taps_count):
@@ -186,7 +189,7 @@
             for offset in range(taps_count)
         ]
     )
-    grad_short = butterfly_sum(local_short, "seq")
+    grad_short = butterfly_sum(local_short, SEQ)
     return (grad_proj, grad_short, grad_filter)
 
 
@@ -196,24 +199,14 @@
     split_mesh = jax.sharding.Mesh(
         mesh.devices.reshape(tp_count, seq_count // tp_count, tp_count), ("hi", "lo", "tp")
     )
-    grad_out_fn = jax.shard_map(
-        output_grad,
-        mesh=split_mesh,
-        in_specs=(P(("hi", "lo"), "tp"), P(("hi", "lo"), "tp")),
-        out_specs=P(("hi", "lo"), "tp"),
-        check_vma=False,
-    )
     in_specs = (
-        P("seq", None, "tp"),
-        P("seq", "tp"),
+        P(SEQ, None, "tp"),
+        P(SEQ, "tp"),
+        P(SEQ, "tp"),
         P(None, None, "tp"),
-        P("seq", "tp"),
-    )
-    out_specs = (P("seq", None, "tp"), P(None, None, "tp"), P("seq", "tp"))
-    body_fn = jax.shard_map(body, mesh=mesh, in_specs=in_specs, out_specs=out_specs, check_vma=False)
-
-    def run(proj, cotangent, out_weight, short_weight, long_filter):
-        grad_out = grad_out_fn(cotangent, out_weight)
-        return body_fn(proj, grad_out, short_weight, long_filter)
-
-    return run
+        P(SEQ, "tp"),
+    )
+    out_specs = (P(SEQ, None, "tp"), P(None, None, "tp"), P(SEQ, "tp"))
+    return jax.shard_map(
+        body, mesh=split_mesh, in_specs=in_specs, out_specs=out_specs, check_vma=False
+    )

time: 355 us -> 331 us (0.932)
  waiting for transfers between devices: 170 us -> 121 us
  blocking collectives: 0 us -> 41.1 us
  starting transfers between devices: 74.7 us -> 56.8 us
  local copies, waits for them, and re-layouts: 26.6 us -> 33.5 us
  matrix products: 56.4 us -> 51.5 us
    all_gather x1, waiting for transfers between devices: 64.1 us -> 13.9 us  [output_grad(): token_rows = lax.all_gather(cotangent, 'hi', axis=0, tiled=True)]
    all_to_all x0 -> x2, blocking collectives: none -> 41.1 us  [the longest x1 21.6 us: body(): lax.all_to_all(grad_conv, SEQ, split_axis=1, concat_axis=0, tiled=True)]
    reduce_scatter x1, waiting for transfers between devices: 25.8 us -> 52.7 us  [output_grad(): lax.psum_scatter(partial_value, 'tp', scatter_dimension=0, tiled=True)]
    all_gather x1, waiting for transfers between devices: 24.2 us -> 0.01 us  [output_grad(): weight_rows = lax.all_gather(out_weight, 'lo', axis=0, tiled=True)]
    all_to_all x6 -> x4, starting transfers between devices: 53.7 us -> 35 us  [the longest x1 11.6 us: body(): lax.all_to_all(long_filter.astype(jnp.bfloat16), SEQ, split_axis=1, conca...]
    all_to_all x6 -> x4, waiting for transfers between devices: 19 us -> 9.47 us  [the longest x1 5.79 us: body(): lax.all_to_all(gated_grad_cols, SEQ, split_axis=0, concat_axis=1, tiled=T...]
    ppermute x2, waiting for transfers between devices: 0.01 us -> 7.1 us  [shifted(): return lax.ppermute(value, axis, pairs)]
    all_to_all x3 -> x4, local copies, waits for them, and re-layouts: 1.45 us -> 5.03 us  [the longest x1 2.27 us: body(): lax.all_to_all(grad_conv, SEQ, split_axis=1, concat_axis=0, tiled=True)]
  transfers between devices with their start and end apart: 17 -> 15, of which waited for: 13 -> 11; matrix products, arithmetic and copies ran while one was open for 16% -> 15% of each run, Pallas kernels for 0% -> 0%
where the time goes in v3:
time: 331 us; the launch traced here: 327 us
  waiting for transfers between devices  121 us (37%)
  starting transfers between devices  56.8 us (17%)
  matrix products  51.5 us (16%)
  blocking collectives  41.1 us (12%)
  local copies, waits for them, and re-layouts  33.5 us (10%)
  between operations  15.2 us (5%)
  other arithmetic  8.26 us (2%)
    reduce_scatter x1, waiting for transfers between devices, output_grad(): lax.psum_scatter(partial_value, 'tp', scatter_dimension=0, tiled=True)  52.7 us
    all_to_all x1, blocking collectives, body(): lax.all_to_all(grad_conv, SEQ, split_axis=1, concat_axis=0, tiled=True)  21.6 us
    ppermute x1, waiting for transfers between devices, output_grad(): return lax.ppermute(summed, ('hi', 'tp'), pairs)  19.9 us
    all_to_all x1, blocking collectives, body(): lax.all_to_all(conv_cols, SEQ, split_axis=0, concat_axis=1, tiled=True)  19.5 us
    ppermute x5, waiting for transfers between devices, butterfly_sum(): lax.ppermute(value, axis, [(i, i ^ stride) for i in range(devices)])  17.2 us
    all_gather x1, waiting for transfers between devices, output_grad(): token_rows = lax.all_gather(cotangent, 'hi', axis=0, tiled=True)  13.9 us
    all_to_all x1, starting transfers between devices, body(): lax.all_to_all(long_filter.astype(jnp.bfloat16), SEQ, split_axis=1, conca...  11.6 us
    all_to_all x1, starting transfers between devices, body(): lax.all_to_all(gated_input, SEQ, split_axis=1, concat_axis=0, tiled=True)  9.56 us
  transfers between devices with their start and end apart: 15, of which 11 were waited for; matrix products, arithmetic and copies ran while one was open for 15% of the time, Pallas kernels for 0%

profile of v3, /device:TPU:6, one launch (start us, length us, event | category | flops | bytes accessed | tf_op | source)
XLA Modules:
  0.0 327.3 jit_solution(17972634252082500172)
XLA Ops:
  9.8 11.6 %all-to-all-start.1 = ((bf16[128,32,32]{0,2,1:T(8,128)(2,1)}), bf16[128,32,32]{0,2,1:T(8,128)(2,1)S(1)}, u32[]{:S(2)}, u32[]{:S(2)}) async-start(bf16[128,32,32]{0,2,1:T(8,128)(2,1)} %bitcast.8), calls=%async_computation.1 | async-start | bytes 524288 | tf_op jit(solution)/shard_map/all_to_all | solution.py:149
  23.9 7.1 %collective-permute-done = bf16[6,3,1024]{2,0,1:T(8,128)(2,1)S(1)} collective-permute-done((bf16[6,3,1024]{2,0,1:T(8,128)(2,1)S(1)}, bf16[6,3,1024]{2,0,1:T(8,128)(2,1)S(1)}, u32[]{:S(2)}, u32[]{:S(2)}) %collective-permute-start) | collective-permute-done | bytes 36896 | tf_op jit(solution)/shard_map/ppermute | solution.py:15
  34.3 9.6 %all-to-all-start = ((bf16[128,32,32]{0,2,1:T(8,128)(2,1)}), bf16[128,32,32]{0,2,1:T(8,128)(2,1)S(1)}, u32[]{:S(2)}, u32[]{:S(2)}) async-start(bf16[128,32,32]{0,2,1:T(8,128)(2,1)} %bitcast.2), calls=%async_computation | async-start | bytes 524288 | tf_op jit(solution)/shard_map/all_to_all | solution.py:153
  52.5 3.7 %all-to-all-done = bf16[128,32,32]{0,2,1:T(8,128)(2,1)S(1)} async-done(((bf16[128,32,32]{0,2,1:T(8,128)(2,1)}), bf16[128,32,32]{0,2,1:T(8,128)(2,1)S(1)}, u32[]{:S(2)}, u32[]{:S(2)}) %all-to-all-start) | async-done | bytes 262176 | tf_op jit(solution)/shard_map/all_to_all | solution.py:153
  64.9 2.5 multiply_add_fusion.6
  80.1 19.5 %all_to_all.81 = bf16[32,128,32]{1,2,0:T(8,128)(2,1)} all-to-all(bf16[32,128,32]{1,2,0:T(8,128)(2,1)S(1)} %copy.52), channel_id=1, replica_groups=mesh['hi'=8,'lo'=4,'tp'=8] {'hi','lo'}, dimensions={0} | all-to-all | bytes 524288 | tf_op jit(solution)/shard_map/all_to_all | solution.py:158
  99.6 13.9 %all-gather.5.cloned.1.call-done = bf16[1024,1024]{1,0:T(8,128)(2,1)} async-done(((bf16[128,1024]{1,0:T(8,128)(2,1)}), bf16[1024,1024]{1,0:T(8,128)(2,1)}) %all-gather.5.cloned.1.call-update) | async-done | bytes 2097168 | tf_op jit(solution)/shard_map/all_gather | solution.py:103
  113.5 6.0 %convolution_convert_fusion = bf16[1024,1024]{1,0:T(8,128)(2,1)} fusion(bf16[1024,1024]{1,0:T(8,128)(2,1)} %all-gather.5.cloned.1.call-done, bf16[1024,1024]{1,0:T(8,128)(2,1)} %all-gather.3.cloned.1.call-done), kind=kOutput, calls=%fused_computation.29 | convolution fusion | flops 2148532224 | bytes 6291456 | tf_op jit(solution)/shard_map/dot_general | solution.py:105
  119.5 52.7 %reduce-scatter.2.cloned.1.call-done = bf16[128,1024]{1,0:T(8,128)(2,1)} async-done(((bf16[1024,1024]{1,0:T(8,128)(2,1)}), bf16[128,1024]{1,0:T(8,128)(2,1)}) %reduce-scatter.2.cloned.1.call-update) | async-done | bytes 262160 | tf_op jit(solution)/shard_map/reduce_scatter | solution.py:111
  172.2 6.6 %collective-permute-start.1 = (bf16[128,1024]{1,0:T(8,128)(2,1)}, bf16[128,1024]{1,0:T(8,128)(2,1)}, u32[]{:S(2)}, u32[]{:S(2)}) collective-permute-start(bf16[128,1024]{1,0:T(8,128)(2,1)} %reduce-scatter.2.cloned.1.call-done), channel_id=1, source_target_pairs={{0,0},{1,32},{2,64},{3,96},{4,128},{5,160},{6,192},{7,224},{32,1},... | collective-permute-start | bytes 786440 | tf_op jit(solution)/shard_map/ppermute | solution.py:119
  179.6 19.9 %collective-permute-done.1 = bf16[128,1024]{1,0:T(8,128)(2,1)} collective-permute-done((bf16[128,1024]{1,0:T(8,128)(2,1)}, bf16[128,1024]{1,0:T(8,128)(2,1)}, u32[]{:S(2)}, u32[]{:S(2)}) %collective-permute-start.1) | collective-permute-done | bytes 262176 | tf_op jit(solution)/shard_map/ppermute | solution.py:119
  203.3 21.6 %all_to_all.82 = bf16[128,32,32]{0,2,1:T(8,128)(2,1)} all-to-all(bf16[128,32,32]{0,2,1:T(8,128)(2,1)} %bitcast.210), channel_id=1, replica_groups=mesh['hi'=8,'lo'=4,'tp'=8] {'hi','lo'}, dimensions={1} | all-to-all | bytes 524288 | tf_op jit(solution)/shard_map/all_to_all | solution.py:162
  224.9 2.3 copy.55
  227.1 3.0 reshape.144
  257.8 7.0 %all-to-all-start.4 = ((bf16[32,128,32]{1,2,0:T(8,128)(2,1)}), bf16[32,128,32]{1,2,0:T(8,128)(2,1)S(1)}, u32[]{:S(2)}, u32[]{:S(2)}) async-start(bf16[32,128,32]{1,2,0:T(8,128)(2,1)} %copy.61), calls=%async_computation.5 | async-start | bytes 524288 | tf_op jit(solution)/shard_map/all_to_all | solution.py:168
  270.7 5.8 %all-to-all-done.4 = bf16[32,128,32]{1,2,0:T(8,128)(2,1)S(1)} async-done(((bf16[32,128,32]{1,2,0:T(8,128)(2,1)}), bf16[32,128,32]{1,2,0:T(8,128)(2,1)S(1)}, u32[]{:S(2)}, u32[]{:S(2)}) %all-to-all-start.4) | async-done | bytes 262176 | tf_op jit(solution)/shard_map/all_to_all | solution.py:168
  276.5 6.8 %all-to-all-start.5 = ((bf16[32,128,32]{1,2,0:T(8,128)(2,1)}), bf16[32,128,32]{1,2,0:T(8,128)(2,1)S(1)}, u32[]{:S(2)}, u32[]{:S(2)}) async-start(bf16[32,128,32]{1,2,0:T(8,128)(2,1)} %copy.66), calls=%async_computation.6 | async-start | bytes 524288 | tf_op jit(solution)/shard_map/all_to_all | solution.py:169
  289.3 4.6 %collective-permute-done.4 = f32[7,3,1024]{2,1,0:T(4,128)S(1)} collective-permute-done((f32[7,3,1024]{2,1,0:T(4,128)S(1)}, f32[7,3,1024]{2,1,0:T(4,128)S(1)}, u32[]{:S(2)}, u32[]{:S(2)}) %collective-permute-start.4) | collective-permute-done | bytes 86048 | tf_op jit(solution)/shard_map/ppermute | solution.py:126
  293.9 3.0 collective-permute-start.5
  297.1 3.1 collective-permute-start.2
  302.6 4.1 %collective-permute-start.6 = (f32[7,3,1024]{2,1,0:T(4,128)S(1)}, f32[7,3,1024]{2,1,0:T(4,128)S(1)}, u32[]{:S(2)}, u32[]{:S(2)}) collective-permute-start(f32[7,3,1024]{2,1,0:T(4,128)S(1)} %add.322), channel_id=1, source_target_pairs={{0,64},{8,72},{16,80},{24,88},{32,96},{40,104},{48,112},{56,120},{... | collective-permute-start | bytes 258056 | tf_op jit(solution)/shard_map/ppermute | solution.py:126
  306.7 6.7 %collective-permute-done.6 = f32[7,3,1024]{2,1,0:T(4,128)S(1)} collective-permute-done((f32[7,3,1024]{2,1,0:T(4,128)S(1)}, f32[7,3,1024]{2,1,0:T(4,128)S(1)}, u32[]{:S(2)}, u32[]{:S(2)}) %collective-permute-start.6) | collective-permute-done | bytes 86048 | tf_op jit(solution)/shard_map/ppermute | solution.py:126
  314.1 2.3 fusion.19
  316.4 3.4 %collective-permute-done.7 = f32[7,3,1024]{2,1,0:T(4,128)S(1)} collective-permute-done((f32[7,3,1024]{2,1,0:T(4,128)S(1)}, f32[7,3,1024]{2,1,0:T(4,128)S(1)}, u32[]{:S(2)}, u32[]{:S(2)}) %collective-permute-start.7) | collective-permute-done | bytes 86048 | tf_op jit(solution)/shard_map/ppermute | solution.py:126
  (144 shorter events, 85.5 us)
Async XLA Ops:
  7.2 14.3 %copy-start.4 = (bf16[128,3,1024]{2,0,1:T(8,128)(2,1)S(1)}, bf16[128,3,1024]{2,0,1:T(8,128)(2,1)}, u32[]{:S(2)}) copy-start(bf16[128,3,1024]{2,0,1:T(8,128)(2,1)} %param.5) | copy-start | bytes 2359300
  7.2 16.4 %copy-start.18 = (f32[7,3,1024]{2,0,1:T(8,128)S(1)}, f32[7,3,1024]{2,0,1:T(8,128)}, u32[]{:S(2)}) copy-start(f32[7,3,1024]{2,0,1:T(8,128)} %param.8) | copy-start | bytes 258052
  7.2 92.4 %all-gather.3.cloned.1.call-start = ((), (), s32[]{:S(2)}) async-start(), calls=%async_computation.7 | async-start | bytes 2621440 | tf_op jit(solution)/shard_map/all_gather | solution.py:102
  9.8 24.5 %all-to-all-start.1 = ((bf16[128,32,32]{0,2,1:T(8,128)(2,1)}), bf16[128,32,32]{0,2,1:T(8,128)(2,1)S(1)}, u32[]{:S(2)}, u32[]{:S(2)}) async-start(bf16[128,32,32]{0,2,1:T(8,128)(2,1)} %bitcast.8), calls=%async_computation.1 | async-start | bytes 524288 | tf_op jit(solution)/shard_map/all_to_all | solution.py:149
  21.4 92.1 %all-gather.5.cloned.1.call-start = ((), (), s32[]{:S(2)}) async-start(), calls=%async_computation.8 | async-start | bytes 2359296 | tf_op jit(solution)/shard_map/all_gather | solution.py:103
  21.5 9.5 %collective-permute-start = (bf16[6,3,1024]{2,0,1:T(8,128)(2,1)S(1)}, bf16[6,3,1024]{2,0,1:T(8,128)(2,1)S(1)}, u32[]{:S(2)}, u32[]{:S(2)}) collective-permute-start(bf16[6,3,1024]{2,0,1:T(8,128)(2,1)S(1)} %slice.87), channel_id=1, source_target_pairs={{0,8},{8,16},{16,24},{24,32},{32,40},{40,48},{48,56},{56,64},{64,7... | collective-permute-start | bytes 110600 | tf_op jit(solution)/shard_map/ppermute | solution.py:15
  34.3 21.8 %all-to-all-start = ((bf16[128,32,32]{0,2,1:T(8,128)(2,1)}), bf16[128,32,32]{0,2,1:T(8,128)(2,1)S(1)}, u32[]{:S(2)}, u32[]{:S(2)}) async-start(bf16[128,32,32]{0,2,1:T(8,128)(2,1)} %bitcast.2), calls=%async_computation | async-start | bytes 524288 | tf_op jit(solution)/shard_map/all_to_all | solution.py:153
  43.9 128.3 %reduce-scatter.2.cloned.1.call-start = ((), (), s32[]{:S(2)}) async-start(), calls=%async_computation.9 | async-start | bytes 2359296 | tf_op jit(solution)/shard_map/reduce_scatter | solution.py:111
  119.4 59.3 %copy-start.7 = (bf16[32,128,32]{1,2,0:T(8,128)(2,1)S(1)}, bf16[32,128,32]{1,2,0:T(8,128)(2,1)}, u32[]{:S(2)}) copy-start(bf16[32,128,32]{1,2,0:T(8,128)(2,1)} %all_to_all.81) | copy-start | bytes 786436
  172.2 27.4 %collective-permute-start.1 = (bf16[128,1024]{1,0:T(8,128)(2,1)}, bf16[128,1024]{1,0:T(8,128)(2,1)}, u32[]{:S(2)}, u32[]{:S(2)}) collective-permute-start(bf16[128,1024]{1,0:T(8,128)(2,1)} %reduce-scatter.2.cloned.1.call-done), channel_id=1, source_target_pairs={{0,0},{1,32},{2,64},{3,96},{4,128},{5,160},{6,192},{7,224},{32,1},... | collective-permute-start | bytes 786440 | tf_op jit(solution)/shard_map/ppermute | solution.py:119
  257.8 18.6 %all-to-all-start.4 = ((bf16[32,128,32]{1,2,0:T(8,128)(2,1)}), bf16[32,128,32]{1,2,0:T(8,128)(2,1)S(1)}, u32[]{:S(2)}, u32[]{:S(2)}) async-start(bf16[32,128,32]{1,2,0:T(8,128)(2,1)} %copy.61), calls=%async_computation.5 | async-start | bytes 524288 | tf_op jit(solution)/shard_map/all_to_all | solution.py:168
  269.6 13.9 %copy-start.1 = (bf16[128,3,1024]{2,0,1:T(8,128)(2,1)S(1)}, bf16[128,3,1024]{2,0,1:T(8,128)(2,1)}, u32[]{:S(2)}) copy-start(bf16[128,3,1024]{2,0,1:T(8,128)(2,1)} %copy-done) | copy-start | bytes 2359300
  276.5 23.7 %all-to-all-start.5 = ((bf16[32,128,32]{1,2,0:T(8,128)(2,1)}), bf16[32,128,32]{1,2,0:T(8,128)(2,1)S(1)}, u32[]{:S(2)}, u32[]{:S(2)}) async-start(bf16[32,128,32]{1,2,0:T(8,128)(2,1)} %copy.66), calls=%async_computation.6 | async-start | bytes 524288 | tf_op jit(solution)/shard_map/all_to_all | solution.py:169
  286.3 1.4 collective-permute-start.3
  287.7 6.2 %collective-permute-start.4 = (f32[7,3,1024]{2,1,0:T(4,128)S(1)}, f32[7,3,1024]{2,1,0:T(4,128)S(1)}, u32[]{:S(2)}, u32[]{:S(2)}) collective-permute-start(f32[7,3,1024]{2,1,0:T(4,128)S(1)} %add.320), channel_id=1, source_target_pairs={{0,16},{8,24},{16,0},{24,8},{32,48},{40,56},{48,32},{56,40},{64,80... | collective-permute-start | bytes 258056 | tf_op jit(solution)/shard_map/ppermute | solution.py:126
  293.9 8.6 %collective-permute-start.5 = (f32[7,3,1024]{2,1,0:T(4,128)S(1)}, f32[7,3,1024]{2,1,0:T(4,128)S(1)}, u32[]{:S(2)}, u32[]{:S(2)}) collective-permute-start(f32[7,3,1024]{2,1,0:T(4,128)S(1)} %add.321), channel_id=1, source_target_pairs={{0,32},{8,40},{16,48},{24,56},{32,0},{40,8},{48,16},{56,24},{64,96... | collective-permute-start | bytes 258056 | tf_op jit(solution)/shard_map/ppermute | solution.py:126
  297.1 9.6 %collective-permute-start.2 = (bf16[6,3,1024]{2,0,1:T(8,128)(2,1)S(1)}, bf16[6,3,1024]{2,0,1:T(8,128)(2,1)S(1)}, u32[]{:S(2)}, u32[]{:S(2)}) collective-permute-start(bf16[6,3,1024]{2,0,1:T(8,128)(2,1)S(1)} %slice.122), channel_id=1, source_target_pairs={{8,0},{16,8},{24,16},{32,24},{40,32},{48,40},{56,48},{64,56},{72,6... | collective-permute-start | bytes 110600 | tf_op jit(solution)/shard_map/ppermute | solution.py:15
  300.3 13.8 %copy-start.9 = (f32[3,1024]{1,0:T(4,128)S(1)}, f32[3,1024]{1,0:T(4,128)}, u32[]{:S(2)}) copy-start(f32[3,1024]{1,0:T(4,128)} %copy-done.8) | copy-start | bytes 36868
  300.3 13.8 %copy-start.11 = (f32[3,1024]{1,0:T(4,128)S(1)}, f32[3,1024]{1,0:T(4,128)}, u32[]{:S(2)}) copy-start(f32[3,1024]{1,0:T(4,128)} %copy-done.10) | copy-start | bytes 36868
  300.3 13.8 %copy-start.13 = (f32[3,1024]{1,0:T(4,128)S(1)}, f32[3,1024]{1,0:T(4,128)}, u32[]{:S(2)}) copy-start(f32[3,1024]{1,0:T(4,128)} %copy-done.12) | copy-start | bytes 36868
  300.3 13.8 %copy-start.15 = (f32[3,1024]{1,0:T(4,128)S(1)}, f32[3,1024]{1,0:T(4,128)}, u32[]{:S(2)}) copy-start(f32[3,1024]{1,0:T(4,128)} %copy-done.14) | copy-start | bytes 36868
  300.3 13.8 %copy-start.17 = (f32[1,3,1024]{2,1,0:T(4,128)S(1)}, f32[1,3,1024]{2,1,0:T(4,128)}, u32[]{:S(2)}) copy-start(f32[1,3,1024]{2,1,0:T(4,128)} %copy-done.16) | copy-start | bytes 36868
  302.6 10.9 %collective-permute-start.6 = (f32[7,3,1024]{2,1,0:T(4,128)S(1)}, f32[7,3,1024]{2,1,0:T(4,128)S(1)}, u32[]{:S(2)}, u32[]{:S(2)}) collective-permute-start(f32[7,3,1024]{2,1,0:T(4,128)S(1)} %add.322), channel_id=1, source_target_pairs={{0,64},{8,72},{16,80},{24,88},{32,96},{40,104},{48,112},{56,120},{... | collective-permute-start | bytes 258056 | tf_op jit(solution)/shard_map/ppermute | solution.py:126
  313.4 6.4 %collective-permute-start.7 = (f32[7,3,1024]{2,1,0:T(4,128)S(1)}, f32[7,3,1024]{2,1,0:T(4,128)S(1)}, u32[]{:S(2)}, u32[]{:S(2)}) collective-permute-start(f32[7,3,1024]{2,1,0:T(4,128)S(1)} %add.323), channel_id=1, source_target_pairs={{0,128},{8,136},{16,144},{24,152},{32,160},{40,168},{48,176},{56,1... | collective-permute-start | bytes 258056 | tf_op jit(solution)/shard_map/ppermute | solution.py:126
  (10 other events, 58.6 us)
Sparse Core Ops, SparseCore 0:
  9.8 36.7 all-gather.2
  49.2 64.1 all-gather.4
  119.6 52.5 reduce-scatter.1

commit v4 on v3

--- a/solution.py
+++ b/solution.py
@@ -108,7 +108,10 @@
         (((1,), (1,)), ((), ())),
         preferred_element_type=jnp.float32,
     ).astype(jnp.bfloat16)
-    summed = lax.psum_scatter(partial_value, "tp", scatter_dimension=0, tiled=True)
+    tp_parts = lax.axis_size("tp")
+    chunks = partial_value.reshape((tp_parts, -1) + partial_value.shape[1:])
+    received = lax.all_to_all(chunks, "tp", split_axis=0, concat_axis=0, tiled=True)
+    summed = jnp.sum(received.astype(jnp.float32), axis=0).astype(jnp.bfloat16)
     hi_count = lax.axis_size("hi")
     tp_count = lax.axis_size("tp")
     pairs = [

time: 331 us -> 308 us (0.931)
  waiting for transfers between devices: 121 us -> 67 us
  blocking collectives: 41.1 us -> 70.5 us
    reduce_scatter x1 -> x0, waiting for transfers between devices: 52.7 us -> none  [output_grad(): lax.psum_scatter(partial_value, 'tp', scatter_dimension=0, tiled=True)]
    all_to_all x0 -> x1, blocking collectives: none -> 31.6 us  [output_grad(): lax.all_to_all(chunks, 'tp', split_axis=0, concat_axis=0, tiled=True)]
  transfers between devices with their start and end apart: 15 -> 14, of which waited for: 11 -> 10; matrix products, arithmetic and copies ran while one was open for 15% -> 16% of each run, Pallas kernels for 0% -> 0%
where the time goes in v4:
time: 308 us; the launch traced here: 305 us
  blocking collectives  70.5 us (23%)
  waiting for transfers between devices  67 us (22%)
  starting transfers between devices  57.2 us (19%)
  matrix products  50.3 us (16%)
  local copies, waits for them, and re-layouts  33.8 us (11%)
  between operations  15.1 us (5%)
  other arithmetic  11 us (4%)
    all_to_all x1, blocking collectives, output_grad(): lax.all_to_all(chunks, 'tp', split_axis=0, concat_axis=0, tiled=True)  31.6 us
    all_to_all x1, blocking collectives, body(): lax.all_to_all(conv_cols, SEQ, split_axis=0, concat_axis=1, tiled=True)  19.5 us
    all_to_all x1, blocking collectives, body(): lax.all_to_all(grad_conv, SEQ, split_axis=1, concat_axis=0, tiled=True)  19.4 us
    ppermute x1, waiting for transfers between devices, output_grad(): return lax.ppermute(summed, ('hi', 'tp'), pairs)  18.6 us
    ppermute x5, waiting for transfers between devices, butterfly_sum(): lax.ppermute(value, axis, [(i, i ^ stride) for i in range(devices)])  17.2 us
    all_gather x1, waiting for transfers between devices, output_grad(): token_rows = lax.all_gather(cotangent, 'hi', axis=0, tiled=True)  13.9 us
    all_to_all x1, starting transfers between devices, body(): lax.all_to_all(long_filter.astype(jnp.bfloat16), SEQ, split_axis=1, conca...  11.6 us
    all_to_all x1, starting transfers between devices, body(): lax.all_to_all(gated_input, SEQ, split_axis=1, concat_axis=0, tiled=True)  10.1 us
  transfers between devices with their start and end apart: 14, of which 10 were waited for; matrix products, arithmetic and copies ran while one was open for 16% of the time, Pallas kernels for 0%

profile of v4, /device:TPU:6, one launch (start us, length us, event | category | flops | bytes accessed | tf_op | source)
XLA Modules:
  0.0 304.8 jit_solution(10279254072747264994)
XLA Ops:
  9.8 11.6 %all-to-all-start.1 = ((bf16[128,32,32]{0,2,1:T(8,128)(2,1)}), bf16[128,32,32]{0,2,1:T(8,128)(2,1)S(1)}, u32[]{:S(2)}, u32[]{:S(2)}) async-start(bf16[128,32,32]{0,2,1:T(8,128)(2,1)} %bitcast.8), calls=%async_computation.1 | async-start | bytes 524288 | tf_op jit(solution)/shard_map/all_to_all | solution.py:152
  23.9 7.1 %collective-permute-done = bf16[6,3,1024]{2,0,1:T(8,128)(2,1)S(1)} collective-permute-done((bf16[6,3,1024]{2,0,1:T(8,128)(2,1)S(1)}, bf16[6,3,1024]{2,0,1:T(8,128)(2,1)S(1)}, u32[]{:S(2)}, u32[]{:S(2)}) %collective-permute-start) | collective-permute-done | bytes 36896 | tf_op jit(solution)/shard_map/ppermute | solution.py:15
  34.3 10.1 %all-to-all-start = ((bf16[128,32,32]{0,2,1:T(8,128)(2,1)}), bf16[128,32,32]{0,2,1:T(8,128)(2,1)S(1)}, u32[]{:S(2)}, u32[]{:S(2)}) async-start(bf16[128,32,32]{0,2,1:T(8,128)(2,1)} %bitcast.2), calls=%async_computation | async-start | bytes 524288 | tf_op jit(solution)/shard_map/all_to_all | solution.py:156
  52.5 3.7 %all-to-all-done = bf16[128,32,32]{0,2,1:T(8,128)(2,1)S(1)} async-done(((bf16[128,32,32]{0,2,1:T(8,128)(2,1)}), bf16[128,32,32]{0,2,1:T(8,128)(2,1)S(1)}, u32[]{:S(2)}, u32[]{:S(2)}) %all-to-all-start) | async-done | bytes 262176 | tf_op jit(solution)/shard_map/all_to_all | solution.py:156
  64.9 2.5 multiply_add_fusion.6
  80.1 19.5 %all_to_all.86 = bf16[32,128,32]{1,2,0:T(8,128)(2,1)} all-to-all(bf16[32,128,32]{1,2,0:T(8,128)(2,1)S(1)} %copy.51), channel_id=1, replica_groups=mesh['hi'=8,'lo'=4,'tp'=8] {'hi','lo'}, dimensions={0} | all-to-all | bytes 524288 | tf_op jit(solution)/shard_map/all_to_all | solution.py:161
  99.6 13.9 %all-gather.5.cloned.1.call-done = bf16[1024,1024]{1,0:T(8,128)(2,1)} async-done(((bf16[128,1024]{1,0:T(8,128)(2,1)}), bf16[1024,1024]{1,0:T(8,128)(2,1)}) %all-gather.5.cloned.1.call-update) | async-done | bytes 2097168 | tf_op jit(solution)/shard_map/all_gather | solution.py:103
  113.5 4.6 %convolution_convert_fusion = bf16[1024,1024]{1,0:T(8,128)(2,1)S(1)} fusion(bf16[1024,1024]{1,0:T(8,128)(2,1)} %all-gather.5.cloned.1.call-done, bf16[1024,1024]{1,0:T(8,128)(2,1)} %all-gather.3.cloned.1.call-done), kind=kOutput, calls=%fused_computation.29 | convolution fusion | flops 2148532224 | bytes 6291456 | tf_op jit(solution)/shard_map/dot_general | solution.py:105
  118.1 31.6 %all_to_all.87 = bf16[8,128,1024]{2,1,0:T(8,128)(2,1)} all-to-all(bf16[8,128,1024]{2,1,0:T(8,128)(2,1)S(1)} %bitcast.202), channel_id=1, replica_groups=mesh['hi'=8,'lo'=4,'tp'=8] {'tp'}, dimensions={0} | all-to-all | bytes 4194304 | tf_op jit(solution)/shard_map/all_to_all | solution.py:113
  149.8 2.8 reduce_sum.75
  152.5 6.9 %collective-permute-start.1 = (bf16[128,1024]{1,0:T(8,128)(2,1)}, bf16[128,1024]{1,0:T(8,128)(2,1)}, u32[]{:S(2)}, u32[]{:S(2)}) collective-permute-start(bf16[128,1024]{1,0:T(8,128)(2,1)} %reduce_sum.75), channel_id=1, source_target_pairs={{0,0},{1,32},{2,64},{3,96},{4,128},{5,160},{6,192},{7,224},{32,1},... | collective-permute-start | bytes 786440 | tf_op jit(solution)/shard_map/ppermute | solution.py:122
  160.3 18.6 %collective-permute-done.1 = bf16[128,1024]{1,0:T(8,128)(2,1)} collective-permute-done((bf16[128,1024]{1,0:T(8,128)(2,1)}, bf16[128,1024]{1,0:T(8,128)(2,1)}, u32[]{:S(2)}, u32[]{:S(2)}) %collective-permute-start.1) | collective-permute-done | bytes 262176 | tf_op jit(solution)/shard_map/ppermute | solution.py:122
  182.7 19.4 %all_to_all.88 = bf16[128,32,32]{0,2,1:T(8,128)(2,1)} all-to-all(bf16[128,32,32]{0,2,1:T(8,128)(2,1)} %bitcast.212), channel_id=1, replica_groups=mesh['hi'=8,'lo'=4,'tp'=8] {'hi','lo'}, dimensions={1} | all-to-all | bytes 524288 | tf_op jit(solution)/shard_map/all_to_all | solution.py:165
  204.3 3.0 reshape.148
  235.0 7.0 %all-to-all-start.5 = ((bf16[32,128,32]{1,2,0:T(8,128)(2,1)}), bf16[32,128,32]{1,2,0:T(8,128)(2,1)S(1)}, u32[]{:S(2)}, u32[]{:S(2)}) async-start(bf16[32,128,32]{1,2,0:T(8,128)(2,1)} %copy.60), calls=%async_computation.5 | async-start | bytes 524288 | tf_op jit(solution)/shard_map/all_to_all | solution.py:171
  247.9 5.8 %all-to-all-done.5 = bf16[32,128,32]{1,2,0:T(8,128)(2,1)S(1)} async-done(((bf16[32,128,32]{1,2,0:T(8,128)(2,1)}), bf16[32,128,32]{1,2,0:T(8,128)(2,1)S(1)}, u32[]{:S(2)}, u32[]{:S(2)}) %all-to-all-start.5) | async-done | bytes 262176 | tf_op jit(solution)/shard_map/all_to_all | solution.py:171
  253.6 6.8 %all-to-all-start.6 = ((bf16[32,128,32]{1,2,0:T(8,128)(2,1)}), bf16[32,128,32]{1,2,0:T(8,128)(2,1)S(1)}, u32[]{:S(2)}, u32[]{:S(2)}) async-start(bf16[32,128,32]{1,2,0:T(8,128)(2,1)} %copy.65), calls=%async_computation.6 | async-start | bytes 524288 | tf_op jit(solution)/shard_map/all_to_all | solution.py:172
  266.5 4.6 %collective-permute-done.4 = f32[7,3,1024]{2,1,0:T(4,128)S(1)} collective-permute-done((f32[7,3,1024]{2,1,0:T(4,128)S(1)}, f32[7,3,1024]{2,1,0:T(4,128)S(1)}, u32[]{:S(2)}, u32[]{:S(2)}) %collective-permute-start.4) | collective-permute-done | bytes 86048 | tf_op jit(solution)/shard_map/ppermute | solution.py:129
  271.1 3.0 collective-permute-start.5
  274.3 3.1 %collective-permute-start.2 = (bf16[6,3,1024]{2,0,1:T(8,128)(2,1)S(1)}, bf16[6,3,1024]{2,0,1:T(8,128)(2,1)S(1)}, u32[]{:S(2)}, u32[]{:S(2)}) collective-permute-start(bf16[6,3,1024]{2,0,1:T(8,128)(2,1)S(1)} %slice.122), channel_id=1, source_target_pairs={{8,0},{16,8},{24,16},{32,24},{40,32},{48,40},{56,48},{64,56},{72,6... | collective-permute-start | bytes 110600 | tf_op jit(solution)/shard_map/ppermute | solution.py:15
  279.7 4.1 %collective-permute-start.6 = (f32[7,3,1024]{2,1,0:T(4,128)S(1)}, f32[7,3,1024]{2,1,0:T(4,128)S(1)}, u32[]{:S(2)}, u32[]{:S(2)}) collective-permute-start(f32[7,3,1024]{2,1,0:T(4,128)S(1)} %add.320), channel_id=1, source_target_pairs={{0,64},{8,72},{16,80},{24,88},{32,96},{40,104},{48,112},{56,120},{... | collective-permute-start | bytes 258056 | tf_op jit(solution)/shard_map/ppermute | solution.py:129
  283.9 6.7 %collective-permute-done.6 = f32[7,3,1024]{2,1,0:T(4,128)S(1)} collective-permute-done((f32[7,3,1024]{2,1,0:T(4,128)S(1)}, f32[7,3,1024]{2,1,0:T(4,128)S(1)}, u32[]{:S(2)}, u32[]{:S(2)}) %collective-permute-start.6) | collective-permute-done | bytes 86048 | tf_op jit(solution)/shard_map/ppermute | solution.py:129
  291.3 2.3 fusion.19
  293.6 3.4 %collective-permute-done.7 = f32[7,3,1024]{2,1,0:T(4,128)S(1)} collective-permute-done((f32[7,3,1024]{2,1,0:T(4,128)S(1)}, f32[7,3,1024]{2,1,0:T(4,128)S(1)}, u32[]{:S(2)}, u32[]{:S(2)}) %collective-permute-start.7) | collective-permute-done | bytes 86048 | tf_op jit(solution)/shard_map/ppermute | solution.py:129
  (143 shorter events, 87.6 us)
Async XLA Ops:
  7.2 14.3 %copy-start.4 = (bf16[128,3,1024]{2,0,1:T(8,128)(2,1)S(1)}, bf16[128,3,1024]{2,0,1:T(8,128)(2,1)}, u32[]{:S(2)}) copy-start(bf16[128,3,1024]{2,0,1:T(8,128)(2,1)} %param.5) | copy-start | bytes 2359300
  7.2 16.4 %copy-start.18 = (f32[7,3,1024]{2,0,1:T(8,128)S(1)}, f32[7,3,1024]{2,0,1:T(8,128)}, u32[]{:S(2)}) copy-start(f32[7,3,1024]{2,0,1:T(8,128)} %param.8) | copy-start | bytes 258052
  7.2 92.4 %all-gather.3.cloned.1.call-start = ((), (), s32[]{:S(2)}) async-start(), calls=%async_computation.7 | async-start | bytes 2621440 | tf_op jit(solution)/shard_map/all_gather | solution.py:102
  9.8 24.5 %all-to-all-start.1 = ((bf16[128,32,32]{0,2,1:T(8,128)(2,1)}), bf16[128,32,32]{0,2,1:T(8,128)(2,1)S(1)}, u32[]{:S(2)}, u32[]{:S(2)}) async-start(bf16[128,32,32]{0,2,1:T(8,128)(2,1)} %bitcast.8), calls=%async_computation.1 | async-start | bytes 524288 | tf_op jit(solution)/shard_map/all_to_all | solution.py:152
  21.4 92.1 %all-gather.5.cloned.1.call-start = ((), (), s32[]{:S(2)}) async-start(), calls=%async_computation.8 | async-start | bytes 2359296 | tf_op jit(solution)/shard_map/all_gather | solution.py:103
  21.5 9.5 %collective-permute-start = (bf16[6,3,1024]{2,0,1:T(8,128)(2,1)S(1)}, bf16[6,3,1024]{2,0,1:T(8,128)(2,1)S(1)}, u32[]{:S(2)}, u32[]{:S(2)}) collective-permute-start(bf16[6,3,1024]{2,0,1:T(8,128)(2,1)S(1)} %slice.87), channel_id=1, source_target_pairs={{0,8},{8,16},{16,24},{24,32},{32,40},{40,48},{48,56},{56,64},{64,7... | collective-permute-start | bytes 110600 | tf_op jit(solution)/shard_map/ppermute | solution.py:15
  23.7 10.6 %copy-start.8 = (f32[3,1024]{1,0:T(4,128)}, f32[3,1024]{1,0:T(4,128)S(1)}, u32[]{:S(2)}) copy-start(f32[3,1024]{1,0:T(4,128)S(1)} %get-tuple-element.56) | copy-start | bytes 36868
  23.7 10.6 %copy-start.10 = (f32[3,1024]{1,0:T(4,128)}, f32[3,1024]{1,0:T(4,128)S(1)}, u32[]{:S(2)}) copy-start(f32[3,1024]{1,0:T(4,128)S(1)} %get-tuple-element.57) | copy-start | bytes 36868
  34.3 21.9 %all-to-all-start = ((bf16[128,32,32]{0,2,1:T(8,128)(2,1)}), bf16[128,32,32]{0,2,1:T(8,128)(2,1)S(1)}, u32[]{:S(2)}, u32[]{:S(2)}) async-start(bf16[128,32,32]{0,2,1:T(8,128)(2,1)} %bitcast.2), calls=%async_computation | async-start | bytes 524288 | tf_op jit(solution)/shard_map/all_to_all | solution.py:156
  152.5 26.4 %collective-permute-start.1 = (bf16[128,1024]{1,0:T(8,128)(2,1)}, bf16[128,1024]{1,0:T(8,128)(2,1)}, u32[]{:S(2)}, u32[]{:S(2)}) collective-permute-start(bf16[128,1024]{1,0:T(8,128)(2,1)} %reduce_sum.75), channel_id=1, source_target_pairs={{0,0},{1,32},{2,64},{3,96},{4,128},{5,160},{6,192},{7,224},{32,1},... | collective-permute-start | bytes 786440 | tf_op jit(solution)/shard_map/ppermute | solution.py:122
  235.0 18.6 %all-to-all-start.5 = ((bf16[32,128,32]{1,2,0:T(8,128)(2,1)}), bf16[32,128,32]{1,2,0:T(8,128)(2,1)S(1)}, u32[]{:S(2)}, u32[]{:S(2)}) async-start(bf16[32,128,32]{1,2,0:T(8,128)(2,1)} %copy.60), calls=%async_computation.5 | async-start | bytes 524288 | tf_op jit(solution)/shard_map/all_to_all | solution.py:171
  246.8 13.9 %copy-start.1 = (bf16[128,3,1024]{2,0,1:T(8,128)(2,1)S(1)}, bf16[128,3,1024]{2,0,1:T(8,128)(2,1)}, u32[]{:S(2)}) copy-start(bf16[128,3,1024]{2,0,1:T(8,128)(2,1)} %copy-done) | copy-start | bytes 2359300
  253.6 23.7 %all-to-all-start.6 = ((bf16[32,128,32]{1,2,0:T(8,128)(2,1)}), bf16[32,128,32]{1,2,0:T(8,128)(2,1)S(1)}, u32[]{:S(2)}, u32[]{:S(2)}) async-start(bf16[32,128,32]{1,2,0:T(8,128)(2,1)} %copy.65), calls=%async_computation.6 | async-start | bytes 524288 | tf_op jit(solution)/shard_map/all_to_all | solution.py:172
  263.5 1.4 collective-permute-start.3
  264.9 6.2 %collective-permute-start.4 = (f32[7,3,1024]{2,1,0:T(4,128)S(1)}, f32[7,3,1024]{2,1,0:T(4,128)S(1)}, u32[]{:S(2)}, u32[]{:S(2)}) collective-permute-start(f32[7,3,1024]{2,1,0:T(4,128)S(1)} %add.318), channel_id=1, source_target_pairs={{0,16},{8,24},{16,0},{24,8},{32,48},{40,56},{48,32},{56,40},{64,80... | collective-permute-start | bytes 258056 | tf_op jit(solution)/shard_map/ppermute | solution.py:129
  271.1 8.6 %collective-permute-start.5 = (f32[7,3,1024]{2,1,0:T(4,128)S(1)}, f32[7,3,1024]{2,1,0:T(4,128)S(1)}, u32[]{:S(2)}, u32[]{:S(2)}) collective-permute-start(f32[7,3,1024]{2,1,0:T(4,128)S(1)} %add.319), channel_id=1, source_target_pairs={{0,32},{8,40},{16,48},{24,56},{32,0},{40,8},{48,16},{56,24},{64,96... | collective-permute-start | bytes 258056 | tf_op jit(solution)/shard_map/ppermute | solution.py:129
  274.3 9.6 %collective-permute-start.2 = (bf16[6,3,1024]{2,0,1:T(8,128)(2,1)S(1)}, bf16[6,3,1024]{2,0,1:T(8,128)(2,1)S(1)}, u32[]{:S(2)}, u32[]{:S(2)}) collective-permute-start(bf16[6,3,1024]{2,0,1:T(8,128)(2,1)S(1)} %slice.122), channel_id=1, source_target_pairs={{8,0},{16,8},{24,16},{32,24},{40,32},{48,40},{56,48},{64,56},{72,6... | collective-permute-start | bytes 110600 | tf_op jit(solution)/shard_map/ppermute | solution.py:15
  277.4 13.8 %copy-start.9 = (f32[3,1024]{1,0:T(4,128)S(1)}, f32[3,1024]{1,0:T(4,128)}, u32[]{:S(2)}) copy-start(f32[3,1024]{1,0:T(4,128)} %copy-done.8) | copy-start | bytes 36868
  277.4 13.8 %copy-start.11 = (f32[3,1024]{1,0:T(4,128)S(1)}, f32[3,1024]{1,0:T(4,128)}, u32[]{:S(2)}) copy-start(f32[3,1024]{1,0:T(4,128)} %copy-done.10) | copy-start | bytes 36868
  277.5 13.8 %copy-start.13 = (f32[3,1024]{1,0:T(4,128)S(1)}, f32[3,1024]{1,0:T(4,128)}, u32[]{:S(2)}) copy-start(f32[3,1024]{1,0:T(4,128)} %copy-done.12) | copy-start | bytes 36868
  277.5 13.8 %copy-start.15 = (f32[3,1024]{1,0:T(4,128)S(1)}, f32[3,1024]{1,0:T(4,128)}, u32[]{:S(2)}) copy-start(f32[3,1024]{1,0:T(4,128)} %copy-done.14) | copy-start | bytes 36868
  277.5 13.8 %copy-start.17 = (f32[1,3,1024]{2,1,0:T(4,128)S(1)}, f32[1,3,1024]{2,1,0:T(4,128)}, u32[]{:S(2)}) copy-start(f32[1,3,1024]{2,1,0:T(4,128)} %copy-done.16) | copy-start | bytes 36868
  279.7 10.9 %collective-permute-start.6 = (f32[7,3,1024]{2,1,0:T(4,128)S(1)}, f32[7,3,1024]{2,1,0:T(4,128)S(1)}, u32[]{:S(2)}, u32[]{:S(2)}) collective-permute-start(f32[7,3,1024]{2,1,0:T(4,128)S(1)} %add.320), channel_id=1, source_target_pairs={{0,64},{8,72},{16,80},{24,88},{32,96},{40,104},{48,112},{56,120},{... | collective-permute-start | bytes 258056 | tf_op jit(solution)/shard_map/ppermute | solution.py:129
  290.6 6.4 %collective-permute-start.7 = (f32[7,3,1024]{2,1,0:T(4,128)S(1)}, f32[7,3,1024]{2,1,0:T(4,128)S(1)}, u32[]{:S(2)}, u32[]{:S(2)}) collective-permute-start(f32[7,3,1024]{2,1,0:T(4,128)S(1)} %add.321), channel_id=1, source_target_pairs={{0,128},{8,136},{16,144},{24,152},{32,160},{40,168},{48,176},{56,1... | collective-permute-start | bytes 258056 | tf_op jit(solution)/shard_map/ppermute | solution.py:129
  (9 other events, 47.1 us)
Sparse Core Ops, SparseCore 0:
  9.8 36.7 all-gather.2
  49.3 64.2 all-gather.4

commit v5 on v3

--- a/solution.py
+++ b/solution.py
@@ -98,17 +98,7 @@
     return (left_array.astype(jnp.float32) * right_array.astype(jnp.float32)).astype(jnp.bfloat16)
 
 
-def output_grad(cotangent, out_weight, ready):
-    weight_rows = lax.all_gather(out_weight, "lo", axis=0, tiled=True)
-    token_rows = lax.all_gather(cotangent, "hi", axis=0, tiled=True)
-    weight_rows, token_rows, _ = lax.optimization_barrier((weight_rows, token_rows, ready))
-    partial_value = lax.dot_general(
-        token_rows,
-        weight_rows,
-        (((1,), (1,)), ((), ())),
-        preferred_element_type=jnp.float32,
-    ).astype(jnp.bfloat16)
-    summed = lax.psum_scatter(partial_value, "tp", scatter_dimension=0, tiled=True)
+def transposed(value):
     hi_count = lax.axis_size("hi")
     tp_count = lax.axis_size("tp")
     pairs = [
@@ -116,7 +106,23 @@
         for row in range(hi_count)
         for col in range(tp_count)
     ]
-    return lax.ppermute(summed, ("hi", "tp"), pairs)
+    return lax.ppermute(value, ("hi", "tp"), pairs)
+
+
+def output_grad(cotangent, out_weight, ready):
+    weight_rows = lax.all_gather(transposed(out_weight), "lo", axis=0, tiled=True)
+    token_rows = lax.all_gather(transposed(cotangent), "tp", axis=0, tiled=True)
+    weight_rows, token_rows, ready = lax.optimization_barrier((weight_rows, token_rows, ready))
+    partial_value = lax.dot_general(
+        token_rows,
+        weight_rows,
+        (((1,), (1,)), ((), ())),
+        preferred_element_type=jnp.float32,
+    ).astype(jnp.bfloat16)
+    hi_parts = lax.axis_size("hi")
+    chunks = partial_value.reshape((hi_parts, -1) + partial_value.shape[1:])
+    received = lax.all_to_all(chunks, "hi", split_axis=0, concat_axis=0, tiled=True)
+    return jnp.sum(received.astype(jnp.float32), axis=0).astype(jnp.bfloat16), ready
 
 
 def butterfly_sum(value, axis):
@@ -156,7 +162,7 @@
         jnp.bfloat16
     )
     conv_out = lax.all_to_all(conv_cols, SEQ, split_axis=0, concat_axis=1, tiled=True)
-    grad_out = output_grad(cotangent, out_weight, conv_out)
+    grad_out, conv_out = output_grad(cotangent, out_weight, conv_out)
     grad_query = times_bf16(grad_out, conv_out)
     grad_conv = times_bf16(grad_out, query_conv)
     grad_cols = lax.all_to_all(grad_conv, SEQ, split_axis=1, concat_axis=0, tiled=True)

time: 331 us -> 360 us (1.088)
  blocking collectives: 41.1 us -> 18.2 us
  starting transfers between devices: 56.8 us -> 78.1 us
  waiting for transfers between devices: 121 us -> 140 us
  other arithmetic: 8.26 us -> 14.2 us
  local copies, waits for them, and re-layouts: 33.5 us -> 37.7 us
    all_to_all x0 -> x2, waiting for transfers between devices: none -> 54.9 us  [the longest x1 46.1 us: output_grad(): lax.all_to_all(chunks, 'hi', split_axis=0, concat_axis=0, tiled=True)]
    reduce_scatter x1 -> x0, waiting for transfers between devices: 52.7 us -> none  [output_grad(): lax.psum_scatter(partial_value, 'tp', scatter_dimension=0, tiled=True)]
    ppermute x1 -> x2, waiting for transfers between devices: 19.9 us -> 56.5 us  [transposed(): return lax.ppermute(value, ('hi', 'tp'), pairs)]
    all_to_all x1 -> x0, blocking collectives: 21.6 us -> none  [body(): lax.all_to_all(grad_conv, SEQ, split_axis=1, concat_axis=0, tiled=True)]
    all_gather x2, waiting for transfers between devices: 13.9 us -> 0.01 us  [the longest x1 0.01 us: output_grad(): lax.all_gather(transposed(out_weight), 'lo', axis=0, tiled=True)]
    all_to_all x0 -> x2, starting transfers between devices: none -> 13.6 us  [the longest x1 7.42 us: output_grad(): lax.all_to_all(chunks, 'hi', split_axis=0, concat_axis=0, tiled=True)]
    ppermute x2, waiting for transfers between devices: 7.1 us -> 0.01 us  [shifted(): return lax.ppermute(value, axis, pairs)]
    ppermute x1 -> x2, starting transfers between devices: 6.56 us -> 11.7 us  [transposed(): return lax.ppermute(value, ('hi', 'tp'), pairs)]
  transfers between devices with their start and end apart: 15 -> 17, of which waited for: 11 -> 11; matrix products, arithmetic and copies ran while one was open for 15% -> 15% of each run, Pallas kernels for 0% -> 0%
where the time goes in v5:
time: 360 us; the launch traced here: 355 us
  waiting for transfers between devices  140 us (39%)
  starting transfers between devices  78.1 us (22%)
  matrix products  51.6 us (14%)
  local copies, waits for them, and re-layouts  37.7 us (10%)
  blocking collectives  18.2 us (5%)
  between operations  15.1 us (4%)
  other arithmetic  14.2 us (4%)
    ppermute x2, waiting for transfers between devices, transposed(): return lax.ppermute(value, ('hi', 'tp'), pairs)  56.5 us
    all_to_all x1, waiting for transfers between devices, output_grad(): lax.all_to_all(chunks, 'hi', split_axis=0, concat_axis=0, tiled=True)  46.1 us
    all_to_all x1, blocking collectives, body(): lax.all_to_all(conv_cols, SEQ, split_axis=0, concat_axis=1, tiled=True)  18.2 us
    ppermute x5, waiting for transfers between devices, butterfly_sum(): lax.ppermute(value, axis, [(i, i ^ stride) for i in range(devices)])  18.2 us
    all_to_all x1, starting transfers between devices, body(): lax.all_to_all(gated_input, SEQ, split_axis=1, concat_axis=0, tiled=True)  12 us
    all_to_all x1, starting transfers between devices, body(): lax.all_to_all(long_filter.astype(jnp.bfloat16), SEQ, split_axis=1, conca...  11.9 us
    ppermute x2, starting transfers between devices, transposed(): return lax.ppermute(value, ('hi', 'tp'), pairs)  11.7 us
    ppermute x5, starting transfers between devices, butterfly_sum(): lax.ppermute(value, axis, [(i, i ^ stride) for i in range(devices)])  9.35 us
  transfers between devices with their start and end apart: 17, of which 11 were waited for; matrix products, arithmetic and copies ran while one was open for 15% of the time, Pallas kernels for 0%

profile of v5, /device:TPU:6, one launch (start us, length us, event | category | flops | bytes accessed | tf_op | source)
XLA Modules:
  0.0 354.8 jit_solution(8697436942345094921)
XLA Ops:
  7.2 7.9 %collective-permute-start = (bf16[256,1024]{1,0:T(8,128)(2,1)}, bf16[256,1024]{1,0:T(8,128)(2,1)S(1)}, u32[]{:S(2)}, u32[]{:S(2)}) collective-permute-start(bf16[256,1024]{1,0:T(8,128)(2,1)} %param.7), channel_id=1, source_target_pairs={{0,0},{1,32},{2,64},{3,96},{4,128},{5,160},{6,192},{7,224},{32,1},... | collective-permute-start | bytes 1572872 | tf_op jit(solution)/shard_map/ppermute | solution.py:109
  15.1 37.4 %collective-permute-done = bf16[256,1024]{1,0:T(8,128)(2,1)S(1)} collective-permute-done((bf16[256,1024]{1,0:T(8,128)(2,1)}, bf16[256,1024]{1,0:T(8,128)(2,1)S(1)}, u32[]{:S(2)}, u32[]{:S(2)}) %collective-permute-start) | collective-permute-done | bytes 524320 | tf_op jit(solution)/shard_map/ppermute | solution.py:109
  58.0 11.9 %all-to-all-start.1 = ((bf16[128,32,32]{0,2,1:T(8,128)(2,1)}), bf16[128,32,32]{0,2,1:T(8,128)(2,1)S(1)}, u32[]{:S(2)}, u32[]{:S(2)}) async-start(bf16[128,32,32]{0,2,1:T(8,128)(2,1)} %bitcast.8), calls=%async_computation.1 | async-start | bytes 524288 | tf_op jit(solution)/shard_map/all_to_all | solution.py:155
  70.0 3.8 %collective-permute-start.1 = (bf16[128,1024]{1,0:T(8,128)(2,1)S(1)}, bf16[128,1024]{1,0:T(8,128)(2,1)S(1)}, u32[]{:S(2)}, u32[]{:S(2)}) collective-permute-start(bf16[128,1024]{1,0:T(8,128)(2,1)S(1)} %copy-done.21), channel_id=1, source_target_pairs={{0,0},{1,32},{2,64},{3,96},{4,128},{5,160},{6,192},{7,224},{32,1},... | collective-permute-start | bytes 786440 | tf_op jit(solution)/shard_map/ppermute | solution.py:109
  77.5 19.1 %collective-permute-done.1 = bf16[128,1024]{1,0:T(8,128)(2,1)S(1)} collective-permute-done((bf16[128,1024]{1,0:T(8,128)(2,1)S(1)}, bf16[128,1024]{1,0:T(8,128)(2,1)S(1)}, u32[]{:S(2)}, u32[]{:S(2)}) %collective-permute-start.1) | collective-permute-done | bytes 262176 | tf_op jit(solution)/shard_map/ppermute | solution.py:109
  97.4 12.0 %all-to-all-start = ((bf16[128,32,32]{0,2,1:T(8,128)(2,1)}), bf16[128,32,32]{0,2,1:T(8,128)(2,1)S(1)}, u32[]{:S(2)}, u32[]{:S(2)}) async-start(bf16[128,32,32]{0,2,1:T(8,128)(2,1)} %bitcast.2), calls=%async_computation | async-start | bytes 524288 | tf_op jit(solution)/shard_map/all_to_all | solution.py:159
  117.4 3.3 all-to-all-done
  129.5 2.5 multiply_add_fusion.6
  144.7 18.2 %all_to_all.83 = bf16[32,128,32]{1,2,0:T(8,128)(2,1)} all-to-all(bf16[32,128,32]{1,2,0:T(8,128)(2,1)S(1)} %copy.51), channel_id=1, replica_groups=mesh['hi'=8,'lo'=4,'tp'=8] {'hi','lo'}, dimensions={0} | all-to-all | bytes 524288 | tf_op jit(solution)/shard_map/all_to_all | solution.py:164
  162.9 6.0 %convolution_convert_fusion = bf16[1024,1024]{1,0:T(8,128)(2,1)} fusion(bf16[1024,1024]{1,0:T(8,128)(2,1)} %all-gather.5.cloned.1.call-done, bf16[1024,1024]{1,0:T(8,128)(2,1)} %all-gather.3.cloned.1.call-done), kind=kOutput, calls=%fused_computation.29 | convolution fusion | flops 2148532224 | bytes 6291456 | tf_op jit(solution)/shard_map/dot_general | solution.py:116
  168.9 7.4 %all-to-all-start.3 = ((bf16[8,128,1024]{2,1,0:T(8,128)(2,1)}), bf16[8,128,1024]{2,1,0:T(8,128)(2,1)}, u32[]{:S(2)}, u32[]{:S(2)}) async-start(bf16[8,128,1024]{2,1,0:T(8,128)(2,1)} %bitcast.198), calls=%async_computation.3 | async-start | bytes 4194304 | tf_op jit(solution)/shard_map/all_to_all | solution.py:124
  180.2 46.1 %all-to-all-done.3 = bf16[8,128,1024]{2,1,0:T(8,128)(2,1)} async-done(((bf16[8,128,1024]{2,1,0:T(8,128)(2,1)}), bf16[8,128,1024]{2,1,0:T(8,128)(2,1)}, u32[]{:S(2)}, u32[]{:S(2)}) %all-to-all-start.3) | async-done | bytes 2097184 | tf_op jit(solution)/shard_map/all_to_all | solution.py:124
  231.1 6.2 %all-to-all-start.4 = ((bf16[128,32,32]{0,2,1:T(8,128)(2,1)}), bf16[128,32,32]{0,2,1:T(8,128)(2,1)}, u32[]{:S(2)}, u32[]{:S(2)}) async-start(bf16[128,32,32]{0,2,1:T(8,128)(2,1)} %multiply_convert_fusion), calls=%async_computation.4 | async-start | bytes 524288 | tf_op jit(solution)/shard_map/all_to_all | solution.py:168
  240.3 8.9 %all-to-all-done.4 = bf16[128,32,32]{0,2,1:T(8,128)(2,1)} async-done(((bf16[128,32,32]{0,2,1:T(8,128)(2,1)}), bf16[128,32,32]{0,2,1:T(8,128)(2,1)}, u32[]{:S(2)}, u32[]{:S(2)}) %all-to-all-start.4) | async-done | bytes 262176 | tf_op jit(solution)/shard_map/all_to_all | solution.py:168
  251.4 3.0 reshape.152
  283.3 7.9 %all-to-all-start.5 = ((bf16[32,128,32]{1,2,0:T(8,128)(2,1)}), bf16[32,128,32]{1,2,0:T(8,128)(2,1)}, u32[]{:S(2)}, u32[]{:S(2)}) async-start(bf16[32,128,32]{1,2,0:T(8,128)(2,1)} %copy.61), calls=%async_computation.5 | async-start | bytes 524288 | tf_op jit(solution)/shard_map/all_to_all | solution.py:174
  295.7 7.0 %all-to-all-done.5 = bf16[32,128,32]{1,2,0:T(8,128)(2,1)} async-done(((bf16[32,128,32]{1,2,0:T(8,128)(2,1)}), bf16[32,128,32]{1,2,0:T(8,128)(2,1)}, u32[]{:S(2)}, u32[]{:S(2)}) %all-to-all-start.5) | async-done | bytes 262176 | tf_op jit(solution)/shard_map/all_to_all | solution.py:174
  302.7 6.8 %all-to-all-start.6 = ((bf16[32,128,32]{1,2,0:T(8,128)(2,1)}), bf16[32,128,32]{1,2,0:T(8,128)(2,1)S(1)}, u32[]{:S(2)}, u32[]{:S(2)}) async-start(bf16[32,128,32]{1,2,0:T(8,128)(2,1)} %copy.66), calls=%async_computation.6 | async-start | bytes 524288 | tf_op jit(solution)/shard_map/all_to_all | solution.py:175
  315.9 4.3 %collective-permute-done.5 = f32[7,3,1024]{2,1,0:T(4,128)S(1)} collective-permute-done((f32[7,3,1024]{2,1,0:T(4,128)S(1)}, f32[7,3,1024]{2,1,0:T(4,128)S(1)}, u32[]{:S(2)}, u32[]{:S(2)}) %collective-permute-start.5) | collective-permute-done | bytes 86048 | tf_op jit(solution)/shard_map/ppermute | solution.py:132
  320.2 3.3 collective-permute-start.6
  323.6 2.8 collective-permute-start.3
  329.1 3.9 %collective-permute-start.7 = (f32[7,3,1024]{2,1,0:T(4,128)S(1)}, f32[7,3,1024]{2,1,0:T(4,128)S(1)}, u32[]{:S(2)}, u32[]{:S(2)}) collective-permute-start(f32[7,3,1024]{2,1,0:T(4,128)S(1)} %add.320), channel_id=1, source_target_pairs={{0,64},{8,72},{16,80},{24,88},{32,96},{40,104},{48,112},{56,120},{... | collective-permute-start | bytes 258056 | tf_op jit(solution)/shard_map/ppermute | solution.py:132
  333.1 7.3 %collective-permute-done.7 = f32[7,3,1024]{2,1,0:T(4,128)S(1)} collective-permute-done((f32[7,3,1024]{2,1,0:T(4,128)S(1)}, f32[7,3,1024]{2,1,0:T(4,128)S(1)}, u32[]{:S(2)}, u32[]{:S(2)}) %collective-permute-start.7) | collective-permute-done | bytes 86048 | tf_op jit(solution)/shard_map/ppermute | solution.py:132
  343.1 3.9 %collective-permute-done.8 = f32[7,3,1024]{2,1,0:T(4,128)S(1)} collective-permute-done((f32[7,3,1024]{2,1,0:T(4,128)S(1)}, f32[7,3,1024]{2,1,0:T(4,128)S(1)}, u32[]{:S(2)}, u32[]{:S(2)}) %collective-permute-start.8) | collective-permute-done | bytes 86048 | tf_op jit(solution)/shard_map/ppermute | solution.py:132
  (156 shorter events, 99.1 us)
Async XLA Ops:
  7.2 67.0 %copy-start.4 = (bf16[128,3,1024]{2,0,1:T(8,128)(2,1)S(1)}, bf16[128,3,1024]{2,0,1:T(8,128)(2,1)}, u32[]{:S(2)}) copy-start(bf16[128,3,1024]{2,0,1:T(8,128)(2,1)} %param.5) | copy-start | bytes 2359300
  7.2 62.8 %copy-start.21 = (bf16[128,1024]{1,0:T(8,128)(2,1)S(1)}, bf16[128,1024]{1,0:T(8,128)(2,1)}, u32[]{:S(2)}) copy-start(bf16[128,1024]{1,0:T(8,128)(2,1)} %param.6) | copy-start | bytes 786436
  7.2 66.6 %copy-start.20 = (f32[7,3,1024]{2,0,1:T(8,128)S(1)}, f32[7,3,1024]{2,0,1:T(8,128)}, u32[]{:S(2)}) copy-start(f32[7,3,1024]{2,0,1:T(8,128)} %param.8) | copy-start | bytes 258052
  7.2 155.7 %all-gather.3.cloned.1.call-start = ((), (), s32[]{:S(2)}) async-start(), calls=%async_computation.7 | async-start | bytes 2621440 | tf_op jit(solution)/shard_map/all_gather | solution.py:113
  7.2 45.3 %collective-permute-start = (bf16[256,1024]{1,0:T(8,128)(2,1)}, bf16[256,1024]{1,0:T(8,128)(2,1)S(1)}, u32[]{:S(2)}, u32[]{:S(2)}) collective-permute-start(bf16[256,1024]{1,0:T(8,128)(2,1)} %param.7), channel_id=1, source_target_pairs={{0,0},{1,32},{2,64},{3,96},{4,128},{5,160},{6,192},{7,224},{32,1},... | collective-permute-start | bytes 1572872 | tf_op jit(solution)/shard_map/ppermute | solution.py:109
  54.2 20.0 %collective-permute-start.2 = (bf16[6,3,1024]{2,0,1:T(8,128)(2,1)S(1)}, bf16[6,3,1024]{2,0,1:T(8,128)(2,1)S(1)}, u32[]{:S(2)}, u32[]{:S(2)}) collective-permute-start(bf16[6,3,1024]{2,0,1:T(8,128)(2,1)S(1)} %slice.87), channel_id=1, source_target_pairs={{0,8},{8,16},{16,24},{24,32},{32,40},{40,48},{48,56},{56,64},{64,7... | collective-permute-start | bytes 110600 | tf_op jit(solution)/shard_map/ppermute | solution.py:15
  58.0 39.4 %all-to-all-start.1 = ((bf16[128,32,32]{0,2,1:T(8,128)(2,1)}), bf16[128,32,32]{0,2,1:T(8,128)(2,1)S(1)}, u32[]{:S(2)}, u32[]{:S(2)}) async-start(bf16[128,32,32]{0,2,1:T(8,128)(2,1)} %bitcast.8), calls=%async_computation.1 | async-start | bytes 524288 | tf_op jit(solution)/shard_map/all_to_all | solution.py:155
  69.9 93.0 %all-gather.5.cloned.1.call-start = ((), (), s32[]{:S(2)}) async-start(), calls=%async_computation.8 | async-start | bytes 2359296 | tf_op jit(solution)/shard_map/all_gather | solution.py:114
  70.0 26.7 %collective-permute-start.1 = (bf16[128,1024]{1,0:T(8,128)(2,1)S(1)}, bf16[128,1024]{1,0:T(8,128)(2,1)S(1)}, u32[]{:S(2)}, u32[]{:S(2)}) collective-permute-start(bf16[128,1024]{1,0:T(8,128)(2,1)S(1)} %copy-done.21), channel_id=1, source_target_pairs={{0,0},{1,32},{2,64},{3,96},{4,128},{5,160},{6,192},{7,224},{32,1},... | collective-permute-start | bytes 786440 | tf_op jit(solution)/shard_map/ppermute | solution.py:109
  74.1 23.2 %copy-start.18 = (f32[1,3,1024]{2,1,0:T(4,128)}, f32[1,3,1024]{2,1,0:T(4,128)S(1)}, u32[]{:S(2)}) copy-start(f32[1,3,1024]{2,1,0:T(4,128)S(1)} %copy.95) | copy-start | bytes 36868
  97.4 23.4 %all-to-all-start = ((bf16[128,32,32]{0,2,1:T(8,128)(2,1)}), bf16[128,32,32]{0,2,1:T(8,128)(2,1)S(1)}, u32[]{:S(2)}, u32[]{:S(2)}) async-start(bf16[128,32,32]{0,2,1:T(8,128)(2,1)} %bitcast.2), calls=%async_computation | async-start | bytes 524288 | tf_op jit(solution)/shard_map/all_to_all | solution.py:159
  168.9 57.3 %all-to-all-start.3 = ((bf16[8,128,1024]{2,1,0:T(8,128)(2,1)}), bf16[8,128,1024]{2,1,0:T(8,128)(2,1)}, u32[]{:S(2)}, u32[]{:S(2)}) async-start(bf16[8,128,1024]{2,1,0:T(8,128)(2,1)} %bitcast.198), calls=%async_computation.3 | async-start | bytes 4194304 | tf_op jit(solution)/shard_map/all_to_all | solution.py:124
  231.1 18.0 %all-to-all-start.4 = ((bf16[128,32,32]{0,2,1:T(8,128)(2,1)}), bf16[128,32,32]{0,2,1:T(8,128)(2,1)}, u32[]{:S(2)}, u32[]{:S(2)}) async-start(bf16[128,32,32]{0,2,1:T(8,128)(2,1)} %multiply_convert_fusion), calls=%async_computation.4 | async-start | bytes 524288 | tf_op jit(solution)/shard_map/all_to_all | solution.py:168
  283.3 19.5 %all-to-all-start.5 = ((bf16[32,128,32]{1,2,0:T(8,128)(2,1)}), bf16[32,128,32]{1,2,0:T(8,128)(2,1)}, u32[]{:S(2)}, u32[]{:S(2)}) async-start(bf16[32,128,32]{1,2,0:T(8,128)(2,1)} %copy.61), calls=%async_computation.5 | async-start | bytes 524288 | tf_op jit(solution)/shard_map/all_to_all | solution.py:174
  294.7 16.2 %copy-start.1 = (bf16[128,3,1024]{2,0,1:T(8,128)(2,1)S(1)}, bf16[128,3,1024]{2,0,1:T(8,128)(2,1)}, u32[]{:S(2)}) copy-start(bf16[128,3,1024]{2,0,1:T(8,128)(2,1)} %copy-done) | copy-start | bytes 2359300
  302.7 23.7 %all-to-all-start.6 = ((bf16[32,128,32]{1,2,0:T(8,128)(2,1)}), bf16[32,128,32]{1,2,0:T(8,128)(2,1)S(1)}, u32[]{:S(2)}, u32[]{:S(2)}) async-start(bf16[32,128,32]{1,2,0:T(8,128)(2,1)} %copy.66), calls=%async_computation.6 | async-start | bytes 524288 | tf_op jit(solution)/shard_map/all_to_all | solution.py:175
  312.9 1.4 collective-permute-start.4
  314.3 5.9 %collective-permute-start.5 = (f32[7,3,1024]{2,1,0:T(4,128)S(1)}, f32[7,3,1024]{2,1,0:T(4,128)S(1)}, u32[]{:S(2)}, u32[]{:S(2)}) collective-permute-start(f32[7,3,1024]{2,1,0:T(4,128)S(1)} %add.318), channel_id=1, source_target_pairs={{0,16},{8,24},{16,0},{24,8},{32,48},{40,56},{48,32},{56,40},{64,80... | collective-permute-start | bytes 258056 | tf_op jit(solution)/shard_map/ppermute | solution.py:132
  320.2 8.9 %collective-permute-start.6 = (f32[7,3,1024]{2,1,0:T(4,128)S(1)}, f32[7,3,1024]{2,1,0:T(4,128)S(1)}, u32[]{:S(2)}, u32[]{:S(2)}) collective-permute-start(f32[7,3,1024]{2,1,0:T(4,128)S(1)} %add.319), channel_id=1, source_target_pairs={{0,32},{8,40},{16,48},{24,56},{32,0},{40,8},{48,16},{56,24},{64,96... | collective-permute-start | bytes 258056 | tf_op jit(solution)/shard_map/ppermute | solution.py:132
  323.6 9.4 %collective-permute-start.3 = (bf16[6,3,1024]{2,0,1:T(8,128)(2,1)S(1)}, bf16[6,3,1024]{2,0,1:T(8,128)(2,1)S(1)}, u32[]{:S(2)}, u32[]{:S(2)}) collective-permute-start(bf16[6,3,1024]{2,0,1:T(8,128)(2,1)S(1)} %slice.122), channel_id=1, source_target_pairs={{8,0},{16,8},{24,16},{32,24},{40,32},{48,40},{56,48},{64,56},{72,6... | collective-permute-start | bytes 110600 | tf_op jit(solution)/shard_map/ppermute | solution.py:15
  326.5 14.4 %copy-start.11 = (f32[3,1024]{1,0:T(4,128)S(1)}, f32[3,1024]{1,0:T(4,128)}, u32[]{:S(2)}) copy-start(f32[3,1024]{1,0:T(4,128)} %copy-done.10) | copy-start | bytes 36868
  326.5 14.4 %copy-start.13 = (f32[3,1024]{1,0:T(4,128)S(1)}, f32[3,1024]{1,0:T(4,128)}, u32[]{:S(2)}) copy-start(f32[3,1024]{1,0:T(4,128)} %copy-done.12) | copy-start | bytes 36868
  329.1 11.2 %collective-permute-start.7 = (f32[7,3,1024]{2,1,0:T(4,128)S(1)}, f32[7,3,1024]{2,1,0:T(4,128)S(1)}, u32[]{:S(2)}, u32[]{:S(2)}) collective-permute-start(f32[7,3,1024]{2,1,0:T(4,128)S(1)} %add.320), channel_id=1, source_target_pairs={{0,64},{8,72},{16,80},{24,88},{32,96},{40,104},{48,112},{56,120},{... | collective-permute-start | bytes 258056 | tf_op jit(solution)/shard_map/ppermute | solution.py:132
  340.4 6.6 %collective-permute-start.8 = (f32[7,3,1024]{2,1,0:T(4,128)S(1)}, f32[7,3,1024]{2,1,0:T(4,128)S(1)}, u32[]{:S(2)}, u32[]{:S(2)}) collective-permute-start(f32[7,3,1024]{2,1,0:T(4,128)S(1)} %add.321), channel_id=1, source_target_pairs={{0,128},{8,136},{16,144},{24,152},{32,160},{40,168},{48,176},{56,1... | collective-permute-start | bytes 258056 | tf_op jit(solution)/shard_map/ppermute | solution.py:132
  (15 other events, 74.1 us)
Sparse Core Ops, SparseCore 0:
  53.5 46.2 all-gather.2
  101.6 57.7 all-gather.4

commit v6 on v4

--- a/solution.py
+++ b/solution.py
@@ -5,7 +5,7 @@
 from jax import lax
 from jax.sharding import PartitionSpec as P
 
-highest = lax.Precision.HIGHEST
+highest = lax.Precision.HIGH
 SEQ = ("hi", "lo")
 
 

time: 308 us -> 300 us (0.974)
  matrix products: 50.3 us -> 35.3 us
  waiting for transfers between devices: 67 us -> 71.8 us
    all_gather x1, waiting for transfers between devices: 13.9 us -> 19.2 us  [output_grad(): token_rows = lax.all_gather(cotangent, 'hi', axis=0, tiled=True)]
    ppermute x1, waiting for transfers between devices: 18.6 us -> 14.8 us  [output_grad(): return lax.ppermute(summed, ('hi', 'tp'), pairs)]
    all_to_all x1, blocking collectives: 19.4 us -> 22.8 us  [body(): lax.all_to_all(grad_conv, SEQ, split_axis=1, concat_axis=0, tiled=True)]
  transfers between devices with their start and end apart: 14 -> 14, of which waited for: 10 -> 10; matrix products, arithmetic and copies ran while one was open for 16% -> 13% of each run, Pallas kernels for 0% -> 0%
where the time goes in v6:
time: 300 us; the launch traced here: 297 us
  waiting for transfers between devices  71.8 us (24%)
  blocking collectives  71.6 us (24%)
  starting transfers between devices  57.5 us (19%)
  matrix products  35.3 us (12%)
  local copies, waits for them, and re-layouts  34.4 us (11%)
  between operations  15 us (5%)
  other arithmetic  11 us (4%)
    all_to_all x1, blocking collectives, output_grad(): lax.all_to_all(chunks, 'tp', split_axis=0, concat_axis=0, tiled=True)  30.6 us
    all_to_all x1, blocking collectives, body(): lax.all_to_all(grad_conv, SEQ, split_axis=1, concat_axis=0, tiled=True)  22.8 us
    all_gather x1, waiting for transfers between devices, output_grad(): token_rows = lax.all_gather(cotangent, 'hi', axis=0, tiled=True)  19.2 us
    all_to_all x1, blocking collectives, body(): lax.all_to_all(conv_cols, SEQ, split_axis=0, concat_axis=1, tiled=True)  18.2 us
    ppermute x5, waiting for transfers between devices, butterfly_sum(): lax.ppermute(value, axis, [(i, i ^ stride) for i in range(devices)])  17.2 us
    ppermute x1, waiting for transfers between devices, output_grad(): return lax.ppermute(summed, ('hi', 'tp'), pairs)  14.8 us
    all_to_all x1, starting transfers between devices, body(): lax.all_to_all(long_filter.astype(jnp.bfloat16), SEQ, split_axis=1, conca...  11.6 us
    all_to_all x1, starting transfers between devices, body(): lax.all_to_all(gated_input, SEQ, split_axis=1, concat_axis=0, tiled=True)  10 us
  transfers between devices with their start and end apart: 14, of which 10 were waited for; matrix products, arithmetic and copies ran while one was open for 13% of the time, Pallas kernels for 0%

profile of v6, /device:TPU:6, one launch (start us, length us, event | category | flops | bytes accessed | tf_op | source)
XLA Modules:
  0.0 296.6 jit_solution(754927535458582863)
XLA Ops:
  9.8 11.6 %all-to-all-start.1 = ((bf16[128,32,32]{0,2,1:T(8,128)(2,1)}), bf16[128,32,32]{0,2,1:T(8,128)(2,1)S(1)}, u32[]{:S(2)}, u32[]{:S(2)}) async-start(bf16[128,32,32]{0,2,1:T(8,128)(2,1)} %bitcast.8), calls=%async_computation.1 | async-start | bytes 524288 | tf_op jit(solution)/shard_map/all_to_all | solution.py:152
  23.9 7.1 %collective-permute-done = bf16[6,3,1024]{2,0,1:T(8,128)(2,1)S(1)} collective-permute-done((bf16[6,3,1024]{2,0,1:T(8,128)(2,1)S(1)}, bf16[6,3,1024]{2,0,1:T(8,128)(2,1)S(1)}, u32[]{:S(2)}, u32[]{:S(2)}) %collective-permute-start) | collective-permute-done | bytes 36896 | tf_op jit(solution)/shard_map/ppermute | solution.py:15
  34.3 10.0 %all-to-all-start = ((bf16[128,32,32]{0,2,1:T(8,128)(2,1)}), bf16[128,32,32]{0,2,1:T(8,128)(2,1)S(1)}, u32[]{:S(2)}, u32[]{:S(2)}) async-start(bf16[128,32,32]{0,2,1:T(8,128)(2,1)} %bitcast.2), calls=%async_computation | async-start | bytes 524288 | tf_op jit(solution)/shard_map/all_to_all | solution.py:156
  50.3 5.8 %all-to-all-done = bf16[128,32,32]{0,2,1:T(8,128)(2,1)S(1)} async-done(((bf16[128,32,32]{0,2,1:T(8,128)(2,1)}), bf16[128,32,32]{0,2,1:T(8,128)(2,1)S(1)}, u32[]{:S(2)}, u32[]{:S(2)}) %all-to-all-start) | async-done | bytes 262176 | tf_op jit(solution)/shard_map/all_to_all | solution.py:156
  74.9 18.2 %all_to_all.86 = bf16[32,128,32]{1,2,0:T(8,128)(2,1)} all-to-all(bf16[32,128,32]{1,2,0:T(8,128)(2,1)S(1)} %copy.51), channel_id=1, replica_groups=mesh['hi'=8,'lo'=4,'tp'=8] {'hi','lo'}, dimensions={0} | all-to-all | bytes 524288 | tf_op jit(solution)/shard_map/all_to_all | solution.py:161
  93.0 19.2 %all-gather.5.cloned.1.call-done = bf16[1024,1024]{1,0:T(8,128)(2,1)} async-done(((bf16[128,1024]{1,0:T(8,128)(2,1)}), bf16[1024,1024]{1,0:T(8,128)(2,1)}) %all-gather.5.cloned.1.call-update) | async-done | bytes 2097168 | tf_op jit(solution)/shard_map/all_gather | solution.py:103
  112.2 4.6 %convolution_convert_fusion = bf16[1024,1024]{1,0:T(8,128)(2,1)S(1)} fusion(bf16[1024,1024]{1,0:T(8,128)(2,1)} %all-gather.5.cloned.1.call-done, bf16[1024,1024]{1,0:T(8,128)(2,1)} %all-gather.3.cloned.1.call-done), kind=kOutput, calls=%fused_computation.29 | convolution fusion | flops 2148532224 | bytes 6291456 | tf_op jit(solution)/shard_map/dot_general | solution.py:105
  116.8 30.6 %all_to_all.87 = bf16[8,128,1024]{2,1,0:T(8,128)(2,1)} all-to-all(bf16[8,128,1024]{2,1,0:T(8,128)(2,1)S(1)} %bitcast.202), channel_id=1, replica_groups=mesh['hi'=8,'lo'=4,'tp'=8] {'tp'}, dimensions={0} | all-to-all | bytes 4194304 | tf_op jit(solution)/shard_map/all_to_all | solution.py:113
  147.4 2.8 reduce_sum.75
  150.1 7.7 %collective-permute-start.1 = (bf16[128,1024]{1,0:T(8,128)(2,1)}, bf16[128,1024]{1,0:T(8,128)(2,1)}, u32[]{:S(2)}, u32[]{:S(2)}) collective-permute-start(bf16[128,1024]{1,0:T(8,128)(2,1)} %reduce_sum.75), channel_id=1, source_target_pairs={{0,0},{1,32},{2,64},{3,96},{4,128},{5,160},{6,192},{7,224},{32,1},... | collective-permute-start | bytes 786440 | tf_op jit(solution)/shard_map/ppermute | solution.py:122
  158.7 14.8 %collective-permute-done.1 = bf16[128,1024]{1,0:T(8,128)(2,1)} collective-permute-done((bf16[128,1024]{1,0:T(8,128)(2,1)}, bf16[128,1024]{1,0:T(8,128)(2,1)}, u32[]{:S(2)}, u32[]{:S(2)}) %collective-permute-start.1) | collective-permute-done | bytes 262176 | tf_op jit(solution)/shard_map/ppermute | solution.py:122
  177.2 22.8 %all_to_all.88 = bf16[128,32,32]{0,2,1:T(8,128)(2,1)} all-to-all(bf16[128,32,32]{0,2,1:T(8,128)(2,1)} %bitcast.212), channel_id=1, replica_groups=mesh['hi'=8,'lo'=4,'tp'=8] {'hi','lo'}, dimensions={1} | all-to-all | bytes 524288 | tf_op jit(solution)/shard_map/all_to_all | solution.py:165
  200.0 2.3 copy.54
  202.3 3.3 %reshape.148 = bf16[64,2048]{1,0:T(8,128)(2,1)} reshape(bf16[32,128,32]{2,1,0:T(8,128)(2,1)} %copy.54) | data formatting | bytes 524288 | tf_op jit(solution)/shard_map/reshape | solution.py:37
  227.0 6.7 %all-to-all-start.5 = ((bf16[32,128,32]{1,2,0:T(8,128)(2,1)}), bf16[32,128,32]{1,2,0:T(8,128)(2,1)S(1)}, u32[]{:S(2)}, u32[]{:S(2)}) async-start(bf16[32,128,32]{1,2,0:T(8,128)(2,1)} %copy.60), calls=%async_computation.5 | async-start | bytes 524288 | tf_op jit(solution)/shard_map/all_to_all | solution.py:171
  238.4 7.1 %all-to-all-done.5 = bf16[32,128,32]{1,2,0:T(8,128)(2,1)S(1)} async-done(((bf16[32,128,32]{1,2,0:T(8,128)(2,1)}), bf16[32,128,32]{1,2,0:T(8,128)(2,1)S(1)}, u32[]{:S(2)}, u32[]{:S(2)}) %all-to-all-start.5) | async-done | bytes 262176 | tf_op jit(solution)/shard_map/all_to_all | solution.py:171
  245.5 6.8 %all-to-all-start.6 = ((bf16[32,128,32]{1,2,0:T(8,128)(2,1)}), bf16[32,128,32]{1,2,0:T(8,128)(2,1)S(1)}, u32[]{:S(2)}, u32[]{:S(2)}) async-start(bf16[32,128,32]{1,2,0:T(8,128)(2,1)} %copy.65), calls=%async_computation.6 | async-start | bytes 524288 | tf_op jit(solution)/shard_map/all_to_all | solution.py:172
  258.3 4.6 %collective-permute-done.4 = f32[7,3,1024]{2,1,0:T(4,128)S(1)} collective-permute-done((f32[7,3,1024]{2,1,0:T(4,128)S(1)}, f32[7,3,1024]{2,1,0:T(4,128)S(1)}, u32[]{:S(2)}, u32[]{:S(2)}) %collective-permute-start.4) | collective-permute-done | bytes 86048 | tf_op jit(solution)/shard_map/ppermute | solution.py:129
  263.0 3.0 %collective-permute-start.5 = (f32[7,3,1024]{2,1,0:T(4,128)S(1)}, f32[7,3,1024]{2,1,0:T(4,128)S(1)}, u32[]{:S(2)}, u32[]{:S(2)}) collective-permute-start(f32[7,3,1024]{2,1,0:T(4,128)S(1)} %add.319), channel_id=1, source_target_pairs={{0,32},{8,40},{16,48},{24,56},{32,0},{40,8},{48,16},{56,24},{64,96... | collective-permute-start | bytes 258056 | tf_op jit(solution)/shard_map/ppermute | solution.py:129
  266.1 3.1 %collective-permute-start.2 = (bf16[6,3,1024]{2,0,1:T(8,128)(2,1)S(1)}, bf16[6,3,1024]{2,0,1:T(8,128)(2,1)S(1)}, u32[]{:S(2)}, u32[]{:S(2)}) collective-permute-start(bf16[6,3,1024]{2,0,1:T(8,128)(2,1)S(1)} %slice.122), channel_id=1, source_target_pairs={{8,0},{16,8},{24,16},{32,24},{40,32},{48,40},{56,48},{64,56},{72,6... | collective-permute-start | bytes 110600 | tf_op jit(solution)/shard_map/ppermute | solution.py:15
  271.6 4.1 %collective-permute-start.6 = (f32[7,3,1024]{2,1,0:T(4,128)S(1)}, f32[7,3,1024]{2,1,0:T(4,128)S(1)}, u32[]{:S(2)}, u32[]{:S(2)}) collective-permute-start(f32[7,3,1024]{2,1,0:T(4,128)S(1)} %add.320), channel_id=1, source_target_pairs={{0,64},{8,72},{16,80},{24,88},{32,96},{40,104},{48,112},{56,120},{... | collective-permute-start | bytes 258056 | tf_op jit(solution)/shard_map/ppermute | solution.py:129
  275.7 6.7 %collective-permute-done.6 = f32[7,3,1024]{2,1,0:T(4,128)S(1)} collective-permute-done((f32[7,3,1024]{2,1,0:T(4,128)S(1)}, f32[7,3,1024]{2,1,0:T(4,128)S(1)}, u32[]{:S(2)}, u32[]{:S(2)}) %collective-permute-start.6) | collective-permute-done | bytes 86048 | tf_op jit(solution)/shard_map/ppermute | solution.py:129
  283.1 2.3 fusion.19
  285.4 3.4 %collective-permute-done.7 = f32[7,3,1024]{2,1,0:T(4,128)S(1)} collective-permute-done((f32[7,3,1024]{2,1,0:T(4,128)S(1)}, f32[7,3,1024]{2,1,0:T(4,128)S(1)}, u32[]{:S(2)}, u32[]{:S(2)}) %collective-permute-start.7) | collective-permute-done | bytes 86048 | tf_op jit(solution)/shard_map/ppermute | solution.py:129
  (143 shorter events, 73.1 us)
Async XLA Ops:
  7.2 14.3 %copy-start.4 = (bf16[128,3,1024]{2,0,1:T(8,128)(2,1)S(1)}, bf16[128,3,1024]{2,0,1:T(8,128)(2,1)}, u32[]{:S(2)}) copy-start(bf16[128,3,1024]{2,0,1:T(8,128)(2,1)} %param.5) | copy-start | bytes 2359300
  7.2 16.4 %copy-start.18 = (f32[7,3,1024]{2,0,1:T(8,128)S(1)}, f32[7,3,1024]{2,0,1:T(8,128)}, u32[]{:S(2)}) copy-start(f32[7,3,1024]{2,0,1:T(8,128)} %param.8) | copy-start | bytes 258052
  7.2 85.8 %all-gather.3.cloned.1.call-start = ((), (), s32[]{:S(2)}) async-start(), calls=%async_computation.7 | async-start | bytes 2621440 | tf_op jit(solution)/shard_map/all_gather | solution.py:102
  9.8 24.5 %all-to-all-start.1 = ((bf16[128,32,32]{0,2,1:T(8,128)(2,1)}), bf16[128,32,32]{0,2,1:T(8,128)(2,1)S(1)}, u32[]{:S(2)}, u32[]{:S(2)}) async-start(bf16[128,32,32]{0,2,1:T(8,128)(2,1)} %bitcast.8), calls=%async_computation.1 | async-start | bytes 524288 | tf_op jit(solution)/shard_map/all_to_all | solution.py:152
  21.4 90.8 %all-gather.5.cloned.1.call-start = ((), (), s32[]{:S(2)}) async-start(), calls=%async_computation.8 | async-start | bytes 2359296 | tf_op jit(solution)/shard_map/all_gather | solution.py:103
  21.5 9.5 %collective-permute-start = (bf16[6,3,1024]{2,0,1:T(8,128)(2,1)S(1)}, bf16[6,3,1024]{2,0,1:T(8,128)(2,1)S(1)}, u32[]{:S(2)}, u32[]{:S(2)}) collective-permute-start(bf16[6,3,1024]{2,0,1:T(8,128)(2,1)S(1)} %slice.87), channel_id=1, source_target_pairs={{0,8},{8,16},{16,24},{24,32},{32,40},{40,48},{48,56},{56,64},{64,7... | collective-permute-start | bytes 110600 | tf_op jit(solution)/shard_map/ppermute | solution.py:15
  23.7 10.6 %copy-start.8 = (f32[3,1024]{1,0:T(4,128)}, f32[3,1024]{1,0:T(4,128)S(1)}, u32[]{:S(2)}) copy-start(f32[3,1024]{1,0:T(4,128)S(1)} %get-tuple-element.56) | copy-start | bytes 36868
  23.7 10.6 %copy-start.10 = (f32[3,1024]{1,0:T(4,128)}, f32[3,1024]{1,0:T(4,128)S(1)}, u32[]{:S(2)}) copy-start(f32[3,1024]{1,0:T(4,128)S(1)} %get-tuple-element.57) | copy-start | bytes 36868
  34.3 21.9 %all-to-all-start = ((bf16[128,32,32]{0,2,1:T(8,128)(2,1)}), bf16[128,32,32]{0,2,1:T(8,128)(2,1)S(1)}, u32[]{:S(2)}, u32[]{:S(2)}) async-start(bf16[128,32,32]{0,2,1:T(8,128)(2,1)} %bitcast.2), calls=%async_computation | async-start | bytes 524288 | tf_op jit(solution)/shard_map/all_to_all | solution.py:156
  150.1 23.3 %collective-permute-start.1 = (bf16[128,1024]{1,0:T(8,128)(2,1)}, bf16[128,1024]{1,0:T(8,128)(2,1)}, u32[]{:S(2)}, u32[]{:S(2)}) collective-permute-start(bf16[128,1024]{1,0:T(8,128)(2,1)} %reduce_sum.75), channel_id=1, source_target_pairs={{0,0},{1,32},{2,64},{3,96},{4,128},{5,160},{6,192},{7,224},{32,1},... | collective-permute-start | bytes 786440 | tf_op jit(solution)/shard_map/ppermute | solution.py:122
  227.0 18.4 %all-to-all-start.5 = ((bf16[32,128,32]{1,2,0:T(8,128)(2,1)}), bf16[32,128,32]{1,2,0:T(8,128)(2,1)S(1)}, u32[]{:S(2)}, u32[]{:S(2)}) async-start(bf16[32,128,32]{1,2,0:T(8,128)(2,1)} %copy.60), calls=%async_computation.5 | async-start | bytes 524288 | tf_op jit(solution)/shard_map/all_to_all | solution.py:171
  237.4 15.2 %copy-start.1 = (bf16[128,3,1024]{2,0,1:T(8,128)(2,1)S(1)}, bf16[128,3,1024]{2,0,1:T(8,128)(2,1)}, u32[]{:S(2)}) copy-start(bf16[128,3,1024]{2,0,1:T(8,128)(2,1)} %copy-done) | copy-start | bytes 2359300
  245.5 23.7 %all-to-all-start.6 = ((bf16[32,128,32]{1,2,0:T(8,128)(2,1)}), bf16[32,128,32]{1,2,0:T(8,128)(2,1)S(1)}, u32[]{:S(2)}, u32[]{:S(2)}) async-start(bf16[32,128,32]{1,2,0:T(8,128)(2,1)} %copy.65), calls=%async_computation.6 | async-start | bytes 524288 | tf_op jit(solution)/shard_map/all_to_all | solution.py:172
  255.3 1.4 collective-permute-start.3
  256.7 6.2 %collective-permute-start.4 = (f32[7,3,1024]{2,1,0:T(4,128)S(1)}, f32[7,3,1024]{2,1,0:T(4,128)S(1)}, u32[]{:S(2)}, u32[]{:S(2)}) collective-permute-start(f32[7,3,1024]{2,1,0:T(4,128)S(1)} %add.318), channel_id=1, source_target_pairs={{0,16},{8,24},{16,0},{24,8},{32,48},{40,56},{48,32},{56,40},{64,80... | collective-permute-start | bytes 258056 | tf_op jit(solution)/shard_map/ppermute | solution.py:129
  263.0 8.6 %collective-permute-start.5 = (f32[7,3,1024]{2,1,0:T(4,128)S(1)}, f32[7,3,1024]{2,1,0:T(4,128)S(1)}, u32[]{:S(2)}, u32[]{:S(2)}) collective-permute-start(f32[7,3,1024]{2,1,0:T(4,128)S(1)} %add.319), channel_id=1, source_target_pairs={{0,32},{8,40},{16,48},{24,56},{32,0},{40,8},{48,16},{56,24},{64,96... | collective-permute-start | bytes 258056 | tf_op jit(solution)/shard_map/ppermute | solution.py:129
  266.1 9.6 %collective-permute-start.2 = (bf16[6,3,1024]{2,0,1:T(8,128)(2,1)S(1)}, bf16[6,3,1024]{2,0,1:T(8,128)(2,1)S(1)}, u32[]{:S(2)}, u32[]{:S(2)}) collective-permute-start(bf16[6,3,1024]{2,0,1:T(8,128)(2,1)S(1)} %slice.122), channel_id=1, source_target_pairs={{8,0},{16,8},{24,16},{32,24},{40,32},{48,40},{56,48},{64,56},{72,6... | collective-permute-start | bytes 110600 | tf_op jit(solution)/shard_map/ppermute | solution.py:15
  269.3 13.8 %copy-start.9 = (f32[3,1024]{1,0:T(4,128)S(1)}, f32[3,1024]{1,0:T(4,128)}, u32[]{:S(2)}) copy-start(f32[3,1024]{1,0:T(4,128)} %copy-done.8) | copy-start | bytes 36868
  269.3 13.8 %copy-start.11 = (f32[3,1024]{1,0:T(4,128)S(1)}, f32[3,1024]{1,0:T(4,128)}, u32[]{:S(2)}) copy-start(f32[3,1024]{1,0:T(4,128)} %copy-done.10) | copy-start | bytes 36868
  269.3 13.8 %copy-start.13 = (f32[3,1024]{1,0:T(4,128)S(1)}, f32[3,1024]{1,0:T(4,128)}, u32[]{:S(2)}) copy-start(f32[3,1024]{1,0:T(4,128)} %copy-done.12) | copy-start | bytes 36868
  269.3 13.8 %copy-start.15 = (f32[3,1024]{1,0:T(4,128)S(1)}, f32[3,1024]{1,0:T(4,128)}, u32[]{:S(2)}) copy-start(f32[3,1024]{1,0:T(4,128)} %copy-done.14) | copy-start | bytes 36868
  269.3 13.8 %copy-start.17 = (f32[1,3,1024]{2,1,0:T(4,128)S(1)}, f32[1,3,1024]{2,1,0:T(4,128)}, u32[]{:S(2)}) copy-start(f32[1,3,1024]{2,1,0:T(4,128)} %copy-done.16) | copy-start | bytes 36868
  271.6 10.9 %collective-permute-start.6 = (f32[7,3,1024]{2,1,0:T(4,128)S(1)}, f32[7,3,1024]{2,1,0:T(4,128)S(1)}, u32[]{:S(2)}, u32[]{:S(2)}) collective-permute-start(f32[7,3,1024]{2,1,0:T(4,128)S(1)} %add.320), channel_id=1, source_target_pairs={{0,64},{8,72},{16,80},{24,88},{32,96},{40,104},{48,112},{56,120},{... | collective-permute-start | bytes 258056 | tf_op jit(solution)/shard_map/ppermute | solution.py:129
  282.5 6.4 %collective-permute-start.7 = (f32[7,3,1024]{2,1,0:T(4,128)S(1)}, f32[7,3,1024]{2,1,0:T(4,128)S(1)}, u32[]{:S(2)}, u32[]{:S(2)}) collective-permute-start(f32[7,3,1024]{2,1,0:T(4,128)S(1)} %add.321), channel_id=1, source_target_pairs={{0,128},{8,136},{16,144},{24,152},{32,160},{40,168},{48,176},{56,1... | collective-permute-start | bytes 258056 | tf_op jit(solution)/shard_map/ppermute | solution.py:129
  (9 other events, 47.7 us)
Sparse Core Ops, SparseCore 0:
  9.8 36.7 all-gather.2
  49.2 62.8 all-gather.4

commit v7 on v6

--- a/solution.py
+++ b/solution.py
@@ -5,7 +5,7 @@
 from jax import lax
 from jax.sharding import PartitionSpec as P
 
-highest = lax.Precision.HIGH
+highest = lax.Precision.DEFAULT
 SEQ = ("hi", "lo")
 
 

time: 300 us -> 301 us (level)
  waiting for transfers between devices: 71.8 us -> 90.7 us
  matrix products: 35.3 us -> 23.1 us
    all_to_all x1, waiting for transfers between devices: 0.01 us -> 9.17 us  [body(): lax.all_to_all(long_filter.astype(jnp.bfloat16), SEQ, split_axis=1, conca...]
    all_gather x1, waiting for transfers between devices: 19.2 us -> 28.1 us  [output_grad(): token_rows = lax.all_gather(cotangent, 'hi', axis=0, tiled=True)]
    ppermute x2, waiting for transfers between devices: 7.1 us -> 0.01 us  [shifted(): return lax.ppermute(value, axis, pairs)]
  transfers between devices with their start and end apart: 14 -> 14, of which waited for: 10 -> 10; matrix products, arithmetic and copies ran while one was open for 13% -> 11% of each run, Pallas kernels for 0% -> 0%
where the time goes in v7:
time: 301 us; the launch traced here: 299 us
  waiting for transfers between devices  90.7 us (30%)
  blocking collectives  70.4 us (23%)
  starting transfers between devices  56.1 us (19%)
  local copies, waits for them, and re-layouts  32.3 us (11%)
  matrix products  23.1 us (8%)
  between operations  15.2 us (5%)
  other arithmetic  11 us (4%)
    all_to_all x1, blocking collectives, output_grad(): lax.all_to_all(chunks, 'tp', split_axis=0, concat_axis=0, tiled=True)  30.6 us
    all_gather x1, waiting for transfers between devices, output_grad(): token_rows = lax.all_gather(cotangent, 'hi', axis=0, tiled=True)  28.1 us
    all_to_all x1, blocking collectives, body(): lax.all_to_all(grad_conv, SEQ, split_axis=1, concat_axis=0, tiled=True)  20.8 us
    all_to_all x1, blocking collectives, body(): lax.all_to_all(conv_cols, SEQ, split_axis=0, concat_axis=1, tiled=True)  18.9 us
    ppermute x1, waiting for transfers between devices, output_grad(): return lax.ppermute(summed, ('hi', 'tp'), pairs)  17.4 us
    ppermute x5, waiting for transfers between devices, butterfly_sum(): lax.ppermute(value, axis, [(i, i ^ stride) for i in range(devices)])  17.2 us
    all_to_all x1, starting transfers between devices, body(): lax.all_to_all(long_filter.astype(jnp.bfloat16), SEQ, split_axis=1, conca...  12.3 us
    ppermute x5, starting transfers between devices, butterfly_sum(): lax.ppermute(value, axis, [(i, i ^ stride) for i in range(devices)])  9.51 us
  transfers between devices with their start and end apart: 14, of which 10 were waited for; matrix products, arithmetic and copies ran while one was open for 11% of the time, Pallas kernels for 0%

profile of v7, /device:TPU:6, one launch (start us, length us, event | category | flops | bytes accessed | tf_op | source)
XLA Modules:
  0.0 298.8 jit_solution(15399011179094269794)
XLA Ops:
  12.6 12.3 %all-to-all-start.1 = ((bf16[128,32,32]{0,2,1:T(8,128)(2,1)}), bf16[128,32,32]{0,2,1:T(8,128)(2,1)S(1)}, u32[]{:S(2)}, u32[]{:S(2)}) async-start(bf16[128,32,32]{0,2,1:T(8,128)(2,1)} %bitcast.8), calls=%async_computation.1 | async-start | bytes 524288 | tf_op jit(solution)/shard_map/all_to_all | solution.py:152
  29.3 9.2 %all-to-all-done.1 = bf16[128,32,32]{0,2,1:T(8,128)(2,1)S(1)} async-done(((bf16[128,32,32]{0,2,1:T(8,128)(2,1)}), bf16[128,32,32]{0,2,1:T(8,128)(2,1)S(1)}, u32[]{:S(2)}, u32[]{:S(2)}) %all-to-all-start.1) | async-done | bytes 262176 | tf_op jit(solution)/shard_map/all_to_all | solution.py:152
  38.5 7.5 %all-to-all-start = ((bf16[128,32,32]{0,2,1:T(8,128)(2,1)}), bf16[128,32,32]{0,2,1:T(8,128)(2,1)S(1)}, u32[]{:S(2)}, u32[]{:S(2)}) async-start(bf16[128,32,32]{0,2,1:T(8,128)(2,1)} %bitcast.2), calls=%async_computation | async-start | bytes 524288 | tf_op jit(solution)/shard_map/all_to_all | solution.py:156
  50.6 8.5 %all-to-all-done = bf16[128,32,32]{0,2,1:T(8,128)(2,1)S(1)} async-done(((bf16[128,32,32]{0,2,1:T(8,128)(2,1)}), bf16[128,32,32]{0,2,1:T(8,128)(2,1)S(1)}, u32[]{:S(2)}, u32[]{:S(2)}) %all-to-all-start) | async-done | bytes 262176 | tf_op jit(solution)/shard_map/all_to_all | solution.py:156
  73.2 18.9 %all_to_all.86 = bf16[32,128,32]{1,2,0:T(8,128)(2,1)} all-to-all(bf16[32,128,32]{1,2,0:T(8,128)(2,1)S(1)} %copy.51), channel_id=1, replica_groups=mesh['hi'=8,'lo'=4,'tp'=8] {'hi','lo'}, dimensions={0} | all-to-all | bytes 524288 | tf_op jit(solution)/shard_map/all_to_all | solution.py:161
  92.1 28.1 %all-gather.5.cloned.1.call-done = bf16[1024,1024]{1,0:T(8,128)(2,1)} async-done(((bf16[128,1024]{1,0:T(8,128)(2,1)}), bf16[1024,1024]{1,0:T(8,128)(2,1)}) %all-gather.5.cloned.1.call-update) | async-done | bytes 2097168 | tf_op jit(solution)/shard_map/all_gather | solution.py:103
  120.2 4.6 %convolution_convert_fusion = bf16[1024,1024]{1,0:T(8,128)(2,1)S(1)} fusion(bf16[1024,1024]{1,0:T(8,128)(2,1)} %all-gather.5.cloned.1.call-done, bf16[1024,1024]{1,0:T(8,128)(2,1)} %all-gather.3.cloned.1.call-done), kind=kOutput, calls=%fused_computation.29 | convolution fusion | flops 2148532224 | bytes 6291456 | tf_op jit(solution)/shard_map/dot_general | solution.py:105
  124.8 30.6 %all_to_all.87 = bf16[8,128,1024]{2,1,0:T(8,128)(2,1)} all-to-all(bf16[8,128,1024]{2,1,0:T(8,128)(2,1)S(1)} %bitcast.196), channel_id=1, replica_groups=mesh['hi'=8,'lo'=4,'tp'=8] {'tp'}, dimensions={0} | all-to-all | bytes 4194304 | tf_op jit(solution)/shard_map/all_to_all | solution.py:113
  155.4 2.8 reduce_sum.75
  158.2 7.8 %collective-permute-start.1 = (bf16[128,1024]{1,0:T(8,128)(2,1)}, bf16[128,1024]{1,0:T(8,128)(2,1)}, u32[]{:S(2)}, u32[]{:S(2)}) collective-permute-start(bf16[128,1024]{1,0:T(8,128)(2,1)} %reduce_sum.75), channel_id=1, source_target_pairs={{0,0},{1,32},{2,64},{3,96},{4,128},{5,160},{6,192},{7,224},{32,1},... | collective-permute-start | bytes 786440 | tf_op jit(solution)/shard_map/ppermute | solution.py:122
  166.8 17.4 %collective-permute-done.1 = bf16[128,1024]{1,0:T(8,128)(2,1)} collective-permute-done((bf16[128,1024]{1,0:T(8,128)(2,1)}, bf16[128,1024]{1,0:T(8,128)(2,1)}, u32[]{:S(2)}, u32[]{:S(2)}) %collective-permute-start.1) | collective-permute-done | bytes 262176 | tf_op jit(solution)/shard_map/ppermute | solution.py:122
  187.9 20.8 %all_to_all.88 = bf16[128,32,32]{0,2,1:T(8,128)(2,1)} all-to-all(bf16[128,32,32]{0,2,1:T(8,128)(2,1)} %bitcast.212), channel_id=1, replica_groups=mesh['hi'=8,'lo'=4,'tp'=8] {'hi','lo'}, dimensions={1} | all-to-all | bytes 524288 | tf_op jit(solution)/shard_map/all_to_all | solution.py:165
  208.8 2.3 copy.54
  211.0 3.0 reshape.148
  228.7 7.1 %all-to-all-start.5 = ((bf16[32,128,32]{1,2,0:T(8,128)(2,1)}), bf16[32,128,32]{1,2,0:T(8,128)(2,1)S(1)}, u32[]{:S(2)}, u32[]{:S(2)}) async-start(bf16[32,128,32]{1,2,0:T(8,128)(2,1)} %copy.60), calls=%async_computation.5 | async-start | bytes 524288 | tf_op jit(solution)/shard_map/all_to_all | solution.py:171
  238.4 9.0 %all-to-all-done.5 = bf16[32,128,32]{1,2,0:T(8,128)(2,1)S(1)} async-done(((bf16[32,128,32]{1,2,0:T(8,128)(2,1)}), bf16[32,128,32]{1,2,0:T(8,128)(2,1)S(1)}, u32[]{:S(2)}, u32[]{:S(2)}) %all-to-all-start.5) | async-done | bytes 262176 | tf_op jit(solution)/shard_map/all_to_all | solution.py:171
  247.4 6.8 %all-to-all-start.6 = ((bf16[32,128,32]{1,2,0:T(8,128)(2,1)}), bf16[32,128,32]{1,2,0:T(8,128)(2,1)S(1)}, u32[]{:S(2)}, u32[]{:S(2)}) async-start(bf16[32,128,32]{1,2,0:T(8,128)(2,1)} %copy.65), calls=%async_computation.6 | async-start | bytes 524288 | tf_op jit(solution)/shard_map/all_to_all | solution.py:172
  260.3 4.6 %collective-permute-done.4 = f32[7,3,1024]{2,1,0:T(4,128)S(1)} collective-permute-done((f32[7,3,1024]{2,1,0:T(4,128)S(1)}, f32[7,3,1024]{2,1,0:T(4,128)S(1)}, u32[]{:S(2)}, u32[]{:S(2)}) %collective-permute-start.4) | collective-permute-done | bytes 86048 | tf_op jit(solution)/shard_map/ppermute | solution.py:129
  264.9 3.0 %collective-permute-start.5 = (f32[7,3,1024]{2,1,0:T(4,128)S(1)}, f32[7,3,1024]{2,1,0:T(4,128)S(1)}, u32[]{:S(2)}, u32[]{:S(2)}) collective-permute-start(f32[7,3,1024]{2,1,0:T(4,128)S(1)} %add.319), channel_id=1, source_target_pairs={{0,32},{8,40},{16,48},{24,56},{32,0},{40,8},{48,16},{56,24},{64,96... | collective-permute-start | bytes 258056 | tf_op jit(solution)/shard_map/ppermute | solution.py:129
  268.0 3.1 %collective-permute-start.2 = (bf16[6,3,1024]{2,0,1:T(8,128)(2,1)S(1)}, bf16[6,3,1024]{2,0,1:T(8,128)(2,1)S(1)}, u32[]{:S(2)}, u32[]{:S(2)}) collective-permute-start(bf16[6,3,1024]{2,0,1:T(8,128)(2,1)S(1)} %slice.122), channel_id=1, source_target_pairs={{8,0},{16,8},{24,16},{32,24},{40,32},{48,40},{56,48},{64,56},{72,6... | collective-permute-start | bytes 110600 | tf_op jit(solution)/shard_map/ppermute | solution.py:15
  273.5 4.1 %collective-permute-start.6 = (f32[7,3,1024]{2,1,0:T(4,128)S(1)}, f32[7,3,1024]{2,1,0:T(4,128)S(1)}, u32[]{:S(2)}, u32[]{:S(2)}) collective-permute-start(f32[7,3,1024]{2,1,0:T(4,128)S(1)} %add.320), channel_id=1, source_target_pairs={{0,64},{8,72},{16,80},{24,88},{32,96},{40,104},{48,112},{56,120},{... | collective-permute-start | bytes 258056 | tf_op jit(solution)/shard_map/ppermute | solution.py:129
  277.7 6.7 %collective-permute-done.6 = f32[7,3,1024]{2,1,0:T(4,128)S(1)} collective-permute-done((f32[7,3,1024]{2,1,0:T(4,128)S(1)}, f32[7,3,1024]{2,1,0:T(4,128)S(1)}, u32[]{:S(2)}, u32[]{:S(2)}) %collective-permute-start.6) | collective-permute-done | bytes 86048 | tf_op jit(solution)/shard_map/ppermute | solution.py:129
  285.0 2.3 fusion.19
  287.3 3.4 %collective-permute-done.7 = f32[7,3,1024]{2,1,0:T(4,128)S(1)} collective-permute-done((f32[7,3,1024]{2,1,0:T(4,128)S(1)}, f32[7,3,1024]{2,1,0:T(4,128)S(1)}, u32[]{:S(2)}, u32[]{:S(2)}) %collective-permute-start.7) | collective-permute-done | bytes 86048 | tf_op jit(solution)/shard_map/ppermute | solution.py:129
  (143 shorter events, 59.7 us)
Async XLA Ops:
  7.2 18.8 %copy-start.4 = (bf16[128,3,1024]{2,0,1:T(8,128)(2,1)S(1)}, bf16[128,3,1024]{2,0,1:T(8,128)(2,1)}, u32[]{:S(2)}) copy-start(bf16[128,3,1024]{2,0,1:T(8,128)(2,1)} %param.5) | copy-start | bytes 2359300
  7.2 18.5 %copy-start.18 = (f32[7,3,1024]{2,0,1:T(8,128)S(1)}, f32[7,3,1024]{2,0,1:T(8,128)}, u32[]{:S(2)}) copy-start(f32[7,3,1024]{2,0,1:T(8,128)} %param.8) | copy-start | bytes 258052
  7.2 84.9 %all-gather.3.cloned.1.call-start = ((), (), s32[]{:S(2)}) async-start(), calls=%async_computation.7 | async-start | bytes 2621440 | tf_op jit(solution)/shard_map/all_gather | solution.py:102
  8.7 17.2 %collective-permute-start = (bf16[6,3,1024]{2,0,1:T(8,128)(2,1)S(1)}, bf16[6,3,1024]{2,0,1:T(8,128)(2,1)S(1)}, u32[]{:S(2)}, u32[]{:S(2)}) collective-permute-start(bf16[6,3,1024]{2,0,1:T(8,128)(2,1)S(1)} %slice.87), channel_id=1, source_target_pairs={{0,8},{8,16},{16,24},{24,32},{32,40},{40,48},{48,56},{56,64},{64,7... | collective-permute-start | bytes 110600 | tf_op jit(solution)/shard_map/ppermute | solution.py:15
  12.6 26.0 %all-to-all-start.1 = ((bf16[128,32,32]{0,2,1:T(8,128)(2,1)}), bf16[128,32,32]{0,2,1:T(8,128)(2,1)S(1)}, u32[]{:S(2)}, u32[]{:S(2)}) async-start(bf16[128,32,32]{0,2,1:T(8,128)(2,1)} %bitcast.8), calls=%async_computation.1 | async-start | bytes 524288 | tf_op jit(solution)/shard_map/all_to_all | solution.py:152
  24.9 95.3 %all-gather.5.cloned.1.call-start = ((), (), s32[]{:S(2)}) async-start(), calls=%async_computation.8 | async-start | bytes 2359296 | tf_op jit(solution)/shard_map/all_gather | solution.py:103
  26.0 12.5 %copy-start.16 = (f32[1,3,1024]{2,1,0:T(4,128)}, f32[1,3,1024]{2,1,0:T(4,128)S(1)}, u32[]{:S(2)}) copy-start(f32[1,3,1024]{2,1,0:T(4,128)S(1)} %copy.94) | copy-start | bytes 36868
  38.5 20.6 %all-to-all-start = ((bf16[128,32,32]{0,2,1:T(8,128)(2,1)}), bf16[128,32,32]{0,2,1:T(8,128)(2,1)S(1)}, u32[]{:S(2)}, u32[]{:S(2)}) async-start(bf16[128,32,32]{0,2,1:T(8,128)(2,1)} %bitcast.2), calls=%async_computation | async-start | bytes 524288 | tf_op jit(solution)/shard_map/all_to_all | solution.py:156
  155.4 10.5 %copy-start.7 = (bf16[32,128,32]{1,2,0:T(8,128)(2,1)S(1)}, bf16[32,128,32]{1,2,0:T(8,128)(2,1)}, u32[]{:S(2)}) copy-start(bf16[32,128,32]{1,2,0:T(8,128)(2,1)} %all_to_all.86) | copy-start | bytes 786436
  158.2 26.0 %collective-permute-start.1 = (bf16[128,1024]{1,0:T(8,128)(2,1)}, bf16[128,1024]{1,0:T(8,128)(2,1)}, u32[]{:S(2)}, u32[]{:S(2)}) collective-permute-start(bf16[128,1024]{1,0:T(8,128)(2,1)} %reduce_sum.75), channel_id=1, source_target_pairs={{0,0},{1,32},{2,64},{3,96},{4,128},{5,160},{6,192},{7,224},{32,1},... | collective-permute-start | bytes 786440 | tf_op jit(solution)/shard_map/ppermute | solution.py:122
  228.7 18.7 %all-to-all-start.5 = ((bf16[32,128,32]{1,2,0:T(8,128)(2,1)}), bf16[32,128,32]{1,2,0:T(8,128)(2,1)S(1)}, u32[]{:S(2)}, u32[]{:S(2)}) async-start(bf16[32,128,32]{1,2,0:T(8,128)(2,1)} %copy.60), calls=%async_computation.5 | async-start | bytes 524288 | tf_op jit(solution)/shard_map/all_to_all | solution.py:171
  237.4 17.1 %copy-start.1 = (bf16[128,3,1024]{2,0,1:T(8,128)(2,1)S(1)}, bf16[128,3,1024]{2,0,1:T(8,128)(2,1)}, u32[]{:S(2)}) copy-start(bf16[128,3,1024]{2,0,1:T(8,128)(2,1)} %copy-done) | copy-start | bytes 2359300
  247.4 23.7 %all-to-all-start.6 = ((bf16[32,128,32]{1,2,0:T(8,128)(2,1)}), bf16[32,128,32]{1,2,0:T(8,128)(2,1)S(1)}, u32[]{:S(2)}, u32[]{:S(2)}) async-start(bf16[32,128,32]{1,2,0:T(8,128)(2,1)} %copy.65), calls=%async_computation.6 | async-start | bytes 524288 | tf_op jit(solution)/shard_map/all_to_all | solution.py:172
  257.2 1.4 collective-permute-start.3
  258.7 6.2 %collective-permute-start.4 = (f32[7,3,1024]{2,1,0:T(4,128)S(1)}, f32[7,3,1024]{2,1,0:T(4,128)S(1)}, u32[]{:S(2)}, u32[]{:S(2)}) collective-permute-start(f32[7,3,1024]{2,1,0:T(4,128)S(1)} %add.318), channel_id=1, source_target_pairs={{0,16},{8,24},{16,0},{24,8},{32,48},{40,56},{48,32},{56,40},{64,80... | collective-permute-start | bytes 258056 | tf_op jit(solution)/shard_map/ppermute | solution.py:129
  264.9 8.6 %collective-permute-start.5 = (f32[7,3,1024]{2,1,0:T(4,128)S(1)}, f32[7,3,1024]{2,1,0:T(4,128)S(1)}, u32[]{:S(2)}, u32[]{:S(2)}) collective-permute-start(f32[7,3,1024]{2,1,0:T(4,128)S(1)} %add.319), channel_id=1, source_target_pairs={{0,32},{8,40},{16,48},{24,56},{32,0},{40,8},{48,16},{56,24},{64,96... | collective-permute-start | bytes 258056 | tf_op jit(solution)/shard_map/ppermute | solution.py:129
  268.0 9.6 %collective-permute-start.2 = (bf16[6,3,1024]{2,0,1:T(8,128)(2,1)S(1)}, bf16[6,3,1024]{2,0,1:T(8,128)(2,1)S(1)}, u32[]{:S(2)}, u32[]{:S(2)}) collective-permute-start(bf16[6,3,1024]{2,0,1:T(8,128)(2,1)S(1)} %slice.122), channel_id=1, source_target_pairs={{8,0},{16,8},{24,16},{32,24},{40,32},{48,40},{56,48},{64,56},{72,6... | collective-permute-start | bytes 110600 | tf_op jit(solution)/shard_map/ppermute | solution.py:15
  271.2 13.8 %copy-start.9 = (f32[3,1024]{1,0:T(4,128)S(1)}, f32[3,1024]{1,0:T(4,128)}, u32[]{:S(2)}) copy-start(f32[3,1024]{1,0:T(4,128)} %copy-done.8) | copy-start | bytes 36868
  271.2 13.8 %copy-start.11 = (f32[3,1024]{1,0:T(4,128)S(1)}, f32[3,1024]{1,0:T(4,128)}, u32[]{:S(2)}) copy-start(f32[3,1024]{1,0:T(4,128)} %copy-done.10) | copy-start | bytes 36868
  271.2 13.8 %copy-start.13 = (f32[3,1024]{1,0:T(4,128)S(1)}, f32[3,1024]{1,0:T(4,128)}, u32[]{:S(2)}) copy-start(f32[3,1024]{1,0:T(4,128)} %copy-done.12) | copy-start | bytes 36868
  271.2 13.8 %copy-start.15 = (f32[3,1024]{1,0:T(4,128)S(1)}, f32[3,1024]{1,0:T(4,128)}, u32[]{:S(2)}) copy-start(f32[3,1024]{1,0:T(4,128)} %copy-done.14) | copy-start | bytes 36868
  271.3 13.8 %copy-start.17 = (f32[1,3,1024]{2,1,0:T(4,128)S(1)}, f32[1,3,1024]{2,1,0:T(4,128)}, u32[]{:S(2)}) copy-start(f32[1,3,1024]{2,1,0:T(4,128)} %copy-done.16) | copy-start | bytes 36868
  273.5 10.9 %collective-permute-start.6 = (f32[7,3,1024]{2,1,0:T(4,128)S(1)}, f32[7,3,1024]{2,1,0:T(4,128)S(1)}, u32[]{:S(2)}, u32[]{:S(2)}) collective-permute-start(f32[7,3,1024]{2,1,0:T(4,128)S(1)} %add.320), channel_id=1, source_target_pairs={{0,64},{8,72},{16,80},{24,88},{32,96},{40,104},{48,112},{56,120},{... | collective-permute-start | bytes 258056 | tf_op jit(solution)/shard_map/ppermute | solution.py:129
  284.4 6.4 %collective-permute-start.7 = (f32[7,3,1024]{2,1,0:T(4,128)S(1)}, f32[7,3,1024]{2,1,0:T(4,128)S(1)}, u32[]{:S(2)}, u32[]{:S(2)}) collective-permute-start(f32[7,3,1024]{2,1,0:T(4,128)S(1)} %add.321), channel_id=1, source_target_pairs={{0,128},{8,136},{16,144},{24,152},{32,160},{40,168},{48,176},{56,1... | collective-permute-start | bytes 258056 | tf_op jit(solution)/shard_map/ppermute | solution.py:129
  (9 other events, 19.7 us)
Sparse Core Ops, SparseCore 0:
  9.8 42.7 all-gather.2
  55.2 64.9 all-gather.4

commit v8 on v6

--- a/solution.py
+++ b/solution.py
@@ -96,6 +96,24 @@
 
 def times_bf16(left_array, right_array):
     return (left_array.astype(jnp.float32) * right_array.astype(jnp.float32)).astype(jnp.bfloat16)
+
+
+SHORT_ROUTES = (
+    (0, 6, 1, 4, 3, 5, 2, 7),
+    (7, 0, 4, 1, 5, 2, 6, 3),
+    (0, 5, 1, 4, 2, 6, 3, 7),
+    (4, 0, 5, 1, 6, 2, 7, 3),
+    (4, 0, 5, 1, 6, 2, 7, 3),
+    (0, 4, 1, 5, 3, 6, 2, 7),
+    (4, 1, 5, 2, 6, 3, 7, 0),
+    (0, 4, 2, 6, 3, 5, 1, 7),
+)
+
+
+def chunk_orders(hi_count, tp_count):
+    if hi_count == len(SHORT_ROUTES) and tp_count == len(SHORT_ROUTES[0]):
+        return SHORT_ROUTES
+    return tuple(tuple(range(tp_count)) for _ in range(hi_count))
 
 
 def output_grad(cotangent, out_weight, ready):
@@ -109,15 +127,16 @@
         preferred_element_type=jnp.float32,
     ).astype(jnp.bfloat16)
     tp_parts = lax.axis_size("tp")
-    chunks = partial_value.reshape((tp_parts, -1) + partial_value.shape[1:])
+    hi_count = lax.axis_size("hi")
+    orders = chunk_orders(hi_count, tp_parts)
+    order_row = jnp.asarray(orders, jnp.int32)[lax.axis_index("hi")]
+    chunks = partial_value.reshape((tp_parts, -1) + partial_value.shape[1:])[order_row]
     received = lax.all_to_all(chunks, "tp", split_axis=0, concat_axis=0, tiled=True)
     summed = jnp.sum(received.astype(jnp.float32), axis=0).astype(jnp.bfloat16)
-    hi_count = lax.axis_size("hi")
-    tp_count = lax.axis_size("tp")
     pairs = [
-        (row * tp_count + col, col * tp_count + row)
+        (row * tp_parts + col, orders[row][col] * tp_parts + row)
         for row in range(hi_count)
-        for col in range(tp_count)
+        for col in range(tp_parts)
     ]
     return lax.ppermute(summed, ("hi", "tp"), pairs)
 

time: 300 us -> 304 us (1.013)
  blocking collectives: 71.6 us -> 57.9 us
  waiting for transfers between devices: 71.8 us -> 78.1 us
  local copies, waits for them, and re-layouts: 34.4 us -> 38.9 us
  starting transfers between devices: 57.5 us -> 61.5 us
    all_to_all x1 -> x0, blocking collectives: 18.2 us -> none  [body(): lax.all_to_all(conv_cols, SEQ, split_axis=0, concat_axis=1, tiled=True)]
    all_to_all x0 -> x1, waiting for transfers between devices: none -> 10.5 us  [body(): lax.all_to_all(conv_cols, SEQ, split_axis=0, concat_axis=1, tiled=True)]
    all_to_all x0 -> x1, starting transfers between devices: none -> 6.57 us  [body(): lax.all_to_all(conv_cols, SEQ, split_axis=0, concat_axis=1, tiled=True)]
    all_to_all x1, blocking collectives: 22.8 us -> 27.3 us  [body(): lax.all_to_all(grad_conv, SEQ, split_axis=1, concat_axis=0, tiled=True)]
    gather x0 -> x1, local copies, waits for them, and re-layouts: none -> 3.74 us  [output_grad(): partial_value.reshape((tp_parts, -1) + partial_value.shape[1:])[order_row]]
    ppermute x1, waiting for transfers between devices: 14.8 us -> 11.7 us  [output_grad(): return lax.ppermute(summed, ('hi', 'tp'), pairs)]
    unnamed x51 -> x49, local copies, waits for them, and re-layouts: 6.51 us -> 6.5 us
  transfers between devices with their start and end apart: 14 -> 15, of which waited for: 10 -> 11; matrix products, arithmetic and copies ran while one was open for 13% -> 14% of each run, Pallas kernels for 0% -> 0%
where the time goes in v8:
time: 304 us; the launch traced here: 300 us
  waiting for transfers between devices  78.1 us (26%)
  starting transfers between devices  61.5 us (20%)
  blocking collectives  57.9 us (19%)
  local copies, waits for them, and re-layouts  38.9 us (13%)
  matrix products  36.5 us (12%)
  between operations  15 us (5%)
  other arithmetic  12.3 us (4%)
    all_to_all x1, blocking collectives, output_grad(): lax.all_to_all(chunks, 'tp', split_axis=0, concat_axis=0, tiled=True)  30.6 us
    all_to_all x1, blocking collectives, body(): lax.all_to_all(grad_conv, SEQ, split_axis=1, concat_axis=0, tiled=True)  27.3 us
    all_gather x1, waiting for transfers between devices, output_grad(): token_rows = lax.all_gather(cotangent, 'hi', axis=0, tiled=True)  18 us
    ppermute x5, waiting for transfers between devices, butterfly_sum(): lax.ppermute(value, axis, [(i, i ^ stride) for i in range(devices)])  17.2 us
    ppermute x1, waiting for transfers between devices, output_grad(): return lax.ppermute(summed, ('hi', 'tp'), pairs)  11.7 us
    all_to_all x1, starting transfers between devices, body(): lax.all_to_all(long_filter.astype(jnp.bfloat16), SEQ, split_axis=1, conca...  11.6 us
    all_to_all x1, waiting for transfers between devices, body(): lax.all_to_all(conv_cols, SEQ, split_axis=0, concat_axis=1, tiled=True)  10.5 us
    all_to_all x1, starting transfers between devices, body(): lax.all_to_all(gated_input, SEQ, split_axis=1, concat_axis=0, tiled=True)  10 us
  transfers between devices with their start and end apart: 15, of which 11 were waited for; matrix products, arithmetic and copies ran while one was open for 14% of the time, Pallas kernels for 0%

profile of v8, /device:TPU:6, one launch (start us, length us, event | category | flops | bytes accessed | tf_op | source)
XLA Modules:
  0.0 300.2 jit_solution(10327809728073295713)
XLA Ops:
  9.8 11.6 %all-to-all-start.1 = ((bf16[128,32,32]{0,2,1:T(8,128)(2,1)}), bf16[128,32,32]{0,2,1:T(8,128)(2,1)S(1)}, u32[]{:S(2)}, u32[]{:S(2)}) async-start(bf16[128,32,32]{0,2,1:T(8,128)(2,1)} %bitcast.8), calls=%async_computation.1 | async-start | bytes 524288 | tf_op jit(solution)/shard_map/all_to_all | solution.py:171
  23.9 7.1 %collective-permute-done = bf16[6,3,1024]{2,0,1:T(8,128)(2,1)S(1)} collective-permute-done((bf16[6,3,1024]{2,0,1:T(8,128)(2,1)S(1)}, bf16[6,3,1024]{2,0,1:T(8,128)(2,1)S(1)}, u32[]{:S(2)}, u32[]{:S(2)}) %collective-permute-start) | collective-permute-done | bytes 36896 | tf_op jit(solution)/shard_map/ppermute | solution.py:15
  34.3 10.0 %all-to-all-start = ((bf16[128,32,32]{0,2,1:T(8,128)(2,1)}), bf16[128,32,32]{0,2,1:T(8,128)(2,1)S(1)}, u32[]{:S(2)}, u32[]{:S(2)}) async-start(bf16[128,32,32]{0,2,1:T(8,128)(2,1)} %bitcast.2), calls=%async_computation | async-start | bytes 524288 | tf_op jit(solution)/shard_map/all_to_all | solution.py:175
  50.3 5.8 %all-to-all-done = bf16[128,32,32]{0,2,1:T(8,128)(2,1)S(1)} async-done(((bf16[128,32,32]{0,2,1:T(8,128)(2,1)}), bf16[128,32,32]{0,2,1:T(8,128)(2,1)S(1)}, u32[]{:S(2)}, u32[]{:S(2)}) %all-to-all-start) | async-done | bytes 262176 | tf_op jit(solution)/shard_map/all_to_all | solution.py:175
  75.5 6.6 %all-to-all-start.2 = ((bf16[32,128,32]{1,2,0:T(8,128)(2,1)}), bf16[32,128,32]{1,2,0:T(8,128)(2,1)S(1)}, u32[]{:S(2)}, u32[]{:S(2)}) async-start(bf16[32,128,32]{1,2,0:T(8,128)(2,1)} %copy.52), calls=%async_computation.2 | async-start | bytes 524288 | tf_op jit(solution)/shard_map/all_to_all | solution.py:180
  83.4 10.5 %all-to-all-done.2 = bf16[32,128,32]{1,2,0:T(8,128)(2,1)S(1)} async-done(((bf16[32,128,32]{1,2,0:T(8,128)(2,1)}), bf16[32,128,32]{1,2,0:T(8,128)(2,1)S(1)}, u32[]{:S(2)}, u32[]{:S(2)}) %all-to-all-start.2) | async-done | bytes 262176 | tf_op jit(solution)/shard_map/all_to_all | solution.py:180
  93.9 18.0 %all-gather.5.cloned.1.call-done = bf16[1024,1024]{1,0:T(8,128)(2,1)} async-done(((bf16[128,1024]{1,0:T(8,128)(2,1)}), bf16[1024,1024]{1,0:T(8,128)(2,1)}) %all-gather.5.cloned.1.call-update) | async-done | bytes 2097168 | tf_op jit(solution)/shard_map/all_gather | solution.py:121
  111.9 5.9 %convolution_convert_fusion = bf16[1024,1024]{1,0:T(8,128)(2,1)} fusion(bf16[1024,1024]{1,0:T(8,128)(2,1)} %all-gather.5.cloned.1.call-done, bf16[1024,1024]{1,0:T(8,128)(2,1)} %all-gather.3.cloned.1.call-done), kind=kOutput, calls=%fused_computation.30 | convolution fusion | flops 2148532224 | bytes 6291456 | tf_op jit(solution)/shard_map/dot_general | solution.py:123
  117.9 3.7 %gather_fusion = bf16[8,128,1024]{2,1,0:T(8,128)(2,1)} fusion(bf16[8,128,1024]{2,1,0:T(8,128)(2,1)} %bitcast.206, s32[1024]{0:T(1024)} %pad_clamp_fusion), kind=kCustom, calls=%fused_computation | custom fusion | bytes 4194336 | tf_op jit(solution)/shard_map/gather | solution.py:133
  121.6 30.6 %all_to_all.86 = bf16[8,128,1024]{2,1,0:T(8,128)(2,1)} all-to-all(bf16[8,128,1024]{2,1,0:T(8,128)(2,1)} %gather_fusion), channel_id=1, replica_groups=mesh['hi'=8,'lo'=4,'tp'=8] {'tp'}, dimensions={0} | all-to-all | bytes 4194304 | tf_op jit(solution)/shard_map/all_to_all | solution.py:134
  152.2 2.7 reduce_sum.75
  154.9 5.1 %collective-permute-start.1 = (bf16[128,1024]{1,0:T(8,128)(2,1)}, bf16[128,1024]{1,0:T(8,128)(2,1)}, u32[]{:S(2)}, u32[]{:S(2)}) collective-permute-start(bf16[128,1024]{1,0:T(8,128)(2,1)} %reduce_sum.75), channel_id=1, source_target_pairs={{0,0},{1,192},{2,32},{3,128},{4,96},{5,160},{6,64},{7,224},{32,225... | collective-permute-start | bytes 786440 | tf_op jit(solution)/shard_map/ppermute | solution.py:141
  160.9 11.7 %collective-permute-done.1 = bf16[128,1024]{1,0:T(8,128)(2,1)} collective-permute-done((bf16[128,1024]{1,0:T(8,128)(2,1)}, bf16[128,1024]{1,0:T(8,128)(2,1)}, u32[]{:S(2)}, u32[]{:S(2)}) %collective-permute-start.1) | collective-permute-done | bytes 262176 | tf_op jit(solution)/shard_map/ppermute | solution.py:141
  176.3 27.3 %all_to_all.87 = bf16[128,32,32]{0,2,1:T(8,128)(2,1)} all-to-all(bf16[128,32,32]{0,2,1:T(8,128)(2,1)} %bitcast.216), channel_id=1, replica_groups=mesh['hi'=8,'lo'=4,'tp'=8] {'hi','lo'}, dimensions={1} | all-to-all | bytes 524288 | tf_op jit(solution)/shard_map/all_to_all | solution.py:184
  205.9 3.4 %reshape.176 = bf16[64,2048]{1,0:T(8,128)(2,1)} reshape(bf16[32,128,32]{2,1,0:T(8,128)(2,1)} %copy.55) | data formatting | bytes 524288 | tf_op jit(solution)/shard_map/reshape | solution.py:37
  230.6 6.7 %all-to-all-start.5 = ((bf16[32,128,32]{1,2,0:T(8,128)(2,1)}), bf16[32,128,32]{1,2,0:T(8,128)(2,1)S(1)}, u32[]{:S(2)}, u32[]{:S(2)}) async-start(bf16[32,128,32]{1,2,0:T(8,128)(2,1)} %copy.61), calls=%async_computation.5 | async-start | bytes 524288 | tf_op jit(solution)/shard_map/all_to_all | solution.py:190
  242.0 7.1 %all-to-all-done.5 = bf16[32,128,32]{1,2,0:T(8,128)(2,1)S(1)} async-done(((bf16[32,128,32]{1,2,0:T(8,128)(2,1)}), bf16[32,128,32]{1,2,0:T(8,128)(2,1)S(1)}, u32[]{:S(2)}, u32[]{:S(2)}) %all-to-all-start.5) | async-done | bytes 262176 | tf_op jit(solution)/shard_map/all_to_all | solution.py:190
  249.1 6.8 %all-to-all-start.6 = ((bf16[32,128,32]{1,2,0:T(8,128)(2,1)}), bf16[32,128,32]{1,2,0:T(8,128)(2,1)S(1)}, u32[]{:S(2)}, u32[]{:S(2)}) async-start(bf16[32,128,32]{1,2,0:T(8,128)(2,1)} %copy.66), calls=%async_computation.6 | async-start | bytes 524288 | tf_op jit(solution)/shard_map/all_to_all | solution.py:191
  261.9 4.6 %collective-permute-done.4 = f32[7,3,1024]{2,1,0:T(4,128)S(1)} collective-permute-done((f32[7,3,1024]{2,1,0:T(4,128)S(1)}, f32[7,3,1024]{2,1,0:T(4,128)S(1)}, u32[]{:S(2)}, u32[]{:S(2)}) %collective-permute-start.4) | collective-permute-done | bytes 86048 | tf_op jit(solution)/shard_map/ppermute | solution.py:148
  266.5 3.0 %collective-permute-start.5 = (f32[7,3,1024]{2,1,0:T(4,128)S(1)}, f32[7,3,1024]{2,1,0:T(4,128)S(1)}, u32[]{:S(2)}, u32[]{:S(2)}) collective-permute-start(f32[7,3,1024]{2,1,0:T(4,128)S(1)} %add.334), channel_id=1, source_target_pairs={{0,32},{8,40},{16,48},{24,56},{32,0},{40,8},{48,16},{56,24},{64,96... | collective-permute-start | bytes 258056 | tf_op jit(solution)/shard_map/ppermute | solution.py:148
  269.7 3.1 %collective-permute-start.2 = (bf16[6,3,1024]{2,0,1:T(8,128)(2,1)S(1)}, bf16[6,3,1024]{2,0,1:T(8,128)(2,1)S(1)}, u32[]{:S(2)}, u32[]{:S(2)}) collective-permute-start(bf16[6,3,1024]{2,0,1:T(8,128)(2,1)S(1)} %slice.124), channel_id=1, source_target_pairs={{8,0},{16,8},{24,16},{32,24},{40,32},{48,40},{56,48},{64,56},{72,6... | collective-permute-start | bytes 110600 | tf_op jit(solution)/shard_map/ppermute | solution.py:15
  275.2 4.1 %collective-permute-start.6 = (f32[7,3,1024]{2,1,0:T(4,128)S(1)}, f32[7,3,1024]{2,1,0:T(4,128)S(1)}, u32[]{:S(2)}, u32[]{:S(2)}) collective-permute-start(f32[7,3,1024]{2,1,0:T(4,128)S(1)} %add.335), channel_id=1, source_target_pairs={{0,64},{8,72},{16,80},{24,88},{32,96},{40,104},{48,112},{56,120},{... | collective-permute-start | bytes 258056 | tf_op jit(solution)/shard_map/ppermute | solution.py:148
  279.3 6.7 %collective-permute-done.6 = f32[7,3,1024]{2,1,0:T(4,128)S(1)} collective-permute-done((f32[7,3,1024]{2,1,0:T(4,128)S(1)}, f32[7,3,1024]{2,1,0:T(4,128)S(1)}, u32[]{:S(2)}, u32[]{:S(2)}) %collective-permute-start.6) | collective-permute-done | bytes 86048 | tf_op jit(solution)/shard_map/ppermute | solution.py:148
  289.0 3.4 %collective-permute-done.7 = f32[7,3,1024]{2,1,0:T(4,128)S(1)} collective-permute-done((f32[7,3,1024]{2,1,0:T(4,128)S(1)}, f32[7,3,1024]{2,1,0:T(4,128)S(1)}, u32[]{:S(2)}, u32[]{:S(2)}) %collective-permute-start.7) | collective-permute-done | bytes 86048 | tf_op jit(solution)/shard_map/ppermute | solution.py:148
  (145 shorter events, 79.5 us)
Async XLA Ops:
  7.2 14.3 %copy-start.4 = (bf16[128,3,1024]{2,0,1:T(8,128)(2,1)S(1)}, bf16[128,3,1024]{2,0,1:T(8,128)(2,1)}, u32[]{:S(2)}) copy-start(bf16[128,3,1024]{2,0,1:T(8,128)(2,1)} %param.6) | copy-start | bytes 2359300
  7.2 16.4 %copy-start.17 = (f32[7,3,1024]{2,0,1:T(8,128)S(1)}, f32[7,3,1024]{2,0,1:T(8,128)}, u32[]{:S(2)}) copy-start(f32[7,3,1024]{2,0,1:T(8,128)} %param.9) | copy-start | bytes 258052
  7.2 86.7 %all-gather.3.cloned.1.call-start = ((), (), s32[]{:S(2)}) async-start(), calls=%async_computation.7 | async-start | bytes 2621440 | tf_op jit(solution)/shard_map/all_gather | solution.py:120
  9.8 24.5 %all-to-all-start.1 = ((bf16[128,32,32]{0,2,1:T(8,128)(2,1)}), bf16[128,32,32]{0,2,1:T(8,128)(2,1)S(1)}, u32[]{:S(2)}, u32[]{:S(2)}) async-start(bf16[128,32,32]{0,2,1:T(8,128)(2,1)} %bitcast.8), calls=%async_computation.1 | async-start | bytes 524288 | tf_op jit(solution)/shard_map/all_to_all | solution.py:171
  21.4 90.5 %all-gather.5.cloned.1.call-start = ((), (), s32[]{:S(2)}) async-start(), calls=%async_computation.8 | async-start | bytes 2359296 | tf_op jit(solution)/shard_map/all_gather | solution.py:121
  21.5 9.5 %collective-permute-start = (bf16[6,3,1024]{2,0,1:T(8,128)(2,1)S(1)}, bf16[6,3,1024]{2,0,1:T(8,128)(2,1)S(1)}, u32[]{:S(2)}, u32[]{:S(2)}) collective-permute-start(bf16[6,3,1024]{2,0,1:T(8,128)(2,1)S(1)} %slice.87), channel_id=1, source_target_pairs={{0,8},{8,16},{16,24},{24,32},{32,40},{40,48},{48,56},{56,64},{64,7... | collective-permute-start | bytes 110600 | tf_op jit(solution)/shard_map/ppermute | solution.py:15
  23.7 10.6 %copy-start.7 = (f32[3,1024]{1,0:T(4,128)}, f32[3,1024]{1,0:T(4,128)S(1)}, u32[]{:S(2)}) copy-start(f32[3,1024]{1,0:T(4,128)S(1)} %get-tuple-element.56) | copy-start | bytes 36868
  34.3 21.8 %all-to-all-start = ((bf16[128,32,32]{0,2,1:T(8,128)(2,1)}), bf16[128,32,32]{0,2,1:T(8,128)(2,1)S(1)}, u32[]{:S(2)}, u32[]{:S(2)}) async-start(bf16[128,32,32]{0,2,1:T(8,128)(2,1)} %bitcast.2), calls=%async_computation | async-start | bytes 524288 | tf_op jit(solution)/shard_map/all_to_all | solution.py:175
  75.5 18.4 %all-to-all-start.2 = ((bf16[32,128,32]{1,2,0:T(8,128)(2,1)}), bf16[32,128,32]{1,2,0:T(8,128)(2,1)S(1)}, u32[]{:S(2)}, u32[]{:S(2)}) async-start(bf16[32,128,32]{1,2,0:T(8,128)(2,1)} %copy.52), calls=%async_computation.2 | async-start | bytes 524288 | tf_op jit(solution)/shard_map/all_to_all | solution.py:180
  154.9 17.6 %collective-permute-start.1 = (bf16[128,1024]{1,0:T(8,128)(2,1)}, bf16[128,1024]{1,0:T(8,128)(2,1)}, u32[]{:S(2)}, u32[]{:S(2)}) collective-permute-start(bf16[128,1024]{1,0:T(8,128)(2,1)} %reduce_sum.75), channel_id=1, source_target_pairs={{0,0},{1,192},{2,32},{3,128},{4,96},{5,160},{6,64},{7,224},{32,225... | collective-permute-start | bytes 786440 | tf_op jit(solution)/shard_map/ppermute | solution.py:141
  230.6 18.4 %all-to-all-start.5 = ((bf16[32,128,32]{1,2,0:T(8,128)(2,1)}), bf16[32,128,32]{1,2,0:T(8,128)(2,1)S(1)}, u32[]{:S(2)}, u32[]{:S(2)}) async-start(bf16[32,128,32]{1,2,0:T(8,128)(2,1)} %copy.61), calls=%async_computation.5 | async-start | bytes 524288 | tf_op jit(solution)/shard_map/all_to_all | solution.py:190
  241.0 15.2 %copy-start.1 = (bf16[128,3,1024]{2,0,1:T(8,128)(2,1)S(1)}, bf16[128,3,1024]{2,0,1:T(8,128)(2,1)}, u32[]{:S(2)}) copy-start(bf16[128,3,1024]{2,0,1:T(8,128)(2,1)} %copy-done) | copy-start | bytes 2359300
  249.1 23.7 %all-to-all-start.6 = ((bf16[32,128,32]{1,2,0:T(8,128)(2,1)}), bf16[32,128,32]{1,2,0:T(8,128)(2,1)S(1)}, u32[]{:S(2)}, u32[]{:S(2)}) async-start(bf16[32,128,32]{1,2,0:T(8,128)(2,1)} %copy.66), calls=%async_computation.6 | async-start | bytes 524288 | tf_op jit(solution)/shard_map/all_to_all | solution.py:191
  258.9 1.4 collective-permute-start.3
  260.3 6.2 %collective-permute-start.4 = (f32[7,3,1024]{2,1,0:T(4,128)S(1)}, f32[7,3,1024]{2,1,0:T(4,128)S(1)}, u32[]{:S(2)}, u32[]{:S(2)}) collective-permute-start(f32[7,3,1024]{2,1,0:T(4,128)S(1)} %add.333), channel_id=1, source_target_pairs={{0,16},{8,24},{16,0},{24,8},{32,48},{40,56},{48,32},{56,40},{64,80... | collective-permute-start | bytes 258056 | tf_op jit(solution)/shard_map/ppermute | solution.py:148
  266.5 8.6 %collective-permute-start.5 = (f32[7,3,1024]{2,1,0:T(4,128)S(1)}, f32[7,3,1024]{2,1,0:T(4,128)S(1)}, u32[]{:S(2)}, u32[]{:S(2)}) collective-permute-start(f32[7,3,1024]{2,1,0:T(4,128)S(1)} %add.334), channel_id=1, source_target_pairs={{0,32},{8,40},{16,48},{24,56},{32,0},{40,8},{48,16},{56,24},{64,96... | collective-permute-start | bytes 258056 | tf_op jit(solution)/shard_map/ppermute | solution.py:148
  269.7 9.6 %collective-permute-start.2 = (bf16[6,3,1024]{2,0,1:T(8,128)(2,1)S(1)}, bf16[6,3,1024]{2,0,1:T(8,128)(2,1)S(1)}, u32[]{:S(2)}, u32[]{:S(2)}) collective-permute-start(bf16[6,3,1024]{2,0,1:T(8,128)(2,1)S(1)} %slice.124), channel_id=1, source_target_pairs={{8,0},{16,8},{24,16},{32,24},{40,32},{48,40},{56,48},{64,56},{72,6... | collective-permute-start | bytes 110600 | tf_op jit(solution)/shard_map/ppermute | solution.py:15
  272.9 13.8 %copy-start.8 = (f32[3,1024]{1,0:T(4,128)S(1)}, f32[3,1024]{1,0:T(4,128)}, u32[]{:S(2)}) copy-start(f32[3,1024]{1,0:T(4,128)} %copy-done.7) | copy-start | bytes 36868
  272.9 13.8 %copy-start.10 = (f32[3,1024]{1,0:T(4,128)S(1)}, f32[3,1024]{1,0:T(4,128)}, u32[]{:S(2)}) copy-start(f32[3,1024]{1,0:T(4,128)} %copy-done.9) | copy-start | bytes 36868
  272.9 13.8 %copy-start.12 = (f32[3,1024]{1,0:T(4,128)S(1)}, f32[3,1024]{1,0:T(4,128)}, u32[]{:S(2)}) copy-start(f32[3,1024]{1,0:T(4,128)} %copy-done.11) | copy-start | bytes 36868
  272.9 13.8 %copy-start.14 = (f32[3,1024]{1,0:T(4,128)S(1)}, f32[3,1024]{1,0:T(4,128)}, u32[]{:S(2)}) copy-start(f32[3,1024]{1,0:T(4,128)} %copy-done.13) | copy-start | bytes 36868
  272.9 13.8 %copy-start.16 = (f32[1,3,1024]{2,1,0:T(4,128)S(1)}, f32[1,3,1024]{2,1,0:T(4,128)}, u32[]{:S(2)}) copy-start(f32[1,3,1024]{2,1,0:T(4,128)} %copy-done.15) | copy-start | bytes 36868
  275.2 10.9 %collective-permute-start.6 = (f32[7,3,1024]{2,1,0:T(4,128)S(1)}, f32[7,3,1024]{2,1,0:T(4,128)S(1)}, u32[]{:S(2)}, u32[]{:S(2)}) collective-permute-start(f32[7,3,1024]{2,1,0:T(4,128)S(1)} %add.335), channel_id=1, source_target_pairs={{0,64},{8,72},{16,80},{24,88},{32,96},{40,104},{48,112},{56,120},{... | collective-permute-start | bytes 258056 | tf_op jit(solution)/shard_map/ppermute | solution.py:148
  286.0 6.4 %collective-permute-start.7 = (f32[7,3,1024]{2,1,0:T(4,128)S(1)}, f32[7,3,1024]{2,1,0:T(4,128)S(1)}, u32[]{:S(2)}, u32[]{:S(2)}) collective-permute-start(f32[7,3,1024]{2,1,0:T(4,128)S(1)} %add.336), channel_id=1, source_target_pairs={{0,128},{8,136},{16,144},{24,152},{32,160},{40,168},{48,176},{56,1... | collective-permute-start | bytes 258056 | tf_op jit(solution)/shard_map/ppermute | solution.py:148
  (9 other events, 47.9 us)
Sparse Core Ops, SparseCore 0:
  9.8 36.7 all-gather.2
  49.2 62.6 all-gather.4

commit v9 on v6

--- a/solution.py
+++ b/solution.py
@@ -98,10 +98,7 @@
     return (left_array.astype(jnp.float32) * right_array.astype(jnp.float32)).astype(jnp.bfloat16)
 
 
-def output_grad(cotangent, out_weight, ready):
-    weight_rows = lax.all_gather(out_weight, "lo", axis=0, tiled=True)
-    token_rows = lax.all_gather(cotangent, "hi", axis=0, tiled=True)
-    weight_rows, token_rows, _ = lax.optimization_barrier((weight_rows, token_rows, ready))
+def reduced_block(token_rows, weight_rows):
     partial_value = lax.dot_general(
         token_rows,
         weight_rows,
@@ -111,7 +108,19 @@
     tp_parts = lax.axis_size("tp")
     chunks = partial_value.reshape((tp_parts, -1) + partial_value.shape[1:])
     received = lax.all_to_all(chunks, "tp", split_axis=0, concat_axis=0, tiled=True)
-    summed = jnp.sum(received.astype(jnp.float32), axis=0).astype(jnp.bfloat16)
+    return jnp.sum(received.astype(jnp.float32), axis=0).astype(jnp.bfloat16)
+
+
+def output_grad(cotangent, out_weight, ready):
+    half = cotangent.shape[0] // 2
+    weight_rows = lax.all_gather(out_weight, "lo", axis=0, tiled=True)
+    first_rows = lax.all_gather(cotangent[:half], "hi", axis=0, tiled=True)
+    second_rows = lax.all_gather(cotangent[half:], "hi", axis=0, tiled=True)
+    weight_rows, first_rows, ready = lax.optimization_barrier((weight_rows, first_rows, ready))
+    first_sum = reduced_block(first_rows, weight_rows)
+    second_rows, first_sum = lax.optimization_barrier((second_rows, first_sum))
+    second_sum = reduced_block(second_rows, weight_rows)
+    summed = jnp.concatenate([first_sum, second_sum], axis=0)
     hi_count = lax.axis_size("hi")
     tp_count = lax.axis_size("tp")
     pairs = [
@@ -119,7 +128,7 @@
         for row in range(hi_count)
         for col in range(tp_count)
     ]
-    return lax.ppermute(summed, ("hi", "tp"), pairs)
+    return lax.ppermute(summed, ("hi", "tp"), pairs), ready
 
 
 def butterfly_sum(value, axis):
@@ -159,7 +168,7 @@
         jnp.bfloat16
     )
     conv_out = lax.all_to_all(conv_cols, SEQ, split_axis=0, concat_axis=1, tiled=True)
-    grad_out = output_grad(cotangent, out_weight, conv_out)
+    grad_out, conv_out = output_grad(cotangent, out_weight, conv_out)
     grad_query = times_bf16(grad_out, conv_out)
     grad_conv = times_bf16(grad_out, query_conv)
     grad_cols = lax.all_to_all(grad_conv, SEQ, split_axis=1, concat_axis=0, tiled=True)

time: 300 us -> 342 us (1.14)
  waiting for transfers between devices: 71.8 us -> 100 us
  blocking collectives: 71.6 us -> 81 us
  other arithmetic: 11 us -> 15.2 us
  starting transfers between devices: 57.5 us -> 53.4 us
    all_gather x1 -> x2, waiting for transfers between devices: 19.2 us -> 31.1 us  [the longest x1 31.1 us: output_grad(): second_rows = lax.all_gather(cotangent[half:], 'hi', axis=0, tiled=True)]
    all_to_all x1, waiting for transfers between devices: 0.01 us -> 10.5 us  [body(): lax.all_to_all(long_filter.astype(jnp.bfloat16), SEQ, split_axis=1, conca...]
    all_to_all x1 -> x2, blocking collectives: 30.6 us -> 40.8 us  [reduced_block(): lax.all_to_all(chunks, 'tp', split_axis=0, concat_axis=0, tiled=True)]
    ppermute x2, waiting for transfers between devices: 7.1 us -> 0.01 us  [shifted(): return lax.ppermute(value, axis, pairs)]
    all_gather x1, waiting for transfers between devices: 0.01 us -> 6.41 us  [output_grad(): weight_rows = lax.all_gather(out_weight, 'lo', axis=0, tiled=True)]
    all_to_all x1, blocking collectives: 22.8 us -> 18.3 us  [body(): lax.all_to_all(grad_conv, SEQ, split_axis=1, concat_axis=0, tiled=True)]
    all_to_all x1, blocking collectives: 18.2 us -> 22 us  [body(): lax.all_to_all(conv_cols, SEQ, split_axis=0, concat_axis=1, tiled=True)]
    ppermute x1, waiting for transfers between devices: 14.8 us -> 18.4 us  [output_grad(): return (lax.ppermute(summed, ('hi', 'tp'), pairs), ready)]
  transfers between devices with their start and end apart: 14 -> 15, of which waited for: 10 -> 11; matrix products, arithmetic and copies ran while one was open for 13% -> 13% of each run, Pallas kernels for 0% -> 0%
where the time goes in v9:
time: 342 us; the launch traced here: 338 us
  waiting for transfers between devices  100 us (29%)
  blocking collectives  81 us (24%)
  starting transfers between devices  53.4 us (16%)
  matrix products  36.9 us (11%)
  local copies, waits for them, and re-layouts  36.3 us (11%)
  other arithmetic  15.2 us (4%)
  between operations  14.7 us (4%)
    all_to_all x2, blocking collectives, reduced_block(): lax.all_to_all(chunks, 'tp', split_axis=0, concat_axis=0, tiled=True)  40.8 us
    all_gather x1, waiting for transfers between devices, output_grad(): second_rows = lax.all_gather(cotangent[half:], 'hi', axis=0, tiled=True)  31.1 us
    all_to_all x1, blocking collectives, body(): lax.all_to_all(conv_cols, SEQ, split_axis=0, concat_axis=1, tiled=True)  22 us
    ppermute x1, waiting for transfers between devices, output_grad(): return (lax.ppermute(summed, ('hi', 'tp'), pairs), ready)  18.4 us
    all_to_all x1, blocking collectives, body(): lax.all_to_all(grad_conv, SEQ, split_axis=1, concat_axis=0, tiled=True)  18.3 us
    ppermute x5, waiting for transfers between devices, butterfly_sum(): lax.ppermute(value, axis, [(i, i ^ stride) for i in range(devices)])  18.2 us
    all_to_all x1, starting transfers between devices, body(): lax.all_to_all(long_filter.astype(jnp.bfloat16), SEQ, split_axis=1, conca...  12.3 us
    all_to_all x1, waiting for transfers between devices, body(): lax.all_to_all(long_filter.astype(jnp.bfloat16), SEQ, split_axis=1, conca...  10.5 us
  transfers between devices with their start and end apart: 15, of which 11 were waited for; matrix products, arithmetic and copies ran while one was open for 13% of the time, Pallas kernels for 0%

profile of v9, /device:TPU:6, one launch (start us, length us, event | category | flops | bytes accessed | tf_op | source)
XLA Modules:
  0.0 337.9 jit_solution(8249934291094460249)
XLA Ops:
  14.4 12.3 %all-to-all-start.1 = ((bf16[128,32,32]{0,2,1:T(8,128)(2,1)}), bf16[128,32,32]{0,2,1:T(8,128)(2,1)S(1)}, u32[]{:S(2)}, u32[]{:S(2)}) async-start(bf16[128,32,32]{0,2,1:T(8,128)(2,1)} %bitcast.8), calls=%async_computation.1 | async-start | bytes 524288 | tf_op jit(solution)/shard_map/all_to_all | solution.py:161
  31.2 10.5 %all-to-all-done.1 = bf16[128,32,32]{0,2,1:T(8,128)(2,1)S(1)} async-done(((bf16[128,32,32]{0,2,1:T(8,128)(2,1)}), bf16[128,32,32]{0,2,1:T(8,128)(2,1)S(1)}, u32[]{:S(2)}, u32[]{:S(2)}) %all-to-all-start.1) | async-done | bytes 262176 | tf_op jit(solution)/shard_map/all_to_all | solution.py:161
  41.6 7.1 %all-to-all-start = ((bf16[128,32,32]{0,2,1:T(8,128)(2,1)}), bf16[128,32,32]{0,2,1:T(8,128)(2,1)S(1)}, u32[]{:S(2)}, u32[]{:S(2)}) async-start(bf16[128,32,32]{0,2,1:T(8,128)(2,1)} %bitcast.2), calls=%async_computation | async-start | bytes 524288 | tf_op jit(solution)/shard_map/all_to_all | solution.py:165
  54.8 5.9 %all-to-all-done = bf16[128,32,32]{0,2,1:T(8,128)(2,1)S(1)} async-done(((bf16[128,32,32]{0,2,1:T(8,128)(2,1)}), bf16[128,32,32]{0,2,1:T(8,128)(2,1)S(1)}, u32[]{:S(2)}, u32[]{:S(2)}) %all-to-all-start) | async-done | bytes 262176 | tf_op jit(solution)/shard_map/all_to_all | solution.py:165
  79.3 22.0 %all_to_all.91 = bf16[32,128,32]{1,2,0:T(8,128)(2,1)} all-to-all(bf16[32,128,32]{1,2,0:T(8,128)(2,1)S(1)} %copy.51), channel_id=1, replica_groups=mesh['hi'=8,'lo'=4,'tp'=8] {'hi','lo'}, dimensions={0} | all-to-all | bytes 524288 | tf_op jit(solution)/shard_map/all_to_all | solution.py:170
  101.3 6.4 %all-gather.6.cloned.1.call-done = bf16[1024,1024]{1,0:T(8,128)(2,1)} async-done(((bf16[256,1024]{1,0:T(8,128)(2,1)}), bf16[1024,1024]{1,0:T(8,128)(2,1)}) %all-gather.6.cloned.1.call-update) | async-done | bytes 2097168 | tf_op jit(solution)/shard_map/all_gather | solution.py:116
  107.7 3.2 convolution_convert_fusion.1
  110.9 22.0 %all_to_all.92 = bf16[8,64,1024]{2,1,0:T(8,128)(2,1)} all-to-all(bf16[8,64,1024]{2,1,0:T(8,128)(2,1)S(1)} %bitcast.214), channel_id=1, replica_groups=mesh['hi'=8,'lo'=4,'tp'=8] {'tp'}, dimensions={0} | all-to-all | bytes 2097152 | tf_op jit(solution)/shard_map/all_to_all | solution.py:110
  135.0 31.1 %all-gather.4.cloned.1.call-done = bf16[512,1024]{1,0:T(8,128)(2,1)} async-done(((bf16[64,1024]{1,0:T(8,128)(2,1)}), bf16[512,1024]{1,0:T(8,128)(2,1)}) %all-gather.4.cloned.1.call-update) | async-done | bytes 1048592 | tf_op jit(solution)/shard_map/all_gather | solution.py:118
  166.1 3.2 convolution_convert_fusion
  169.3 18.8 %all_to_all.93 = bf16[8,64,1024]{2,1,0:T(8,128)(2,1)} all-to-all(bf16[8,64,1024]{2,1,0:T(8,128)(2,1)S(1)} %bitcast.213), channel_id=1, replica_groups=mesh['hi'=8,'lo'=4,'tp'=8] {'tp'}, dimensions={0} | all-to-all | bytes 2097152 | tf_op jit(solution)/shard_map/all_to_all | solution.py:110
  191.9 5.6 %collective-permute-start.1 = (bf16[128,1024]{1,0:T(8,128)(2,1)}, bf16[128,1024]{1,0:T(8,128)(2,1)}, u32[]{:S(2)}, u32[]{:S(2)}) collective-permute-start(bf16[128,1024]{1,0:T(8,128)(2,1)} %pad_maximum_fusion.3), channel_id=1, source_target_pairs={{0,0},{1,32},{2,64},{3,96},{4,128},{5,160},{6,192},{7,224},{32,1},... | collective-permute-start | bytes 786440 | tf_op jit(solution)/shard_map/ppermute | solution.py:131
  198.3 18.4 %collective-permute-done.1 = bf16[128,1024]{1,0:T(8,128)(2,1)} collective-permute-done((bf16[128,1024]{1,0:T(8,128)(2,1)}, bf16[128,1024]{1,0:T(8,128)(2,1)}, u32[]{:S(2)}, u32[]{:S(2)}) %collective-permute-start.1) | collective-permute-done | bytes 262176 | tf_op jit(solution)/shard_map/ppermute | solution.py:131
  220.5 18.3 %all_to_all.94 = bf16[128,32,32]{0,2,1:T(8,128)(2,1)} all-to-all(bf16[128,32,32]{0,2,1:T(8,128)(2,1)} %bitcast.216), channel_id=1, replica_groups=mesh['hi'=8,'lo'=4,'tp'=8] {'hi','lo'}, dimensions={1} | all-to-all | bytes 524288 | tf_op jit(solution)/shard_map/all_to_all | solution.py:174
  241.1 3.4 reshape.152
  267.0 7.4 %all-to-all-start.6 = ((bf16[32,128,32]{1,2,0:T(8,128)(2,1)}), bf16[32,128,32]{1,2,0:T(8,128)(2,1)}, u32[]{:S(2)}, u32[]{:S(2)}) async-start(bf16[32,128,32]{1,2,0:T(8,128)(2,1)} %copy.60), calls=%async_computation.6 | async-start | bytes 524288 | tf_op jit(solution)/shard_map/all_to_all | solution.py:180
  277.8 8.3 %all-to-all-done.6 = bf16[32,128,32]{1,2,0:T(8,128)(2,1)} async-done(((bf16[32,128,32]{1,2,0:T(8,128)(2,1)}), bf16[32,128,32]{1,2,0:T(8,128)(2,1)}, u32[]{:S(2)}, u32[]{:S(2)}) %all-to-all-start.6) | async-done | bytes 262176 | tf_op jit(solution)/shard_map/all_to_all | solution.py:180
  286.2 6.8 %all-to-all-start.7 = ((bf16[32,128,32]{1,2,0:T(8,128)(2,1)}), bf16[32,128,32]{1,2,0:T(8,128)(2,1)S(1)}, u32[]{:S(2)}, u32[]{:S(2)}) async-start(bf16[32,128,32]{1,2,0:T(8,128)(2,1)} %copy.65), calls=%async_computation.7 | async-start | bytes 524288 | tf_op jit(solution)/shard_map/all_to_all | solution.py:181
  299.3 4.3 %collective-permute-done.4 = f32[7,3,1024]{2,1,0:T(4,128)S(1)} collective-permute-done((f32[7,3,1024]{2,1,0:T(4,128)S(1)}, f32[7,3,1024]{2,1,0:T(4,128)S(1)}, u32[]{:S(2)}, u32[]{:S(2)}) %collective-permute-start.4) | collective-permute-done | bytes 86048 | tf_op jit(solution)/shard_map/ppermute | solution.py:138
  303.6 3.3 collective-permute-start.5
  307.0 2.8 collective-permute-start.2
  312.5 3.9 %collective-permute-start.6 = (f32[7,3,1024]{2,1,0:T(4,128)S(1)}, f32[7,3,1024]{2,1,0:T(4,128)S(1)}, u32[]{:S(2)}, u32[]{:S(2)}) collective-permute-start(f32[7,3,1024]{2,1,0:T(4,128)S(1)} %add.320), channel_id=1, source_target_pairs={{0,64},{8,72},{16,80},{24,88},{32,96},{40,104},{48,112},{56,120},{... | collective-permute-start | bytes 258056 | tf_op jit(solution)/shard_map/ppermute | solution.py:138
  316.5 7.3 %collective-permute-done.6 = f32[7,3,1024]{2,1,0:T(4,128)S(1)} collective-permute-done((f32[7,3,1024]{2,1,0:T(4,128)S(1)}, f32[7,3,1024]{2,1,0:T(4,128)S(1)}, u32[]{:S(2)}, u32[]{:S(2)}) %collective-permute-start.6) | collective-permute-done | bytes 86048 | tf_op jit(solution)/shard_map/ppermute | solution.py:138
  326.6 3.9 %collective-permute-done.7 = f32[7,3,1024]{2,1,0:T(4,128)S(1)} collective-permute-done((f32[7,3,1024]{2,1,0:T(4,128)S(1)}, f32[7,3,1024]{2,1,0:T(4,128)S(1)}, u32[]{:S(2)}, u32[]{:S(2)}) %collective-permute-start.7) | collective-permute-done | bytes 86048 | tf_op jit(solution)/shard_map/ppermute | solution.py:138
  (151 shorter events, 87.1 us)
Async XLA Ops:
  7.2 20.7 %copy-start.4 = (bf16[128,3,1024]{2,0,1:T(8,128)(2,1)S(1)}, bf16[128,3,1024]{2,0,1:T(8,128)(2,1)}, u32[]{:S(2)}) copy-start(bf16[128,3,1024]{2,0,1:T(8,128)(2,1)} %param.5) | copy-start | bytes 2359300
  7.2 20.3 %copy-start.18 = (f32[7,3,1024]{2,0,1:T(8,128)S(1)}, f32[7,3,1024]{2,0,1:T(8,128)}, u32[]{:S(2)}) copy-start(f32[7,3,1024]{2,0,1:T(8,128)} %param.8) | copy-start | bytes 258052
  7.2 94.1 %all-gather.8.cloned.1.call-start = ((), (), s32[]{:S(2)}) async-start(), calls=%async_computation.10 | async-start | bytes 1179648 | tf_op jit(solution)/shard_map/all_gather | solution.py:117
  9.0 98.7 %all-gather.6.cloned.1.call-start = ((), (), s32[]{:S(2)}) async-start(), calls=%async_computation.9 | async-start | bytes 2621440 | tf_op jit(solution)/shard_map/all_gather | solution.py:116
  10.6 17.2 %collective-permute-start = (bf16[6,3,1024]{2,0,1:T(8,128)(2,1)S(1)}, bf16[6,3,1024]{2,0,1:T(8,128)(2,1)S(1)}, u32[]{:S(2)}, u32[]{:S(2)}) collective-permute-start(bf16[6,3,1024]{2,0,1:T(8,128)(2,1)S(1)} %slice.95), channel_id=1, source_target_pairs={{0,8},{8,16},{16,24},{24,32},{32,40},{40,48},{48,56},{56,64},{64,7... | collective-permute-start | bytes 110600 | tf_op jit(solution)/shard_map/ppermute | solution.py:15
  14.4 27.2 %all-to-all-start.1 = ((bf16[128,32,32]{0,2,1:T(8,128)(2,1)}), bf16[128,32,32]{0,2,1:T(8,128)(2,1)S(1)}, u32[]{:S(2)}, u32[]{:S(2)}) async-start(bf16[128,32,32]{0,2,1:T(8,128)(2,1)} %bitcast.8), calls=%async_computation.1 | async-start | bytes 524288 | tf_op jit(solution)/shard_map/all_to_all | solution.py:161
  26.7 139.4 %all-gather.4.cloned.1.call-start = ((), (), s32[]{:S(2)}) async-start(), calls=%async_computation.8 | async-start | bytes 1179648 | tf_op jit(solution)/shard_map/all_gather | solution.py:118
  41.6 19.0 %all-to-all-start = ((bf16[128,32,32]{0,2,1:T(8,128)(2,1)}), bf16[128,32,32]{0,2,1:T(8,128)(2,1)S(1)}, u32[]{:S(2)}, u32[]{:S(2)}) async-start(bf16[128,32,32]{0,2,1:T(8,128)(2,1)} %bitcast.2), calls=%async_computation | async-start | bytes 524288 | tf_op jit(solution)/shard_map/all_to_all | solution.py:165
  169.3 28.2 %copy-start.7 = (bf16[32,128,32]{1,2,0:T(8,128)(2,1)S(1)}, bf16[32,128,32]{1,2,0:T(8,128)(2,1)}, u32[]{:S(2)}) copy-start(bf16[32,128,32]{1,2,0:T(8,128)(2,1)} %all_to_all.91) | copy-start | bytes 786436
  191.9 24.9 %collective-permute-start.1 = (bf16[128,1024]{1,0:T(8,128)(2,1)}, bf16[128,1024]{1,0:T(8,128)(2,1)}, u32[]{:S(2)}, u32[]{:S(2)}) collective-permute-start(bf16[128,1024]{1,0:T(8,128)(2,1)} %pad_maximum_fusion.3), channel_id=1, source_target_pairs={{0,0},{1,32},{2,64},{3,96},{4,128},{5,160},{6,192},{7,224},{32,1},... | collective-permute-start | bytes 786440 | tf_op jit(solution)/shard_map/ppermute | solution.py:131
  267.0 19.1 %all-to-all-start.6 = ((bf16[32,128,32]{1,2,0:T(8,128)(2,1)}), bf16[32,128,32]{1,2,0:T(8,128)(2,1)}, u32[]{:S(2)}, u32[]{:S(2)}) async-start(bf16[32,128,32]{1,2,0:T(8,128)(2,1)} %copy.60), calls=%async_computation.6 | async-start | bytes 524288 | tf_op jit(solution)/shard_map/all_to_all | solution.py:180
  276.8 17.5 %copy-start.1 = (bf16[128,3,1024]{2,0,1:T(8,128)(2,1)S(1)}, bf16[128,3,1024]{2,0,1:T(8,128)(2,1)}, u32[]{:S(2)}) copy-start(bf16[128,3,1024]{2,0,1:T(8,128)(2,1)} %copy-done) | copy-start | bytes 2359300
  286.2 23.7 %all-to-all-start.7 = ((bf16[32,128,32]{1,2,0:T(8,128)(2,1)}), bf16[32,128,32]{1,2,0:T(8,128)(2,1)S(1)}, u32[]{:S(2)}, u32[]{:S(2)}) async-start(bf16[32,128,32]{1,2,0:T(8,128)(2,1)} %copy.65), calls=%async_computation.7 | async-start | bytes 524288 | tf_op jit(solution)/shard_map/all_to_all | solution.py:181
  296.3 1.4 collective-permute-start.3
  297.7 5.9 %collective-permute-start.4 = (f32[7,3,1024]{2,1,0:T(4,128)S(1)}, f32[7,3,1024]{2,1,0:T(4,128)S(1)}, u32[]{:S(2)}, u32[]{:S(2)}) collective-permute-start(f32[7,3,1024]{2,1,0:T(4,128)S(1)} %add.318), channel_id=1, source_target_pairs={{0,16},{8,24},{16,0},{24,8},{32,48},{40,56},{48,32},{56,40},{64,80... | collective-permute-start | bytes 258056 | tf_op jit(solution)/shard_map/ppermute | solution.py:138
  303.6 8.9 %collective-permute-start.5 = (f32[7,3,1024]{2,1,0:T(4,128)S(1)}, f32[7,3,1024]{2,1,0:T(4,128)S(1)}, u32[]{:S(2)}, u32[]{:S(2)}) collective-permute-start(f32[7,3,1024]{2,1,0:T(4,128)S(1)} %add.319), channel_id=1, source_target_pairs={{0,32},{8,40},{16,48},{24,56},{32,0},{40,8},{48,16},{56,24},{64,96... | collective-permute-start | bytes 258056 | tf_op jit(solution)/shard_map/ppermute | solution.py:138
  307.0 9.4 %collective-permute-start.2 = (bf16[6,3,1024]{2,0,1:T(8,128)(2,1)S(1)}, bf16[6,3,1024]{2,0,1:T(8,128)(2,1)S(1)}, u32[]{:S(2)}, u32[]{:S(2)}) collective-permute-start(bf16[6,3,1024]{2,0,1:T(8,128)(2,1)S(1)} %slice.130), channel_id=1, source_target_pairs={{8,0},{16,8},{24,16},{32,24},{40,32},{48,40},{56,48},{64,56},{72,6... | collective-permute-start | bytes 110600 | tf_op jit(solution)/shard_map/ppermute | solution.py:15
  309.9 14.4 %copy-start.9 = (f32[3,1024]{1,0:T(4,128)S(1)}, f32[3,1024]{1,0:T(4,128)}, u32[]{:S(2)}) copy-start(f32[3,1024]{1,0:T(4,128)} %copy-done.8) | copy-start | bytes 36868
  309.9 14.4 %copy-start.11 = (f32[3,1024]{1,0:T(4,128)S(1)}, f32[3,1024]{1,0:T(4,128)}, u32[]{:S(2)}) copy-start(f32[3,1024]{1,0:T(4,128)} %copy-done.10) | copy-start | bytes 36868
  309.9 14.4 %copy-start.13 = (f32[3,1024]{1,0:T(4,128)S(1)}, f32[3,1024]{1,0:T(4,128)}, u32[]{:S(2)}) copy-start(f32[3,1024]{1,0:T(4,128)} %copy-done.12) | copy-start | bytes 36868
  309.9 14.3 %copy-start.15 = (f32[3,1024]{1,0:T(4,128)S(1)}, f32[3,1024]{1,0:T(4,128)}, u32[]{:S(2)}) copy-start(f32[3,1024]{1,0:T(4,128)} %copy-done.14) | copy-start | bytes 36868
  309.9 14.3 %copy-start.17 = (f32[1,3,1024]{2,1,0:T(4,128)S(1)}, f32[1,3,1024]{2,1,0:T(4,128)}, u32[]{:S(2)}) copy-start(f32[1,3,1024]{2,1,0:T(4,128)} %copy-done.16) | copy-start | bytes 36868
  312.5 11.2 %collective-permute-start.6 = (f32[7,3,1024]{2,1,0:T(4,128)S(1)}, f32[7,3,1024]{2,1,0:T(4,128)S(1)}, u32[]{:S(2)}, u32[]{:S(2)}) collective-permute-start(f32[7,3,1024]{2,1,0:T(4,128)S(1)} %add.320), channel_id=1, source_target_pairs={{0,64},{8,72},{16,80},{24,88},{32,96},{40,104},{48,112},{56,120},{... | collective-permute-start | bytes 258056 | tf_op jit(solution)/shard_map/ppermute | solution.py:138
  323.8 6.6 %collective-permute-start.7 = (f32[7,3,1024]{2,1,0:T(4,128)S(1)}, f32[7,3,1024]{2,1,0:T(4,128)S(1)}, u32[]{:S(2)}, u32[]{:S(2)}) collective-permute-start(f32[7,3,1024]{2,1,0:T(4,128)S(1)} %add.321), channel_id=1, source_target_pairs={{0,128},{8,136},{16,144},{24,152},{32,160},{40,168},{48,176},{56,1... | collective-permute-start | bytes 258056 | tf_op jit(solution)/shard_map/ppermute | solution.py:138
  (10 other events, 34.0 us)
Sparse Core Ops, SparseCore 0:
  10.6 59.3 all-gather.7
  71.9 35.7 all-gather.5
  110.3 55.7 all-gather.3

commit v10 on v7

--- a/solution.py
+++ b/solution.py
@@ -126,7 +126,10 @@
     devices = lax.axis_size(axis)
     stride = 1
     while stride < devices:
-        value = value + lax.ppermute(value, axis, [(i, i ^ stride) for i in range(devices)])
+        sent = value.astype(jnp.bfloat16)
+        value = sent.astype(jnp.float32) + lax.ppermute(
+            sent, axis, [(i, i ^ stride) for i in range(devices)]
+        ).astype(jnp.float32)
         stride *= 2
     return value
 

time: 301 us -> 300 us (level)
    ppermute x5, waiting for transfers between devices: 17.2 us -> 13.8 us  [butterfly_sum(): lax.ppermute(sent, axis, [(i, i ^ stride) for i in range(devices)])]
    unnamed x51 -> x53, local copies, waits for them, and re-layouts: 6.76 us -> 6.08 us
  transfers between devices with their start and end apart: 14 -> 14, of which waited for: 10 -> 9; matrix products, arithmetic and copies ran while one was open for 11% -> 11% of each run, Pallas kernels for 0% -> 0%
where the time goes in v10:
time: 300 us; the launch traced here: 297 us
  waiting for transfers between devices  88.7 us (30%)
  blocking collectives  70.4 us (23%)
  starting transfers between devices  56.1 us (19%)
  local copies, waits for them, and re-layouts  31.6 us (11%)
  matrix products  24 us (8%)
  between operations  15.2 us (5%)
  other arithmetic  11.1 us (4%)
    all_to_all x1, blocking collectives, output_grad(): lax.all_to_all(chunks, 'tp', split_axis=0, concat_axis=0, tiled=True)  30.6 us
    all_gather x1, waiting for transfers between devices, output_grad(): token_rows = lax.all_gather(cotangent, 'hi', axis=0, tiled=True)  28.1 us
    all_to_all x1, blocking collectives, body(): lax.all_to_all(grad_conv, SEQ, split_axis=1, concat_axis=0, tiled=True)  20.8 us
    all_to_all x1, blocking collectives, body(): lax.all_to_all(conv_cols, SEQ, split_axis=0, concat_axis=1, tiled=True)  18.9 us
    ppermute x1, waiting for transfers between devices, output_grad(): return lax.ppermute(summed, ('hi', 'tp'), pairs)  17.3 us
    ppermute x5, waiting for transfers between devices, butterfly_sum(): lax.ppermute(sent, axis, [(i, i ^ stride) for i in range(devices)])  13.8 us
    all_to_all x1, starting transfers between devices, body(): lax.all_to_all(long_filter.astype(jnp.bfloat16), SEQ, split_axis=1, conca...  12.3 us
    all_to_all x1, waiting for transfers between devices, body(): lax.all_to_all(gated_grad_cols, SEQ, split_axis=0, concat_axis=1, tiled=T...  9.71 us
  transfers between devices with their start and end apart: 14, of which 9 were waited for; matrix products, arithmetic and copies ran while one was open for 11% of the time, Pallas kernels for 0%

profile of v10, /device:TPU:6, one launch (start us, length us, event | category | flops | bytes accessed | tf_op | source)
XLA Modules:
  0.0 297.1 jit_solution(17379013713951476613)
XLA Ops:
  12.6 12.3 %all-to-all-start.1 = ((bf16[128,32,32]{0,2,1:T(8,128)(2,1)}), bf16[128,32,32]{0,2,1:T(8,128)(2,1)S(1)}, u32[]{:S(2)}, u32[]{:S(2)}) async-start(bf16[128,32,32]{0,2,1:T(8,128)(2,1)} %bitcast.8), calls=%async_computation.1 | async-start | bytes 524288 | tf_op jit(solution)/shard_map/all_to_all | solution.py:155
  29.3 9.2 %all-to-all-done.1 = bf16[128,32,32]{0,2,1:T(8,128)(2,1)S(1)} async-done(((bf16[128,32,32]{0,2,1:T(8,128)(2,1)}), bf16[128,32,32]{0,2,1:T(8,128)(2,1)S(1)}, u32[]{:S(2)}, u32[]{:S(2)}) %all-to-all-start.1) | async-done | bytes 262176 | tf_op jit(solution)/shard_map/all_to_all | solution.py:155
  38.5 7.5 %all-to-all-start = ((bf16[128,32,32]{0,2,1:T(8,128)(2,1)}), bf16[128,32,32]{0,2,1:T(8,128)(2,1)S(1)}, u32[]{:S(2)}, u32[]{:S(2)}) async-start(bf16[128,32,32]{0,2,1:T(8,128)(2,1)} %bitcast.2), calls=%async_computation | async-start | bytes 524288 | tf_op jit(solution)/shard_map/all_to_all | solution.py:159
  50.6 8.5 %all-to-all-done = bf16[128,32,32]{0,2,1:T(8,128)(2,1)S(1)} async-done(((bf16[128,32,32]{0,2,1:T(8,128)(2,1)}), bf16[128,32,32]{0,2,1:T(8,128)(2,1)S(1)}, u32[]{:S(2)}, u32[]{:S(2)}) %all-to-all-start) | async-done | bytes 262176 | tf_op jit(solution)/shard_map/all_to_all | solution.py:159
  73.2 18.9 %all_to_all.86 = bf16[32,128,32]{1,2,0:T(8,128)(2,1)} all-to-all(bf16[32,128,32]{1,2,0:T(8,128)(2,1)S(1)} %copy.51), channel_id=1, replica_groups=mesh['hi'=8,'lo'=4,'tp'=8] {'hi','lo'}, dimensions={0} | all-to-all | bytes 524288 | tf_op jit(solution)/shard_map/all_to_all | solution.py:164
  92.1 28.1 %all-gather.5.cloned.1.call-done = bf16[1024,1024]{1,0:T(8,128)(2,1)} async-done(((bf16[128,1024]{1,0:T(8,128)(2,1)}), bf16[1024,1024]{1,0:T(8,128)(2,1)}) %all-gather.5.cloned.1.call-update) | async-done | bytes 2097168 | tf_op jit(solution)/shard_map/all_gather | solution.py:103
  120.2 4.6 %convolution_convert_fusion = bf16[1024,1024]{1,0:T(8,128)(2,1)S(1)} fusion(bf16[1024,1024]{1,0:T(8,128)(2,1)} %all-gather.5.cloned.1.call-done, bf16[1024,1024]{1,0:T(8,128)(2,1)} %all-gather.3.cloned.1.call-done), kind=kOutput, calls=%fused_computation.29 | convolution fusion | flops 2148532224 | bytes 6291456 | tf_op jit(solution)/shard_map/dot_general | solution.py:105
  124.8 30.6 %all_to_all.87 = bf16[8,128,1024]{2,1,0:T(8,128)(2,1)} all-to-all(bf16[8,128,1024]{2,1,0:T(8,128)(2,1)S(1)} %bitcast.196), channel_id=1, replica_groups=mesh['hi'=8,'lo'=4,'tp'=8] {'tp'}, dimensions={0} | all-to-all | bytes 4194304 | tf_op jit(solution)/shard_map/all_to_all | solution.py:113
  155.4 2.8 reduce_sum.75
  158.2 7.8 %collective-permute-start.1 = (bf16[128,1024]{1,0:T(8,128)(2,1)}, bf16[128,1024]{1,0:T(8,128)(2,1)}, u32[]{:S(2)}, u32[]{:S(2)}) collective-permute-start(bf16[128,1024]{1,0:T(8,128)(2,1)} %reduce_sum.75), channel_id=1, source_target_pairs={{0,0},{1,32},{2,64},{3,96},{4,128},{5,160},{6,192},{7,224},{32,1},... | collective-permute-start | bytes 786440 | tf_op jit(solution)/shard_map/ppermute | solution.py:122
  166.8 17.3 %collective-permute-done.1 = bf16[128,1024]{1,0:T(8,128)(2,1)} collective-permute-done((bf16[128,1024]{1,0:T(8,128)(2,1)}, bf16[128,1024]{1,0:T(8,128)(2,1)}, u32[]{:S(2)}, u32[]{:S(2)}) %collective-permute-start.1) | collective-permute-done | bytes 262176 | tf_op jit(solution)/shard_map/ppermute | solution.py:122
  184.2 2.0 fusion.76
  187.9 20.8 %all_to_all.88 = bf16[128,32,32]{0,2,1:T(8,128)(2,1)} all-to-all(bf16[128,32,32]{0,2,1:T(8,128)(2,1)} %bitcast.212), channel_id=1, replica_groups=mesh['hi'=8,'lo'=4,'tp'=8] {'hi','lo'}, dimensions={1} | all-to-all | bytes 524288 | tf_op jit(solution)/shard_map/all_to_all | solution.py:168
  208.8 2.3 copy.54
  211.0 3.0 %reshape.148 = bf16[64,2048]{1,0:T(8,128)(2,1)} reshape(bf16[32,128,32]{2,1,0:T(8,128)(2,1)} %copy.54) | data formatting | bytes 524288 | tf_op jit(solution)/shard_map/reshape | solution.py:37
  228.1 7.1 %all-to-all-start.5 = ((bf16[32,128,32]{1,2,0:T(8,128)(2,1)}), bf16[32,128,32]{1,2,0:T(8,128)(2,1)S(1)}, u32[]{:S(2)}, u32[]{:S(2)}) async-start(bf16[32,128,32]{1,2,0:T(8,128)(2,1)} %copy.60), calls=%async_computation.5 | async-start | bytes 524288 | tf_op jit(solution)/shard_map/all_to_all | solution.py:174
  237.1 9.7 %all-to-all-done.5 = bf16[32,128,32]{1,2,0:T(8,128)(2,1)S(1)} async-done(((bf16[32,128,32]{1,2,0:T(8,128)(2,1)}), bf16[32,128,32]{1,2,0:T(8,128)(2,1)S(1)}, u32[]{:S(2)}, u32[]{:S(2)}) %all-to-all-start.5) | async-done | bytes 262176 | tf_op jit(solution)/shard_map/all_to_all | solution.py:174
  251.4 6.8 %all-to-all-start.6 = ((bf16[32,128,32]{1,2,0:T(8,128)(2,1)}), bf16[32,128,32]{1,2,0:T(8,128)(2,1)S(1)}, u32[]{:S(2)}, u32[]{:S(2)}) async-start(bf16[32,128,32]{1,2,0:T(8,128)(2,1)} %copy.65), calls=%async_computation.6 | async-start | bytes 524288 | tf_op jit(solution)/shard_map/all_to_all | solution.py:175
  259.8 7.8 %collective-permute-done.4 = bf16[7,3,1024]{2,1,0:T(4,128)(2,1)S(1)} collective-permute-done((bf16[7,3,1024]{2,1,0:T(4,128)(2,1)S(1)}, bf16[7,3,1024]{2,1,0:T(4,128)(2,1)S(1)}, u32[]{:S(2)}, u32[]{:S(2)}) %collective-permute-start.4) | collective-permute-done | bytes 43040 | tf_op jit(solution)/shard_map/ppermute | solution.py:130
  271.2 3.8 %collective-permute-start.2 = (bf16[6,3,1024]{2,0,1:T(8,128)(2,1)S(1)}, bf16[6,3,1024]{2,0,1:T(8,128)(2,1)S(1)}, u32[]{:S(2)}, u32[]{:S(2)}) collective-permute-start(bf16[6,3,1024]{2,0,1:T(8,128)(2,1)S(1)} %slice.122), channel_id=1, source_target_pairs={{8,0},{16,8},{24,16},{32,24},{40,32},{48,40},{56,48},{64,56},{72,6... | collective-permute-start | bytes 110600 | tf_op jit(solution)/shard_map/ppermute | solution.py:15
  275.1 3.5 %collective-permute-start.6 = (bf16[7,3,1024]{2,1,0:T(4,128)(2,1)S(1)}, bf16[7,3,1024]{2,1,0:T(4,128)(2,1)S(1)}, u32[]{:S(2)}, u32[]{:S(2)}) collective-permute-start(bf16[7,3,1024]{2,1,0:T(4,128)(2,1)S(1)} %add_convert_fusion.1), channel_id=1, source_target_pairs={{0,64},{8,72},{16,80},{24,88},{32,96},{40,104},{48,112},{56,120},{... | collective-permute-start | bytes 129032 | tf_op jit(solution)/shard_map/ppermute | solution.py:130
  278.6 4.7 %collective-permute-done.6 = bf16[7,3,1024]{2,1,0:T(4,128)(2,1)S(1)} collective-permute-done((bf16[7,3,1024]{2,1,0:T(4,128)(2,1)S(1)}, bf16[7,3,1024]{2,1,0:T(4,128)(2,1)S(1)}, u32[]{:S(2)}, u32[]{:S(2)}) %collective-permute-start.6) | collective-permute-done | bytes 43040 | tf_op jit(solution)/shard_map/ppermute | solution.py:130
  283.3 2.1 collective-permute-start.7
  285.5 2.3 fusion.19
  (145 shorter events, 58.5 us)
Async XLA Ops:
  7.2 18.8 %copy-start.4 = (bf16[128,3,1024]{2,0,1:T(8,128)(2,1)S(1)}, bf16[128,3,1024]{2,0,1:T(8,128)(2,1)}, u32[]{:S(2)}) copy-start(bf16[128,3,1024]{2,0,1:T(8,128)(2,1)} %param.5) | copy-start | bytes 2359300
  7.2 18.5 %copy-start.19 = (f32[7,3,1024]{2,0,1:T(8,128)S(1)}, f32[7,3,1024]{2,0,1:T(8,128)}, u32[]{:S(2)}) copy-start(f32[7,3,1024]{2,0,1:T(8,128)} %param.8) | copy-start | bytes 258052
  7.2 84.9 %all-gather.3.cloned.1.call-start = ((), (), s32[]{:S(2)}) async-start(), calls=%async_computation.7 | async-start | bytes 2621440 | tf_op jit(solution)/shard_map/all_gather | solution.py:102
  8.7 17.2 %collective-permute-start = (bf16[6,3,1024]{2,0,1:T(8,128)(2,1)S(1)}, bf16[6,3,1024]{2,0,1:T(8,128)(2,1)S(1)}, u32[]{:S(2)}, u32[]{:S(2)}) collective-permute-start(bf16[6,3,1024]{2,0,1:T(8,128)(2,1)S(1)} %slice.87), channel_id=1, source_target_pairs={{0,8},{8,16},{16,24},{24,32},{32,40},{40,48},{48,56},{56,64},{64,7... | collective-permute-start | bytes 110600 | tf_op jit(solution)/shard_map/ppermute | solution.py:15
  12.6 26.0 %all-to-all-start.1 = ((bf16[128,32,32]{0,2,1:T(8,128)(2,1)}), bf16[128,32,32]{0,2,1:T(8,128)(2,1)S(1)}, u32[]{:S(2)}, u32[]{:S(2)}) async-start(bf16[128,32,32]{0,2,1:T(8,128)(2,1)} %bitcast.8), calls=%async_computation.1 | async-start | bytes 524288 | tf_op jit(solution)/shard_map/all_to_all | solution.py:155
  24.9 95.3 %all-gather.5.cloned.1.call-start = ((), (), s32[]{:S(2)}) async-start(), calls=%async_computation.8 | async-start | bytes 2359296 | tf_op jit(solution)/shard_map/all_gather | solution.py:103
  26.0 12.5 %copy-start.17 = (f32[1,3,1024]{2,1,0:T(4,128)}, f32[1,3,1024]{2,1,0:T(4,128)S(1)}, u32[]{:S(2)}) copy-start(f32[1,3,1024]{2,1,0:T(4,128)S(1)} %copy.94) | copy-start | bytes 36868
  38.5 20.6 %all-to-all-start = ((bf16[128,32,32]{0,2,1:T(8,128)(2,1)}), bf16[128,32,32]{0,2,1:T(8,128)(2,1)S(1)}, u32[]{:S(2)}, u32[]{:S(2)}) async-start(bf16[128,32,32]{0,2,1:T(8,128)(2,1)} %bitcast.2), calls=%async_computation | async-start | bytes 524288 | tf_op jit(solution)/shard_map/all_to_all | solution.py:159
  155.4 10.6 %copy-start.8 = (bf16[32,128,32]{1,2,0:T(8,128)(2,1)S(1)}, bf16[32,128,32]{1,2,0:T(8,128)(2,1)}, u32[]{:S(2)}) copy-start(bf16[32,128,32]{1,2,0:T(8,128)(2,1)} %all_to_all.86) | copy-start | bytes 786436
  158.2 26.0 %collective-permute-start.1 = (bf16[128,1024]{1,0:T(8,128)(2,1)}, bf16[128,1024]{1,0:T(8,128)(2,1)}, u32[]{:S(2)}, u32[]{:S(2)}) collective-permute-start(bf16[128,1024]{1,0:T(8,128)(2,1)} %reduce_sum.75), channel_id=1, source_target_pairs={{0,0},{1,32},{2,64},{3,96},{4,128},{5,160},{6,192},{7,224},{32,1},... | collective-permute-start | bytes 786440 | tf_op jit(solution)/shard_map/ppermute | solution.py:122
  228.1 18.7 %all-to-all-start.5 = ((bf16[32,128,32]{1,2,0:T(8,128)(2,1)}), bf16[32,128,32]{1,2,0:T(8,128)(2,1)S(1)}, u32[]{:S(2)}, u32[]{:S(2)}) async-start(bf16[32,128,32]{1,2,0:T(8,128)(2,1)} %copy.60), calls=%async_computation.5 | async-start | bytes 524288 | tf_op jit(solution)/shard_map/all_to_all | solution.py:174
  235.9 11.2 %copy-start.1 = (bf16[128,3,1024]{2,0,1:T(8,128)(2,1)S(1)}, bf16[128,3,1024]{2,0,1:T(8,128)(2,1)}, u32[]{:S(2)}) copy-start(bf16[128,3,1024]{2,0,1:T(8,128)(2,1)} %copy-done) | copy-start | bytes 2359300
  249.1 9.1 %collective-permute-start.3 = (bf16[7,3,1024]{2,1,0:T(4,128)(2,1)S(1)}, bf16[7,3,1024]{2,1,0:T(4,128)(2,1)S(1)}, u32[]{:S(2)}, u32[]{:S(2)}) collective-permute-start(bf16[7,3,1024]{2,1,0:T(4,128)(2,1)S(1)} %constant_dynamic-update-slice_fusion), channel_id=1, source_target_pairs={{0,8},{8,0},{16,24},{24,16},{32,40},{40,32},{48,56},{56,48},{64,72... | collective-permute-start | bytes 129032 | tf_op jit(solution)/shard_map/ppermute | solution.py:130
  251.4 18.7 %all-to-all-start.6 = ((bf16[32,128,32]{1,2,0:T(8,128)(2,1)}), bf16[32,128,32]{1,2,0:T(8,128)(2,1)S(1)}, u32[]{:S(2)}, u32[]{:S(2)}) async-start(bf16[32,128,32]{1,2,0:T(8,128)(2,1)} %copy.65), calls=%async_computation.6 | async-start | bytes 524288 | tf_op jit(solution)/shard_map/all_to_all | solution.py:175
  258.3 9.3 %collective-permute-start.4 = (bf16[7,3,1024]{2,1,0:T(4,128)(2,1)S(1)}, bf16[7,3,1024]{2,1,0:T(4,128)(2,1)S(1)}, u32[]{:S(2)}, u32[]{:S(2)}) collective-permute-start(bf16[7,3,1024]{2,1,0:T(4,128)(2,1)S(1)} %add_convert_fusion.3), channel_id=1, source_target_pairs={{0,16},{8,24},{16,0},{24,8},{32,48},{40,56},{48,32},{56,40},{64,80... | collective-permute-start | bytes 129032 | tf_op jit(solution)/shard_map/ppermute | solution.py:130
  267.7 7.3 %collective-permute-start.5 = (bf16[7,3,1024]{2,1,0:T(4,128)(2,1)S(1)}, bf16[7,3,1024]{2,1,0:T(4,128)(2,1)S(1)}, u32[]{:S(2)}, u32[]{:S(2)}) collective-permute-start(bf16[7,3,1024]{2,1,0:T(4,128)(2,1)S(1)} %add_convert_fusion.2), channel_id=1, source_target_pairs={{0,32},{8,40},{16,48},{24,56},{32,0},{40,8},{48,16},{56,24},{64,96... | collective-permute-start | bytes 129032 | tf_op jit(solution)/shard_map/ppermute | solution.py:130
  270.2 15.3 %copy-start.10 = (f32[3,1024]{1,0:T(4,128)S(1)}, f32[3,1024]{1,0:T(4,128)}, u32[]{:S(2)}) copy-start(f32[3,1024]{1,0:T(4,128)} %copy-done.9) | copy-start | bytes 36868
  270.2 15.3 %copy-start.12 = (f32[3,1024]{1,0:T(4,128)S(1)}, f32[3,1024]{1,0:T(4,128)}, u32[]{:S(2)}) copy-start(f32[3,1024]{1,0:T(4,128)} %copy-done.11) | copy-start | bytes 36868
  270.2 15.3 %copy-start.14 = (f32[3,1024]{1,0:T(4,128)S(1)}, f32[3,1024]{1,0:T(4,128)}, u32[]{:S(2)}) copy-start(f32[3,1024]{1,0:T(4,128)} %copy-done.13) | copy-start | bytes 36868
  270.2 15.3 %copy-start.16 = (f32[3,1024]{1,0:T(4,128)S(1)}, f32[3,1024]{1,0:T(4,128)}, u32[]{:S(2)}) copy-start(f32[3,1024]{1,0:T(4,128)} %copy-done.15) | copy-start | bytes 36868
  270.2 15.3 %copy-start.18 = (f32[1,3,1024]{2,1,0:T(4,128)S(1)}, f32[1,3,1024]{2,1,0:T(4,128)}, u32[]{:S(2)}) copy-start(f32[1,3,1024]{2,1,0:T(4,128)} %copy-done.17) | copy-start | bytes 36868
  271.2 7.3 %collective-permute-start.2 = (bf16[6,3,1024]{2,0,1:T(8,128)(2,1)S(1)}, bf16[6,3,1024]{2,0,1:T(8,128)(2,1)S(1)}, u32[]{:S(2)}, u32[]{:S(2)}) collective-permute-start(bf16[6,3,1024]{2,0,1:T(8,128)(2,1)S(1)} %slice.122), channel_id=1, source_target_pairs={{8,0},{16,8},{24,16},{32,24},{40,32},{48,40},{56,48},{64,56},{72,6... | collective-permute-start | bytes 110600 | tf_op jit(solution)/shard_map/ppermute | solution.py:15
  275.1 8.2 %collective-permute-start.6 = (bf16[7,3,1024]{2,1,0:T(4,128)(2,1)S(1)}, bf16[7,3,1024]{2,1,0:T(4,128)(2,1)S(1)}, u32[]{:S(2)}, u32[]{:S(2)}) collective-permute-start(bf16[7,3,1024]{2,1,0:T(4,128)(2,1)S(1)} %add_convert_fusion.1), channel_id=1, source_target_pairs={{0,64},{8,72},{16,80},{24,88},{32,96},{40,104},{48,112},{56,120},{... | collective-permute-start | bytes 129032 | tf_op jit(solution)/shard_map/ppermute | solution.py:130
  283.3 5.8 %collective-permute-start.7 = (bf16[7,3,1024]{2,1,0:T(4,128)(2,1)S(1)}, bf16[7,3,1024]{2,1,0:T(4,128)(2,1)S(1)}, u32[]{:S(2)}, u32[]{:S(2)}) collective-permute-start(bf16[7,3,1024]{2,1,0:T(4,128)(2,1)S(1)} %add_convert_fusion), channel_id=1, source_target_pairs={{0,128},{8,136},{16,144},{24,152},{32,160},{40,168},{48,176},{56,1... | collective-permute-start | bytes 129032 | tf_op jit(solution)/shard_map/ppermute | solution.py:130
  (10 other events, 30.9 us)
Sparse Core Ops, SparseCore 0:
  9.8 42.7 all-gather.2
  55.2 64.9 all-gather.4

commit v11 on v7

--- a/solution.py
+++ b/solution.py
@@ -122,11 +122,26 @@
     return lax.ppermute(summed, ("hi", "tp"), pairs)
 
 
+Z_ORDER = (0, 1, 2, 3, 6, 7, 4, 5)
+
+
+def butterfly_labels(devices):
+    if devices != 4 * len(Z_ORDER):
+        return list(range(devices))
+    return [
+        (index // 16) * 16 + Z_ORDER[(index // 2) % 8] * 2 + index % 2
+        for index in range(devices)
+    ]
+
+
 def butterfly_sum(value, axis):
     devices = lax.axis_size(axis)
+    labels = butterfly_labels(devices)
+    owner = {label: index for index, label in enumerate(labels)}
     stride = 1
     while stride < devices:
-        value = value + lax.ppermute(value, axis, [(i, i ^ stride) for i in range(devices)])
+        pairs = [(i, owner[labels[i] ^ stride]) for i in range(devices)]
+        value = value + lax.ppermute(value, axis, pairs)
         stride *= 2
     return value
 

time: 301 us -> 298 us (0.990)
  no operation moved by 1% of the time
where the time goes in v11:
time: 298 us; the launch traced here: 295 us
  waiting for transfers between devices  89.6 us (30%)
  blocking collectives  70.4 us (24%)
  starting transfers between devices  53.3 us (18%)
  local copies, waits for them, and re-layouts  32.3 us (11%)
  matrix products  23.1 us (8%)
  between operations  15.2 us (5%)
  other arithmetic  11 us (4%)
    all_to_all x1, blocking collectives, output_grad(): lax.all_to_all(chunks, 'tp', split_axis=0, concat_axis=0, tiled=True)  30.6 us
    all_gather x1, waiting for transfers between devices, output_grad(): token_rows = lax.all_gather(cotangent, 'hi', axis=0, tiled=True)  28.1 us
    all_to_all x1, blocking collectives, body(): lax.all_to_all(grad_conv, SEQ, split_axis=1, concat_axis=0, tiled=True)  20.8 us
    all_to_all x1, blocking collectives, body(): lax.all_to_all(conv_cols, SEQ, split_axis=0, concat_axis=1, tiled=True)  18.9 us
    ppermute x1, waiting for transfers between devices, output_grad(): return lax.ppermute(summed, ('hi', 'tp'), pairs)  17.4 us
    ppermute x5, waiting for transfers between devices, butterfly_sum(): value = value + lax.ppermute(value, axis, pairs)  16.1 us
    all_to_all x1, starting transfers between devices, body(): lax.all_to_all(long_filter.astype(jnp.bfloat16), SEQ, split_axis=1, conca...  12.3 us
    all_to_all x1, waiting for transfers between devices, body(): lax.all_to_all(long_filter.astype(jnp.bfloat16), SEQ, split_axis=1, conca...  9.17 us
  transfers between devices with their start and end apart: 14, of which 10 were waited for; matrix products, arithmetic and copies ran while one was open for 11% of the time, Pallas kernels for 0%

profile of v11, /device:TPU:6, one launch (start us, length us, event | category | flops | bytes accessed | tf_op | source)
XLA Modules:
  0.0 294.9 jit_solution(12905559641661611814)
XLA Ops:
  12.6 12.3 %all-to-all-start.1 = ((bf16[128,32,32]{0,2,1:T(8,128)(2,1)}), bf16[128,32,32]{0,2,1:T(8,128)(2,1)S(1)}, u32[]{:S(2)}, u32[]{:S(2)}) async-start(bf16[128,32,32]{0,2,1:T(8,128)(2,1)} %bitcast.8), calls=%async_computation.1 | async-start | bytes 524288 | tf_op jit(solution)/shard_map/all_to_all | solution.py:167
  29.3 9.2 %all-to-all-done.1 = bf16[128,32,32]{0,2,1:T(8,128)(2,1)S(1)} async-done(((bf16[128,32,32]{0,2,1:T(8,128)(2,1)}), bf16[128,32,32]{0,2,1:T(8,128)(2,1)S(1)}, u32[]{:S(2)}, u32[]{:S(2)}) %all-to-all-start.1) | async-done | bytes 262176 | tf_op jit(solution)/shard_map/all_to_all | solution.py:167
  38.5 7.5 %all-to-all-start = ((bf16[128,32,32]{0,2,1:T(8,128)(2,1)}), bf16[128,32,32]{0,2,1:T(8,128)(2,1)S(1)}, u32[]{:S(2)}, u32[]{:S(2)}) async-start(bf16[128,32,32]{0,2,1:T(8,128)(2,1)} %bitcast.2), calls=%async_computation | async-start | bytes 524288 | tf_op jit(solution)/shard_map/all_to_all | solution.py:171
  50.6 8.5 %all-to-all-done = bf16[128,32,32]{0,2,1:T(8,128)(2,1)S(1)} async-done(((bf16[128,32,32]{0,2,1:T(8,128)(2,1)}), bf16[128,32,32]{0,2,1:T(8,128)(2,1)S(1)}, u32[]{:S(2)}, u32[]{:S(2)}) %all-to-all-start) | async-done | bytes 262176 | tf_op jit(solution)/shard_map/all_to_all | solution.py:171
  73.2 18.9 %all_to_all.86 = bf16[32,128,32]{1,2,0:T(8,128)(2,1)} all-to-all(bf16[32,128,32]{1,2,0:T(8,128)(2,1)S(1)} %copy.51), channel_id=1, replica_groups=mesh['hi'=8,'lo'=4,'tp'=8] {'hi','lo'}, dimensions={0} | all-to-all | bytes 524288 | tf_op jit(solution)/shard_map/all_to_all | solution.py:176
  92.1 28.1 %all-gather.5.cloned.1.call-done = bf16[1024,1024]{1,0:T(8,128)(2,1)} async-done(((bf16[128,1024]{1,0:T(8,128)(2,1)}), bf16[1024,1024]{1,0:T(8,128)(2,1)}) %all-gather.5.cloned.1.call-update) | async-done | bytes 2097168 | tf_op jit(solution)/shard_map/all_gather | solution.py:103
  120.2 4.6 %convolution_convert_fusion = bf16[1024,1024]{1,0:T(8,128)(2,1)S(1)} fusion(bf16[1024,1024]{1,0:T(8,128)(2,1)} %all-gather.5.cloned.1.call-done, bf16[1024,1024]{1,0:T(8,128)(2,1)} %all-gather.3.cloned.1.call-done), kind=kOutput, calls=%fused_computation.29 | convolution fusion | flops 2148532224 | bytes 6291456 | tf_op jit(solution)/shard_map/dot_general | solution.py:105
  124.8 30.6 %all_to_all.87 = bf16[8,128,1024]{2,1,0:T(8,128)(2,1)} all-to-all(bf16[8,128,1024]{2,1,0:T(8,128)(2,1)S(1)} %bitcast.196), channel_id=1, replica_groups=mesh['hi'=8,'lo'=4,'tp'=8] {'tp'}, dimensions={0} | all-to-all | bytes 4194304 | tf_op jit(solution)/shard_map/all_to_all | solution.py:113
  155.4 2.8 reduce_sum.75
  158.2 7.8 %collective-permute-start.1 = (bf16[128,1024]{1,0:T(8,128)(2,1)}, bf16[128,1024]{1,0:T(8,128)(2,1)}, u32[]{:S(2)}, u32[]{:S(2)}) collective-permute-start(bf16[128,1024]{1,0:T(8,128)(2,1)} %reduce_sum.75), channel_id=1, source_target_pairs={{0,0},{1,32},{2,64},{3,96},{4,128},{5,160},{6,192},{7,224},{32,1},... | collective-permute-start | bytes 786440 | tf_op jit(solution)/shard_map/ppermute | solution.py:122
  166.8 17.4 %collective-permute-done.1 = bf16[128,1024]{1,0:T(8,128)(2,1)} collective-permute-done((bf16[128,1024]{1,0:T(8,128)(2,1)}, bf16[128,1024]{1,0:T(8,128)(2,1)}, u32[]{:S(2)}, u32[]{:S(2)}) %collective-permute-start.1) | collective-permute-done | bytes 262176 | tf_op jit(solution)/shard_map/ppermute | solution.py:122
  184.2 2.0 fusion.76
  187.9 20.8 %all_to_all.88 = bf16[128,32,32]{0,2,1:T(8,128)(2,1)} all-to-all(bf16[128,32,32]{0,2,1:T(8,128)(2,1)} %bitcast.212), channel_id=1, replica_groups=mesh['hi'=8,'lo'=4,'tp'=8] {'hi','lo'}, dimensions={1} | all-to-all | bytes 524288 | tf_op jit(solution)/shard_map/all_to_all | solution.py:180
  208.8 2.3 copy.54
  211.0 3.0 %reshape.148 = bf16[64,2048]{1,0:T(8,128)(2,1)} reshape(bf16[32,128,32]{2,1,0:T(8,128)(2,1)} %copy.54) | data formatting | bytes 524288 | tf_op jit(solution)/shard_map/reshape | solution.py:37
  228.7 7.1 %all-to-all-start.5 = ((bf16[32,128,32]{1,2,0:T(8,128)(2,1)}), bf16[32,128,32]{1,2,0:T(8,128)(2,1)S(1)}, u32[]{:S(2)}, u32[]{:S(2)}) async-start(bf16[32,128,32]{1,2,0:T(8,128)(2,1)} %copy.60), calls=%async_computation.5 | async-start | bytes 524288 | tf_op jit(solution)/shard_map/all_to_all | solution.py:186
  238.4 9.0 %all-to-all-done.5 = bf16[32,128,32]{1,2,0:T(8,128)(2,1)S(1)} async-done(((bf16[32,128,32]{1,2,0:T(8,128)(2,1)}), bf16[32,128,32]{1,2,0:T(8,128)(2,1)S(1)}, u32[]{:S(2)}, u32[]{:S(2)}) %all-to-all-start.5) | async-done | bytes 262176 | tf_op jit(solution)/shard_map/all_to_all | solution.py:186
  247.4 6.8 %all-to-all-start.6 = ((bf16[32,128,32]{1,2,0:T(8,128)(2,1)}), bf16[32,128,32]{1,2,0:T(8,128)(2,1)S(1)}, u32[]{:S(2)}, u32[]{:S(2)}) async-start(bf16[32,128,32]{1,2,0:T(8,128)(2,1)} %copy.65), calls=%async_computation.6 | async-start | bytes 524288 | tf_op jit(solution)/shard_map/all_to_all | solution.py:187
  260.3 4.6 %collective-permute-done.4 = f32[7,3,1024]{2,1,0:T(4,128)S(1)} collective-permute-done((f32[7,3,1024]{2,1,0:T(4,128)S(1)}, f32[7,3,1024]{2,1,0:T(4,128)S(1)}, u32[]{:S(2)}, u32[]{:S(2)}) %collective-permute-start.4) | collective-permute-done | bytes 86048 | tf_op jit(solution)/shard_map/ppermute | solution.py:144
  264.9 3.0 %collective-permute-start.5 = (f32[7,3,1024]{2,1,0:T(4,128)S(1)}, f32[7,3,1024]{2,1,0:T(4,128)S(1)}, u32[]{:S(2)}, u32[]{:S(2)}) collective-permute-start(f32[7,3,1024]{2,1,0:T(4,128)S(1)} %add.319), channel_id=1, source_target_pairs={{0,32},{8,40},{16,48},{24,56},{32,0},{40,8},{48,16},{56,24},{64,96... | collective-permute-start | bytes 258056 | tf_op jit(solution)/shard_map/ppermute | solution.py:144
  268.0 3.1 %collective-permute-start.2 = (bf16[6,3,1024]{2,0,1:T(8,128)(2,1)S(1)}, bf16[6,3,1024]{2,0,1:T(8,128)(2,1)S(1)}, u32[]{:S(2)}, u32[]{:S(2)}) collective-permute-start(bf16[6,3,1024]{2,0,1:T(8,128)(2,1)S(1)} %slice.122), channel_id=1, source_target_pairs={{8,0},{16,8},{24,16},{32,24},{40,32},{48,40},{56,48},{64,56},{72,6... | collective-permute-start | bytes 110600 | tf_op jit(solution)/shard_map/ppermute | solution.py:15
  274.9 5.6 %collective-permute-done.6 = f32[7,3,1024]{2,1,0:T(4,128)S(1)} collective-permute-done((f32[7,3,1024]{2,1,0:T(4,128)S(1)}, f32[7,3,1024]{2,1,0:T(4,128)S(1)}, u32[]{:S(2)}, u32[]{:S(2)}) %collective-permute-start.6) | collective-permute-done | bytes 86048 | tf_op jit(solution)/shard_map/ppermute | solution.py:144
  281.1 2.3 fusion.19
  283.4 3.5 %collective-permute-done.7 = f32[7,3,1024]{2,1,0:T(4,128)S(1)} collective-permute-done((f32[7,3,1024]{2,1,0:T(4,128)S(1)}, f32[7,3,1024]{2,1,0:T(4,128)S(1)}, u32[]{:S(2)}, u32[]{:S(2)}) %collective-permute-start.7) | collective-permute-done | bytes 86048 | tf_op jit(solution)/shard_map/ppermute | solution.py:144
  (143 shorter events, 59.0 us)
Async XLA Ops:
  7.2 18.8 %copy-start.4 = (bf16[128,3,1024]{2,0,1:T(8,128)(2,1)S(1)}, bf16[128,3,1024]{2,0,1:T(8,128)(2,1)}, u32[]{:S(2)}) copy-start(bf16[128,3,1024]{2,0,1:T(8,128)(2,1)} %param.5) | copy-start | bytes 2359300
  7.2 18.5 %copy-start.18 = (f32[7,3,1024]{2,0,1:T(8,128)S(1)}, f32[7,3,1024]{2,0,1:T(8,128)}, u32[]{:S(2)}) copy-start(f32[7,3,1024]{2,0,1:T(8,128)} %param.8) | copy-start | bytes 258052
  7.2 84.9 %all-gather.3.cloned.1.call-start = ((), (), s32[]{:S(2)}) async-start(), calls=%async_computation.7 | async-start | bytes 2621440 | tf_op jit(solution)/shard_map/all_gather | solution.py:102
  8.7 17.2 %collective-permute-start = (bf16[6,3,1024]{2,0,1:T(8,128)(2,1)S(1)}, bf16[6,3,1024]{2,0,1:T(8,128)(2,1)S(1)}, u32[]{:S(2)}, u32[]{:S(2)}) collective-permute-start(bf16[6,3,1024]{2,0,1:T(8,128)(2,1)S(1)} %slice.87), channel_id=1, source_target_pairs={{0,8},{8,16},{16,24},{24,32},{32,40},{40,48},{48,56},{56,64},{64,7... | collective-permute-start | bytes 110600 | tf_op jit(solution)/shard_map/ppermute | solution.py:15
  12.6 26.0 %all-to-all-start.1 = ((bf16[128,32,32]{0,2,1:T(8,128)(2,1)}), bf16[128,32,32]{0,2,1:T(8,128)(2,1)S(1)}, u32[]{:S(2)}, u32[]{:S(2)}) async-start(bf16[128,32,32]{0,2,1:T(8,128)(2,1)} %bitcast.8), calls=%async_computation.1 | async-start | bytes 524288 | tf_op jit(solution)/shard_map/all_to_all | solution.py:167
  24.9 95.3 %all-gather.5.cloned.1.call-start = ((), (), s32[]{:S(2)}) async-start(), calls=%async_computation.8 | async-start | bytes 2359296 | tf_op jit(solution)/shard_map/all_gather | solution.py:103
  26.0 12.5 %copy-start.16 = (f32[1,3,1024]{2,1,0:T(4,128)}, f32[1,3,1024]{2,1,0:T(4,128)S(1)}, u32[]{:S(2)}) copy-start(f32[1,3,1024]{2,1,0:T(4,128)S(1)} %copy.94) | copy-start | bytes 36868
  38.5 20.6 %all-to-all-start = ((bf16[128,32,32]{0,2,1:T(8,128)(2,1)}), bf16[128,32,32]{0,2,1:T(8,128)(2,1)S(1)}, u32[]{:S(2)}, u32[]{:S(2)}) async-start(bf16[128,32,32]{0,2,1:T(8,128)(2,1)} %bitcast.2), calls=%async_computation | async-start | bytes 524288 | tf_op jit(solution)/shard_map/all_to_all | solution.py:171
  155.4 10.5 %copy-start.7 = (bf16[32,128,32]{1,2,0:T(8,128)(2,1)S(1)}, bf16[32,128,32]{1,2,0:T(8,128)(2,1)}, u32[]{:S(2)}) copy-start(bf16[32,128,32]{1,2,0:T(8,128)(2,1)} %all_to_all.86) | copy-start | bytes 786436
  158.2 26.0 %collective-permute-start.1 = (bf16[128,1024]{1,0:T(8,128)(2,1)}, bf16[128,1024]{1,0:T(8,128)(2,1)}, u32[]{:S(2)}, u32[]{:S(2)}) collective-permute-start(bf16[128,1024]{1,0:T(8,128)(2,1)} %reduce_sum.75), channel_id=1, source_target_pairs={{0,0},{1,32},{2,64},{3,96},{4,128},{5,160},{6,192},{7,224},{32,1},... | collective-permute-start | bytes 786440 | tf_op jit(solution)/shard_map/ppermute | solution.py:122
  228.7 18.7 %all-to-all-start.5 = ((bf16[32,128,32]{1,2,0:T(8,128)(2,1)}), bf16[32,128,32]{1,2,0:T(8,128)(2,1)S(1)}, u32[]{:S(2)}, u32[]{:S(2)}) async-start(bf16[32,128,32]{1,2,0:T(8,128)(2,1)} %copy.60), calls=%async_computation.5 | async-start | bytes 524288 | tf_op jit(solution)/shard_map/all_to_all | solution.py:186
  237.4 17.1 %copy-start.1 = (bf16[128,3,1024]{2,0,1:T(8,128)(2,1)S(1)}, bf16[128,3,1024]{2,0,1:T(8,128)(2,1)}, u32[]{:S(2)}) copy-start(bf16[128,3,1024]{2,0,1:T(8,128)(2,1)} %copy-done) | copy-start | bytes 2359300
  247.4 23.7 %all-to-all-start.6 = ((bf16[32,128,32]{1,2,0:T(8,128)(2,1)}), bf16[32,128,32]{1,2,0:T(8,128)(2,1)S(1)}, u32[]{:S(2)}, u32[]{:S(2)}) async-start(bf16[32,128,32]{1,2,0:T(8,128)(2,1)} %copy.65), calls=%async_computation.6 | async-start | bytes 524288 | tf_op jit(solution)/shard_map/all_to_all | solution.py:187
  257.2 1.4 collective-permute-start.3
  258.7 6.2 %collective-permute-start.4 = (f32[7,3,1024]{2,1,0:T(4,128)S(1)}, f32[7,3,1024]{2,1,0:T(4,128)S(1)}, u32[]{:S(2)}, u32[]{:S(2)}) collective-permute-start(f32[7,3,1024]{2,1,0:T(4,128)S(1)} %add.318), channel_id=1, source_target_pairs={{0,16},{8,24},{16,0},{24,8},{32,48},{40,56},{48,32},{56,40},{64,80... | collective-permute-start | bytes 258056 | tf_op jit(solution)/shard_map/ppermute | solution.py:144
  264.9 8.6 %collective-permute-start.5 = (f32[7,3,1024]{2,1,0:T(4,128)S(1)}, f32[7,3,1024]{2,1,0:T(4,128)S(1)}, u32[]{:S(2)}, u32[]{:S(2)}) collective-permute-start(f32[7,3,1024]{2,1,0:T(4,128)S(1)} %add.319), channel_id=1, source_target_pairs={{0,32},{8,40},{16,48},{24,56},{32,0},{40,8},{48,16},{56,24},{64,96... | collective-permute-start | bytes 258056 | tf_op jit(solution)/shard_map/ppermute | solution.py:144
  268.0 6.7 %collective-permute-start.2 = (bf16[6,3,1024]{2,0,1:T(8,128)(2,1)S(1)}, bf16[6,3,1024]{2,0,1:T(8,128)(2,1)S(1)}, u32[]{:S(2)}, u32[]{:S(2)}) collective-permute-start(bf16[6,3,1024]{2,0,1:T(8,128)(2,1)S(1)} %slice.122), channel_id=1, source_target_pairs={{8,0},{16,8},{24,16},{32,24},{40,32},{48,40},{56,48},{64,56},{72,6... | collective-permute-start | bytes 110600 | tf_op jit(solution)/shard_map/ppermute | solution.py:15
  271.2 9.9 %copy-start.9 = (f32[3,1024]{1,0:T(4,128)S(1)}, f32[3,1024]{1,0:T(4,128)}, u32[]{:S(2)}) copy-start(f32[3,1024]{1,0:T(4,128)} %copy-done.8) | copy-start | bytes 36868
  271.2 9.9 %copy-start.11 = (f32[3,1024]{1,0:T(4,128)S(1)}, f32[3,1024]{1,0:T(4,128)}, u32[]{:S(2)}) copy-start(f32[3,1024]{1,0:T(4,128)} %copy-done.10) | copy-start | bytes 36868
  271.2 9.9 %copy-start.13 = (f32[3,1024]{1,0:T(4,128)S(1)}, f32[3,1024]{1,0:T(4,128)}, u32[]{:S(2)}) copy-start(f32[3,1024]{1,0:T(4,128)} %copy-done.12) | copy-start | bytes 36868
  271.2 9.9 %copy-start.15 = (f32[3,1024]{1,0:T(4,128)S(1)}, f32[3,1024]{1,0:T(4,128)}, u32[]{:S(2)}) copy-start(f32[3,1024]{1,0:T(4,128)} %copy-done.14) | copy-start | bytes 36868
  271.3 9.9 %copy-start.17 = (f32[1,3,1024]{2,1,0:T(4,128)S(1)}, f32[1,3,1024]{2,1,0:T(4,128)}, u32[]{:S(2)}) copy-start(f32[1,3,1024]{2,1,0:T(4,128)} %copy-done.16) | copy-start | bytes 36868
  273.5 7.0 %collective-permute-start.6 = (f32[7,3,1024]{2,1,0:T(4,128)S(1)}, f32[7,3,1024]{2,1,0:T(4,128)S(1)}, u32[]{:S(2)}, u32[]{:S(2)}) collective-permute-start(f32[7,3,1024]{2,1,0:T(4,128)S(1)} %add.320), channel_id=1, source_target_pairs={{0,96},{8,104},{16,112},{24,120},{32,64},{40,72},{48,80},{56,88},{... | collective-permute-start | bytes 258056 | tf_op jit(solution)/shard_map/ppermute | solution.py:144
  280.5 6.4 %collective-permute-start.7 = (f32[7,3,1024]{2,1,0:T(4,128)S(1)}, f32[7,3,1024]{2,1,0:T(4,128)S(1)}, u32[]{:S(2)}, u32[]{:S(2)}) collective-permute-start(f32[7,3,1024]{2,1,0:T(4,128)S(1)} %add.321), channel_id=1, source_target_pairs={{0,128},{8,136},{16,144},{24,152},{32,160},{40,168},{48,176},{56,1... | collective-permute-start | bytes 258056 | tf_op jit(solution)/shard_map/ppermute | solution.py:144
  (9 other events, 19.7 us)
Sparse Core Ops, SparseCore 0:
  9.8 42.7 all-gather.2
  55.2 64.9 all-gather.4
